TPU v7x, 512 devices: a whole 4x4x16 slice. The times are simulated.
512 devices in a mesh: island: 32 (over y, z_hi, core), fsdp: 16 (over x, z_lo).
Axes of the slice: x: 4, y: 4, z: 16 (z_hi: 4, z_lo: 4; z = z_hi * 4 + z_lo), core: 2. Of those that a mesh axis runs over, the one named last changes fastest.
Arguments:
- hidden: bfloat16 [65536, 4096], P(('island', 'fsdp')), may hold values from -6 to 6
- query_rows: bfloat16 [65536, 4096], P(('island', 'fsdp')), may hold values from -150 to 150
- key_rows: bfloat16 [65536, 512], P(('island', 'fsdp')), may hold values from -6 to 6
- targets: bfloat16 [65536, 4096], P(('island', 'fsdp')), may hold values from -6 to 6
- segment_ids: int32 [512, 128], P(('island', 'fsdp')), may hold values from 0 to 3, never falling along the last dimension, each value on 1 to 48 neighbouring positions
- first_moment: float32 [32, 4096, 512], P('island', 'fsdp'), may hold values from -0.0020716018 to 0.0020716018
- second_moment: float32 [32, 4096, 512], P('island', 'fsdp'), may hold values from 5.9604645e-08 to 9.536743e-07
- anchor: float32 [4096, 512], P('fsdp', 'island'), may hold values from -6 to 6
- outer_momentum: float32 [4096, 512], P('fsdp', 'island'), may hold values from -0.3 to 0.3
- token_counts: int32 [32], P('island'), may hold values from 4096 to 12287
Outputs:
- new_anchor: float32 [4096, 512], P('fsdp', 'island')
- new_momentum: float32 [4096, 512], P('fsdp', 'island')
Inputs may be any that keep to these rules, and one draw needn't show every extreme that they name: `segment_ids`: each row is one sequence: document numbers from 0 that never fall, each document 1 to 48 tokens, one of exactly 48.
All inputs are finite; a program needn't handle non-finite values.
Results may differ from a plain program's by a relative error of at most 0.004.
Values may be sent and summed in bfloat16 or wider, within the bound.
No kernel may reach another device: no remote copies, remote signals or barrier semaphores. Data moves between devices by JAX's collectives and lax.ppermute only.
A program may use at most 64 MiB of HBM per device.

v0:
```python
import math

import jax
import jax.numpy as jnp
from jax import lax
from jax.sharding import PartitionSpec as P

KVH = 4
QPK = 8
HD = 128


beta_one = 0.9
beta_two = 0.95
inner_rate = 0.05
decay = 0.1
epsilon = 1e-08
outer_rate = 0.7
outer_beta = 0.9


def attention_weights(query_rows, key_rows, segments):
    length = segments.shape[0]
    queries = query_rows.reshape(length, KVH, QPK, HD)
    keyed = key_rows.reshape(length, KVH, HD)
    scores = jnp.einsum("tgjd,sgd->gjts", queries, keyed, preferred_element_type=jnp.float32) * (
        1.0 / math.sqrt(HD)
    )
    place = jnp.arange(length)
    allowed = (place[None, :] <= place[:, None]) & (segments[:, None] == segments[None, :])
    scores = jnp.where(allowed[None, None], scores, -jnp.inf)
    highest = jnp.max(scores, axis=-1, keepdims=True)
    expo = jnp.exp(scores - highest)
    return (expo / jnp.sum(expo, axis=-1, keepdims=True)).astype(jnp.bfloat16)


def on_device(
    hidden,
    query_rows,
    key_rows,
    targets,
    segment_ids,
    first_moment,
    second_moment,
    anchor,
    outer_momentum,
    token_counts,
):
    rows = hidden.shape[0]
    width = key_rows.shape[1]
    group_rows = rows * lax.axis_size("fsdp")
    scale_in = 1.0 / math.sqrt(hidden.shape[1])
    attention = attention_weights(query_rows, key_rows, segment_ids[0])
    master = lax.all_gather(anchor, "island", axis=1, tiled=True)
    start_point = master
    block = master.shape[0]
    first = first_moment[0]
    second = second_moment[0]
    feature_rows = lax.all_to_all(hidden, "fsdp", split_axis=1, concat_axis=0, tiled=True)
    for inner_step in range(2):
        sent_rows = master.astype(jnp.bfloat16)
        add_piece = lax.all_gather(sent_rows, "fsdp", axis=0, tiled=True)
        count = add_piece.shape[0] // block
        columns = hidden.reshape(rows, count, block)
        blocks = jnp.einsum(
            "rks,ksw->krw",
            columns,
            add_piece.reshape(count, block, width),
            preferred_element_type=jnp.float32,
        )
        projected = jnp.sum(blocks.astype(jnp.bfloat16).astype(jnp.float32), axis=0)
        values = (projected * scale_in).astype(jnp.bfloat16)
        mixed = jnp.einsum(
            "gjts,sgd->tgjd",
            attention,
            values.reshape(rows, KVH, HD),
            preferred_element_type=jnp.float32,
        )
        error = (
            (mixed.reshape(rows, KVH * QPK * HD) - targets.astype(jnp.float32)) / group_rows
        ).astype(jnp.bfloat16)
        back = jnp.einsum(
            "gjts,tgjd->sgd",
            attention,
            error.reshape(rows, KVH, QPK, HD),
            preferred_element_type=jnp.float32,
        )
        value_grad = (back.reshape(rows, width) * scale_in).astype(jnp.bfloat16)
        grad = lax.dot_general(
            feature_rows,
            lax.all_gather(value_grad, "fsdp", axis=0, tiled=True),
            (((0,), (0,)), ((), ())),
            preferred_element_type=jnp.float32,
        )
        first = beta_one * first + (1.0 - beta_one) * grad
        second = beta_two * second + (1.0 - beta_two) * grad * grad
        master = master - inner_rate * (first / (jnp.sqrt(second) + epsilon) + decay * master)
    delta = start_point - master
    groups = lax.axis_size("island")
    own_count = token_counts[0].astype(jnp.float32)
    total_count = lax.psum(own_count, "island")
    received = lax.all_to_all(
        own_count / total_count * delta, "island", split_axis=1, concat_axis=0, tiled=True
    )
    average = jnp.sum(received.reshape(groups, block, anchor.shape[1]), axis=0)
    new_momentum = outer_beta * outer_momentum + average
    new_anchor = anchor - outer_rate * (average + outer_beta * new_momentum)
    return (new_anchor, new_momentum)


def solution(mesh):
    in_specs = (
        P(("island", "fsdp"), None),
        P(("island", "fsdp"), None),
        P(("island", "fsdp"), None),
        P(("island", "fsdp"), None),
        P(("island", "fsdp"), None),
        P("island", "fsdp", None),
        P("island", "fsdp", None),
        P("fsdp", "island"),
        P("fsdp", "island"),
        P("island"),
    )
    out_specs = (P("fsdp", "island"), P("fsdp", "island"))
    return jax.shard_map(
        on_device, mesh=mesh, in_specs=in_specs, out_specs=out_specs, check_vma=False
    )
```

profile of v0, /device:TPU:1, one launch (start us, length us, event | category | flops | bytes accessed | tf_op | source)
XLA Modules:
  0.0 569.2 jit_solution(821876358735540044)
XLA Ops:
  7.2 0.0 copy-start.4
  7.2 0.0 all-gather.5.cloned.1.call-start
  7.2 63.1 %all_gather.15 = f32[256,512]{0,1:T(8,128)S(1)} all-gather(f32[256,16]{0,1:T(8,128)} %param.17), channel_id=1, replica_groups=mesh['island'=32,'fsdp'=16] {'island'}, dimensions={1}, use_global_device_ids=true | all-gather | bytes 540672 | tf_op jit(solution)/shard_map/all_gather | solution.py:54
  70.3 0.8 copy-done.1
  71.1 0.7 convert_element_type.76
  71.8 0.0 all-gather.5.cloned.1.call-update
  71.8 0.0 copy-done.4
  71.8 0.0 copy-start.5
  71.9 1.3 copy.59
  73.2 5.5 all-to-all-start
  78.7 0.0 all-gather.7.cloned.1.call-start
  78.7 0.0 copy-done.5
  78.7 0.2 copy.86
  79.0 0.0 copy-done.18
  79.0 0.1 fusion.42
  79.1 1.0 fusion.49
  80.1 0.3 divide_convert_fusion
  80.4 1.7 copy.67
  82.1 112.5 %all-gather.5.cloned.1.call-done = bf16[4096,512]{0,1:T(8,128)(2,1)} async-done(((bf16[256,512]{0,1:T(8,128)(2,1)}), bf16[4096,512]{0,1:T(8,128)(2,1)}) %all-gather.5.cloned.1.call-update) | async-done | bytes 4194320 | tf_op jit(solution)/shard_map/all_gather | solution.py:62
  194.6 6.5 %copy.60 = bf16[4096,512]{1,0:T(8,128)(2,1)} copy(bf16[4096,512]{0,1:T(8,128)(2,1)} %all-gather.5.cloned.1.call-done) | data formatting | bytes 8388608 | tf_op jit(solution)/shard_map/all_gather | solution.py:62
  201.1 3.3 convert_reduce_fusion.1
  204.5 0.1 copy.82
  204.6 0.4 fusion.54
  205.0 1.9 copy.66
  206.9 2.2 fusion.16
  209.1 0.2 copy.87
  209.3 1.0 copy-done.6
  210.3 1.1 fusion.13
  211.4 0.0 all-gather.7.cloned.1.call-update
  211.5 0.0 all-gather.9.cloned.1.call-start
  211.5 0.2 copy.58
  211.7 0.0 copy-done.11
  211.7 0.0 copy-start.12
  211.7 1.0 copy.69
  212.8 0.0 all-to-all-done
  212.8 1.5 copy.68
  214.3 73.4 %all-gather.7.cloned.1.call-done = bf16[2048,512]{0,1:T(8,128)(2,1)} async-done(((bf16[128,512]{0,1:T(8,128)(2,1)}), bf16[2048,512]{0,1:T(8,128)(2,1)}) %all-gather.7.cloned.1.call-update) | async-done | bytes 2097168 | tf_op jit(solution)/shard_map/all_gather | solution.py:91
  287.7 3.5 fusion.32
  291.2 0.0 all-gather.9.cloned.1.call-update
  291.2 0.0 all-gather.11.cloned.1.call-start
  291.3 118.8 %all-gather.9.cloned.1.call-done = bf16[4096,512]{0,1:T(8,128)(2,1)} async-done(((bf16[256,512]{0,1:T(8,128)(2,1)}), bf16[4096,512]{0,1:T(8,128)(2,1)}) %all-gather.9.cloned.1.call-update) | async-done | bytes 4194320 | tf_op jit(solution)/shard_map/all_gather | solution.py:62
  410.1 3.8 convert_reduce_fusion
  413.9 0.4 fusion.55
  414.3 0.0 copy-start
  414.3 1.9 copy.73
  416.2 1.9 fusion.15
  418.1 0.2 copy.88
  418.3 1.0 copy-done.7
  419.3 1.1 fusion.14
  420.5 0.0 all-gather.11.cloned.1.call-update
  421.1 93.8 %psum.7 = f32[]{:T(128)} all-reduce(f32[]{:T(128)} %bitcast), channel_id=1, replica_groups=mesh['island'=32,'fsdp'=16] {'island'}, use_global_device_ids=true, to_apply=%region_0.1 | all-reduce | flops 1 | bytes 8 | tf_op jit(solution)/shard_map/psum | solution.py:101
  515.6 0.0 all-gather.11.cloned.1.call-done
  515.6 0.0 copy-done.3
  515.6 0.0 copy-done.9
  515.7 0.0 copy-done.13
  515.7 0.0 copy-done.14
  515.7 0.0 copy-done.19
  515.7 0.0 copy-start.16
  515.7 0.0 copy-start.17
  515.7 2.9 fusion.31
  518.6 43.4 %all_to_all.29 = f32[256,32,16]{0,2,1:T(8,128)S(1)} all-to-all(f32[256,32,16]{0,2,1:T(8,128)S(1)} %bitcast.114), channel_id=1, replica_groups=mesh['island'=32,'fsdp'=16] {'island'}, dimensions={1} | all-to-all | bytes 1048576 | tf_op jit(solution)/shard_map/all_to_all | solution.py:102
  562.0 0.0 copy-done.16
  562.0 0.0 copy-done.17
  562.0 0.6 multiply_subtract_fusion.1
  (24 shorter events, 0.2 us)
Async XLA Ops:
  7.2 64.7 %copy-start.4 = (bf16[128,4096]{1,0:T(8,128)(2,1)S(1)}, bf16[128,4096]{1,0:T(8,128)(2,1)}, u32[]{:S(2)}) copy-start(bf16[128,4096]{1,0:T(8,128)(2,1)} %param.10) | copy-start | bytes 3145732
  7.2 187.4 %all-gather.5.cloned.1.call-start = ((), (), s32[]{:S(2)}) async-start(), calls=%async_computation.2 | async-start | bytes 4456448 | tf_op jit(solution)/shard_map/all_gather | solution.py:62
  70.3 0.8 copy-start.1
  71.8 6.9 %copy-start.5 = (bf16[128,4096]{1,0:T(8,128)(2,1)S(1)}, bf16[128,4096]{1,0:T(8,128)(2,1)}, u32[]{:S(2)}) copy-start(bf16[128,4096]{1,0:T(8,128)(2,1)} %param.11) | copy-start | bytes 3145732
  73.2 5.8 %copy-start.15 = (bf16[128,512]{1,0:T(8,128)(2,1)S(1)}, bf16[128,512]{1,0:T(8,128)(2,1)}, u32[]{:S(2)}) copy-start(bf16[128,512]{1,0:T(8,128)(2,1)} %param.12) | copy-start | bytes 393220
  73.2 5.9 %copy-start.18 = (s32[1,128]{1,0:T(1,128)S(1)}, s32[1,128]{1,0:T(1,128)}, u32[]{:S(2)}) copy-start(s32[1,128]{1,0:T(1,128)} %param.14) | copy-start | bytes 1540
  73.2 139.6 %all-to-all-start = ((bf16[128,16,256]{0,2,1:T(8,128)(2,1)}), bf16[128,16,256]{0,2,1:T(8,128)(2,1)}, u32[]{:S(2)}, u32[]{:S(2)}) async-start(bf16[128,16,256]{0,2,1:T(8,128)(2,1)} %bitcast.2), calls=%async_computation | async-start | bytes 2097152 | tf_op jit(solution)/shard_map/all_to_all | solution.py:59
  78.7 209.0 %all-gather.7.cloned.1.call-start = ((), (), s32[]{:S(2)}) async-start(), calls=%async_computation.3 | async-start | bytes 2228224 | tf_op jit(solution)/shard_map/all_gather | solution.py:91
  209.1 1.2 copy-start.6
  210.3 1.2 copy-start.10
  210.3 1.4 copy-start.11
  211.5 76.2 %copy-start.2 = (f32[256,512]{0,1:T(8,128)S(1)}, f32[256,512]{0,1:T(8,128)}, u32[]{:S(2)}) copy-start(f32[256,512]{0,1:T(8,128)} %copy-done.1) | copy-start | bytes 1572868
  211.5 198.6 %all-gather.9.cloned.1.call-start = ((), (), s32[]{:S(2)}) async-start(), calls=%async_computation.4 | async-start | bytes 4456448 | tf_op jit(solution)/shard_map/all_gather | solution.py:62
  211.7 79.5 %copy-start.12 = (f32[1,256,512]{1,2,0:T(8,128)}, f32[1,256,512]{1,2,0:T(8,128)S(1)}, u32[]{:S(2)}) copy-start(f32[1,256,512]{1,2,0:T(8,128)S(1)} %copy.58) | copy-start | bytes 1572868
  214.3 76.9 %copy-start.8 = (bf16[16,128,256]{2,1,0:T(8,128)(2,1)}, bf16[16,128,256]{2,1,0:T(8,128)(2,1)S(1)}, u32[]{:S(2)}) copy-start(bf16[16,128,256]{2,1,0:T(8,128)(2,1)S(1)} %copy.68) | copy-start | bytes 3145732
  291.2 224.4 %all-gather.11.cloned.1.call-start = ((), (), s32[]{:S(2)}) async-start(), calls=%async_computation.5 | async-start | bytes 2228224 | tf_op jit(solution)/shard_map/all_gather | solution.py:91
  414.3 1.9 copy-start
  418.1 1.2 copy-start.7
  419.3 96.3 %copy-start.3 = (f32[256,512]{0,1:T(8,128)S(1)}, f32[256,512]{0,1:T(8,128)}, u32[]{:S(2)}) copy-start(f32[256,512]{0,1:T(8,128)} %copy-done.1) | copy-start | bytes 1572868
  419.3 96.3 %copy-start.9 = (bf16[16,128,256]{2,1,0:T(8,128)(2,1)S(1)}, bf16[16,128,256]{2,1,0:T(8,128)(2,1)}, u32[]{:S(2)}) copy-start(bf16[16,128,256]{2,1,0:T(8,128)(2,1)} %copy-done.8) | copy-start | bytes 3145732
  419.3 96.3 %copy-start.13 = (f32[1,256,512]{1,2,0:T(8,128)S(1)}, f32[1,256,512]{1,2,0:T(8,128)}, u32[]{:S(2)}) copy-start(f32[1,256,512]{1,2,0:T(8,128)} %copy-done.12) | copy-start | bytes 1572868
  419.3 96.3 %copy-start.14 = (f32[1,256,512]{1,2,0:T(8,128)S(1)}, f32[1,256,512]{1,2,0:T(8,128)}, u32[]{:S(2)}) copy-start(f32[1,256,512]{1,2,0:T(8,128)} %copy.69) | copy-start | bytes 1572868
  419.3 96.4 %copy-start.19 = (f32[256,512]{0,1:T(8,128)S(1)}, f32[256,512]{0,1:T(8,128)}, u32[]{:S(2)}) copy-start(f32[256,512]{0,1:T(8,128)} %get-tuple-element.7) | copy-start | bytes 1572868
  515.7 46.3 %copy-start.16 = (f32[256,16]{0,1:T(8,128)S(1)}, f32[256,16]{0,1:T(8,128)}, u32[]{:S(2)}) copy-start(f32[256,16]{0,1:T(8,128)} %param.17) | copy-start | bytes 49156
  515.7 46.3 %copy-start.17 = (f32[256,16]{0,1:T(8,128)S(1)}, f32[256,16]{0,1:T(8,128)}, u32[]{:S(2)}) copy-start(f32[256,16]{0,1:T(8,128)} %param.18) | copy-start | bytes 49156
Sparse Core Ops, SparseCore 0:
  72.0 122.5 all-gather.4
  211.6 76.0 all-gather.6
  291.4 118.6 all-gather.8
  420.6 86.2 all-gather.10
where the time goes:
time: 575 us; the launch traced here: 569 us
  waiting for transfers between devices  305 us (53%)
  blocking collectives  200 us (35%)
  local copies, waits for them, and re-layouts  19.7 us (3%)
  matrix products  17.6 us (3%)
  between operations  15.4 us (3%)
  other arithmetic  5.84 us (1%)
    all_gather x2, waiting for transfers between devices, on_device(): add_piece = lax.all_gather(sent_rows, 'fsdp', axis=0, tiled=True)  231 us
    psum x1, blocking collectives, on_device(): total_count = lax.psum(own_count, 'island')  93.8 us
    all_gather x2, waiting for transfers between devices, on_device(): lax.all_gather(value_grad, 'fsdp', axis=0, tiled=True)  73.4 us
    all_gather x1, blocking collectives, on_device(): master = lax.all_gather(anchor, 'island', axis=1, tiled=True)  63.1 us
    all_to_all x1, blocking collectives, on_device(): lax.all_to_all(own_count / total_count * delta, 'island', split_axis=1, c...  43.4 us
  transfers between devices with their start and end apart: 5, of which 3 were waited for; matrix products, arithmetic and copies ran while one was open for 4% of the time, Pallas kernels for 0%

commit v1 on v0

--- a/solution.py
+++ b/solution.py
@@ -48,7 +48,8 @@
 ):
     rows = hidden.shape[0]
     width = key_rows.shape[1]
-    group_rows = rows * lax.axis_size("fsdp")
+    members = lax.axis_size("fsdp")
+    group_rows = rows * members
     scale_in = 1.0 / math.sqrt(hidden.shape[1])
     attention = attention_weights(query_rows, key_rows, segment_ids[0])
     master = lax.all_gather(anchor, "island", axis=1, tiled=True)
@@ -58,17 +59,13 @@
     second = second_moment[0]
     feature_rows = lax.all_to_all(hidden, "fsdp", split_axis=1, concat_axis=0, tiled=True)
     for inner_step in range(2):
-        sent_rows = master.astype(jnp.bfloat16)
-        add_piece = lax.all_gather(sent_rows, "fsdp", axis=0, tiled=True)
-        count = add_piece.shape[0] // block
-        columns = hidden.reshape(rows, count, block)
-        blocks = jnp.einsum(
-            "rks,ksw->krw",
-            columns,
-            add_piece.reshape(count, block, width),
-            preferred_element_type=jnp.float32,
+        partial = jnp.dot(
+            feature_rows, master.astype(jnp.bfloat16), preferred_element_type=jnp.float32
+        ).astype(jnp.bfloat16)
+        pieces = lax.all_to_all(
+            partial.reshape(members, rows, width), "fsdp", split_axis=0, concat_axis=0, tiled=True
         )
-        projected = jnp.sum(blocks.astype(jnp.bfloat16).astype(jnp.float32), axis=0)
+        projected = jnp.sum(pieces.astype(jnp.float32), axis=0)
         values = (projected * scale_in).astype(jnp.bfloat16)
         mixed = jnp.einsum(
             "gjts,sgd->tgjd",
@@ -97,12 +94,16 @@
         master = master - inner_rate * (first / (jnp.sqrt(second) + epsilon) + decay * master)
     delta = start_point - master
     groups = lax.axis_size("island")
+    cols = anchor.shape[1]
     own_count = token_counts[0].astype(jnp.float32)
-    total_count = lax.psum(own_count, "island")
+    weighted = jnp.concatenate(
+        [own_count * delta, jnp.full((1, delta.shape[1]), own_count, jnp.float32)], axis=0
+    )
     received = lax.all_to_all(
-        own_count / total_count * delta, "island", split_axis=1, concat_axis=0, tiled=True
+        weighted.reshape(block + 1, groups, cols), "island", split_axis=1, concat_axis=0, tiled=True
     )
-    average = jnp.sum(received.reshape(groups, block, anchor.shape[1]), axis=0)
+    summed = jnp.sum(received.reshape(groups, block + 1, cols), axis=0)
+    average = summed[:block] / summed[block:]
     new_momentum = outer_beta * outer_momentum + average
     new_anchor = anchor - outer_rate * (average + outer_beta * new_momentum)
     return (new_anchor, new_momentum)

time: 575 us -> 458 us (0.80)
  the two profiles are of different devices: /device:TPU:1 before, /device:TPU:64 now
where the time goes in v1:
time: 458 us
  waiting for transfers between devices  205 us (45%)
  blocking collectives  177 us (39%)
  matrix products  18.6 us (4%)
  starting transfers between devices  17.3 us (4%)
  local copies, waits for them, and re-layouts  16.3 us (4%)
  between operations  15 us (3%)
  other arithmetic  8.63 us (2%)
    all_gather x2, waiting for transfers between devices, on_device(): lax.all_gather(value_grad, 'fsdp', axis=0, tiled=True)  167 us
    all_gather x1, blocking collectives, on_device(): master = lax.all_gather(anchor, 'island', axis=1, tiled=True)  73.5 us
    all_to_all x1, blocking collectives, on_device(): lax.all_to_all(weighted.reshape(block + 1, groups, cols), 'island', split...  58.3 us
    all_to_all x1, blocking collectives, on_device(): lax.all_to_all(partial.reshape(members, rows, width), 'fsdp', split_axis=...  45.4 us
    all_to_all x1, waiting for transfers between devices, on_device(): lax.all_to_all(partial.reshape(members, rows, width), 'fsdp', split_axis=...  37.5 us
  transfers between devices with their start and end apart: 4, of which 3 were waited for; matrix products, arithmetic and copies ran while one was open for 2% of the time, Pallas kernels for 0%

profile of v1, /device:TPU:64, one launch (start us, length us, event | category | flops | bytes accessed | tf_op | source)
XLA Modules:
  0.0 457.6 jit_solution(3912609663833411937)
XLA Ops:
  7.2 0.0 copy-start.12
  7.2 2.3 copy.64
  9.4 8.4 %all-to-all-start = ((bf16[128,16,256]{0,2,1:T(8,128)(2,1)}), bf16[128,16,256]{0,2,1:T(8,128)(2,1)S(1)}, u32[]{:S(2)}, u32[]{:S(2)}) async-start(bf16[128,16,256]{0,2,1:T(8,128)(2,1)} %bitcast.2), calls=%async_computation | async-start | bytes 2097152 | tf_op jit(solution)/shard_map/all_to_all | solution.py:60
  17.9 0.0 copy-done.12
  17.9 73.5 %all_gather.9 = f32[256,512]{0,1:T(8,128)S(1)} all-gather(f32[256,16]{0,1:T(8,128)S(1)} %copy-done.12), channel_id=1, replica_groups=mesh['island'=32,'fsdp'=16] {'island'}, dimensions={1}, use_global_device_ids=true | all-gather | bytes 540672 | tf_op jit(solution)/shard_map/all_gather | solution.py:55
  91.4 0.0 all-to-all-done
  91.4 0.5 copy.65
  91.9 2.0 convolution_convert_fusion.1
  94.0 8.8 %all-to-all-start.1 = ((bf16[16,128,512]{2,1,0:T(8,128)(2,1)}), bf16[16,128,512]{2,1,0:T(8,128)(2,1)}, u32[]{:S(2)}, u32[]{:S(2)}) async-start(bf16[16,128,512]{2,1,0:T(8,128)(2,1)} %bitcast.5), calls=%async_computation.1 | async-start | bytes 4194304 | tf_op jit(solution)/shard_map/all_to_all | solution.py:65
  102.8 0.0 copy-start.14
  102.8 0.0 all-gather.3.cloned.1.call-start
  102.9 0.0 copy-done.2
  102.9 1.2 copy.93
  104.1 0.0 copy-done.11
  104.1 0.0 copy-done.14
  104.2 0.1 fusion.44
  104.2 3.5 fusion.56
  107.7 1.8 divide_convert_fusion
  109.6 1.7 copy.71
  111.3 37.5 %all-to-all-done.1 = bf16[16,128,512]{2,1,0:T(8,128)(2,1)} async-done(((bf16[16,128,512]{2,1,0:T(8,128)(2,1)}), bf16[16,128,512]{2,1,0:T(8,128)(2,1)}, u32[]{:S(2)}, u32[]{:S(2)}) %all-to-all-start.1) | async-done | bytes 2097184 | tf_op jit(solution)/shard_map/all_to_all | solution.py:65
  148.8 1.9 convert_reduce_fusion.1
  150.7 0.1 copy.87
  150.8 1.8 fusion.61
  152.6 2.9 copy.70
  155.5 2.2 fusion.12
  157.7 0.0 copy-start.3
  157.7 0.2 copy.94
  157.9 1.0 copy-done.3
  158.9 1.1 fusion.9
  160.0 0.0 all-gather.3.cloned.1.call-update
  160.1 0.0 all-gather.5.cloned.1.call-start
  160.1 0.2 copy.80
  160.3 0.0 copy-start
  160.3 0.0 copy-start.5
  160.3 81.8 %all-gather.3.cloned.1.call-done = bf16[2048,512]{0,1:T(8,128)(2,1)} async-done(((bf16[128,512]{0,1:T(8,128)(2,1)}), bf16[2048,512]{0,1:T(8,128)(2,1)}) %all-gather.3.cloned.1.call-update) | async-done | bytes 2097168 | tf_op jit(solution)/shard_map/all_gather | solution.py:88
  242.1 2.4 convolution_bitcast_fusion.1
  244.5 0.0 copy-start.9
  244.5 0.8 copy-done.9
  245.3 0.0 copy-done.5
  245.3 0.0 copy-done.7
  245.3 1.1 fusion.6
  246.4 0.0 copy-done
  246.4 0.5 copy.117
  247.0 45.4 %all_to_all.38 = bf16[16,128,512]{1,2,0:T(8,128)(2,1)S(1)} all-to-all(bf16[16,128,512]{1,2,0:T(8,128)(2,1)S(1)} %bitcast.108), channel_id=1, replica_groups=mesh['island'=32,'fsdp'=16] {'fsdp'}, dimensions={0} | all-to-all | bytes 4194304 | tf_op jit(solution)/shard_map/all_to_all | solution.py:65
  292.4 0.3 convert_reduce_fusion
  292.6 0.1 copy.75
  292.8 0.1 copy.90
  292.9 1.8 fusion.62
  294.7 1.9 copy.78
  296.6 1.5 fusion.11
  298.2 0.2 copy.95
  298.4 1.0 copy-done.4
  299.4 1.1 fusion.10
  300.6 0.0 all-gather.5.cloned.1.call-update
  301.2 85.3 %all-gather.5.cloned.1.call-done = bf16[2048,512]{0,1:T(8,128)(2,1)} async-done(((bf16[128,512]{0,1:T(8,128)(2,1)}), bf16[2048,512]{0,1:T(8,128)(2,1)}) %all-gather.5.cloned.1.call-update) | async-done | bytes 2097168 | tf_op jit(solution)/shard_map/all_gather | solution.py:88
  386.5 0.0 copy-done.6
  386.5 3.8 fusion.27
  390.3 1.2 copy.91
  391.6 0.0 copy-start.13
  391.6 0.1 concatenate.3.clone
  391.6 58.3 %all_to_all.39 = f32[257,32,16]{0,2,1:T(8,128)S(1)} all-to-all(f32[257,32,16]{0,2,1:T(8,128)S(1)} %bitcast.110), channel_id=1, replica_groups=mesh['island'=32,'fsdp'=16] {'island'}, dimensions={1} | all-to-all | bytes 1052672 | tf_op jit(solution)/shard_map/all_to_all | solution.py:102
  449.9 0.1 reduce_sum.39
  450.0 0.1 slice_reduce_fusion
  450.1 0.7 multiply_subtract_fusion.1
  (15 shorter events, 0.1 us)
Async XLA Ops:
  7.2 10.7 %copy-start.12 = (f32[256,16]{0,1:T(8,128)S(1)}, f32[256,16]{0,1:T(8,128)}, u32[]{:S(2)}) copy-start(f32[256,16]{0,1:T(8,128)} %param.17) | copy-start | bytes 49156
  9.4 82.0 %all-to-all-start = ((bf16[128,16,256]{0,2,1:T(8,128)(2,1)}), bf16[128,16,256]{0,2,1:T(8,128)(2,1)S(1)}, u32[]{:S(2)}, u32[]{:S(2)}) async-start(bf16[128,16,256]{0,2,1:T(8,128)(2,1)} %bitcast.2), calls=%async_computation | async-start | bytes 2097152 | tf_op jit(solution)/shard_map/all_to_all | solution.py:60
  94.0 8.9 %copy-start.2 = (bf16[128,4096]{1,0:T(8,128)(2,1)S(1)}, bf16[128,4096]{1,0:T(8,128)(2,1)}, u32[]{:S(2)}) copy-start(bf16[128,4096]{1,0:T(8,128)(2,1)} %param.11) | copy-start | bytes 3145732
  94.0 54.8 %all-to-all-start.1 = ((bf16[16,128,512]{2,1,0:T(8,128)(2,1)}), bf16[16,128,512]{2,1,0:T(8,128)(2,1)}, u32[]{:S(2)}, u32[]{:S(2)}) async-start(bf16[16,128,512]{2,1,0:T(8,128)(2,1)} %bitcast.5), calls=%async_computation.1 | async-start | bytes 4194304 | tf_op jit(solution)/shard_map/all_to_all | solution.py:65
  102.8 1.3 copy-start.11
  102.8 1.3 copy-start.14
  102.8 139.3 %all-gather.3.cloned.1.call-start = ((), (), s32[]{:S(2)}) async-start(), calls=%async_computation.4 | async-start | bytes 2228224 | tf_op jit(solution)/shard_map/all_gather | solution.py:88
  157.7 1.2 copy-start.3
  160.1 226.5 %all-gather.5.cloned.1.call-start = ((), (), s32[]{:S(2)}) async-start(), calls=%async_computation.5 | async-start | bytes 2228224 | tf_op jit(solution)/shard_map/all_gather | solution.py:88
  160.3 86.1 %copy-start = (f32[256,512]{1,0:T(8,128)}, f32[256,512]{1,0:T(8,128)S(1)}, u32[]{:S(2)}) copy-start(f32[256,512]{1,0:T(8,128)S(1)} %copy.80) | copy-start | bytes 1572868
  160.3 85.0 %copy-start.5 = (f32[1,256,512]{2,1,0:T(8,128)S(1)}, f32[1,256,512]{2,1,0:T(8,128)}, u32[]{:S(2)}) copy-start(f32[1,256,512]{2,1,0:T(8,128)} %param.15) | copy-start | bytes 1572868
  242.1 3.2 copy-start.7
  244.5 0.8 copy-start.9
  298.2 1.2 copy-start.4
  299.4 87.1 %copy-start.1 = (f32[256,512]{1,0:T(8,128)S(1)}, f32[256,512]{1,0:T(8,128)}, u32[]{:S(2)}) copy-start(f32[256,512]{1,0:T(8,128)} %copy-done) | copy-start | bytes 1572868
  299.4 87.1 %copy-start.6 = (f32[1,256,512]{2,1,0:T(8,128)S(1)}, f32[1,256,512]{2,1,0:T(8,128)}, u32[]{:S(2)}) copy-start(f32[1,256,512]{2,1,0:T(8,128)} %param.15) | copy-start | bytes 1572868
  299.4 87.1 %copy-start.8 = (f32[1,256,512]{2,1,0:T(8,128)S(1)}, f32[1,256,512]{2,1,0:T(8,128)}, u32[]{:S(2)}) copy-start(f32[1,256,512]{2,1,0:T(8,128)} %param.16) | copy-start | bytes 1572868
  299.4 87.1 %copy-start.10 = (f32[256,512]{1,0:T(8,128)S(1)}, f32[256,512]{1,0:T(8,128)}, u32[]{:S(2)}) copy-start(f32[256,512]{1,0:T(8,128)} %copy-done.9) | copy-start | bytes 1572868
  391.6 58.5 %copy-start.13 = (f32[256,16]{0,1:T(8,128)S(1)}, f32[256,16]{0,1:T(8,128)}, u32[]{:S(2)}) copy-start(f32[256,16]{0,1:T(8,128)} %param.18) | copy-start | bytes 49156
Sparse Core Ops, SparseCore 0:
  160.2 81.8 all-gather.2
  300.7 85.7 all-gather.4

commit v2 on v1

--- a/solution.py
+++ b/solution.py
@@ -34,6 +34,36 @@
     return (expo / jnp.sum(expo, axis=-1, keepdims=True)).astype(jnp.bfloat16)
 
 
+def _shift(cols, rows, dx, dz):
+    return [
+        (a * cols + b, ((a + dx) % rows) * cols + (b + dz) % cols)
+        for a in range(rows)
+        for b in range(cols)
+    ]
+
+
+def ring_offsets(size):
+    return [0, -1, 1, -2][:size] if size == 4 else list(range(0, -size, -1))
+
+
+def ring_gather(piece, rows, cols):
+    def along(part, size, dx, dz):
+        if size == 1:
+            return [part]
+        if size == 4:
+            up = lax.ppermute(part, "fsdp", _shift(cols, rows, dx, dz))
+            down = lax.ppermute(part, "fsdp", _shift(cols, rows, -dx, -dz))
+            far = lax.ppermute(up, "fsdp", _shift(cols, rows, dx, dz))
+            return [part, up, down, far]
+        got = [part]
+        for _ in range(size - 1):
+            got.append(lax.ppermute(got[-1], "fsdp", _shift(cols, rows, dx, dz)))
+        return got
+
+    row = jnp.concatenate(along(piece, cols, 0, 1), axis=0)
+    return jnp.concatenate(along(row, rows, 1, 0), axis=0)
+
+
 def on_device(
     hidden,
     query_rows,
@@ -52,12 +82,28 @@
     group_rows = rows * members
     scale_in = 1.0 / math.sqrt(hidden.shape[1])
     attention = attention_weights(query_rows, key_rows, segment_ids[0])
-    master = lax.all_gather(anchor, "island", axis=1, tiled=True)
+    groups = lax.axis_size("island")
+    copies = jnp.broadcast_to(anchor[None], (groups,) + anchor.shape)
+    master = (
+        lax.all_to_all(copies, "island", split_axis=0, concat_axis=0, tiled=True)
+        .transpose(1, 0, 2)
+        .reshape(anchor.shape[0], groups * anchor.shape[1])
+    )
     start_point = master
     block = master.shape[0]
     first = first_moment[0]
     second = second_moment[0]
     feature_rows = lax.all_to_all(hidden, "fsdp", split_axis=1, concat_axis=0, tiled=True)
+    grid_cols = 4 if members % 4 == 0 else 1
+    grid_rows = members // grid_cols
+    me = lax.axis_index("fsdp")
+    me_x, me_z = me // grid_cols, me % grid_cols
+    take_x = (me_x + jnp.array(ring_offsets(grid_rows))) % grid_rows
+    take_z = (me_z + jnp.array(ring_offsets(grid_cols))) % grid_cols
+    order = (take_x[:, None] * grid_cols + take_z[None, :]).reshape(-1)
+    ring_rows = jnp.take(
+        feature_rows.reshape(members, rows, block), order, axis=0
+    ).reshape(group_rows, block)
     for inner_step in range(2):
         partial = jnp.dot(
             feature_rows, master.astype(jnp.bfloat16), preferred_element_type=jnp.float32
@@ -84,8 +130,8 @@
         )
         value_grad = (back.reshape(rows, width) * scale_in).astype(jnp.bfloat16)
         grad = lax.dot_general(
-            feature_rows,
-            lax.all_gather(value_grad, "fsdp", axis=0, tiled=True),
+            ring_rows,
+            ring_gather(value_grad, grid_rows, grid_cols),
             (((0,), (0,)), ((), ())),
             preferred_element_type=jnp.float32,
         )
@@ -93,7 +139,6 @@
         second = beta_two * second + (1.0 - beta_two) * grad * grad
         master = master - inner_rate * (first / (jnp.sqrt(second) + epsilon) + decay * master)
     delta = start_point - master
-    groups = lax.axis_size("island")
     cols = anchor.shape[1]
     own_count = token_counts[0].astype(jnp.float32)
     weighted = jnp.concatenate(

time: 458 us -> 357 us (0.78)
  the two profiles are of different devices: /device:TPU:64 before, /device:TPU:1 now
where the time goes in v2:
time: 357 us; the launch traced here: 356 us
  waiting for transfers between devices  131 us (37%)
  blocking collectives  110 us (31%)
  starting transfers between devices  69.8 us (20%)
  local copies, waits for them, and re-layouts  19.3 us (5%)
  matrix products  13.3 us (4%)
  other arithmetic  10.3 us (3%)
    all_to_all x1, blocking collectives, on_device(): lax.all_to_all(partial.reshape(members, rows, width), 'fsdp', split_axis=...  56.4 us
    all_to_all x1, blocking collectives, on_device(): lax.all_to_all(weighted.reshape(block + 1, groups, cols), 'island', split...  53.9 us
    all_to_all x1, waiting for transfers between devices, on_device(): lax.all_to_all(partial.reshape(members, rows, width), 'fsdp', split_axis=...  41.1 us
    all_to_all x1, waiting for transfers between devices, on_device(): lax.all_to_all(hidden, 'fsdp', split_axis=1, concat_axis=0, tiled=True)  27 us
    all_to_all x1, waiting for transfers between devices, on_device(): lax.all_to_all(copies, 'island', split_axis=0, concat_axis=0, tiled=True)  26.6 us
    ppermute x4, waiting for transfers between devices, along(): far = lax.ppermute(up, 'fsdp', _shift(cols, rows, dx, dz))  26.1 us
    ppermute x4, starting transfers between devices, along(): down = lax.ppermute(part, 'fsdp', _shift(cols, rows, -dx, -dz))  19.7 us
    all_to_all x1, starting transfers between devices, on_device(): lax.all_to_all(copies, 'island', split_axis=0, concat_axis=0, tiled=True)  19.4 us
  transfers between devices with their start and end apart: 15, of which 12 were waited for; matrix products, arithmetic and copies ran while one was open for 4% of the time, Pallas kernels for 0%

profile of v2, /device:TPU:1, one launch (start us, length us, event | category | flops | bytes accessed | tf_op | source)
XLA Modules:
  0.0 356.2 jit_solution(14722565123456112493)
XLA Ops:
  0.6 1.7 broadcast_in_dim.40
  2.3 19.4 %all-to-all-start = ((f32[32,256,16]{1,2,0:T(8,128)}), f32[32,256,16]{1,2,0:T(8,128)S(1)}, u32[]{:S(2)}, u32[]{:S(2)}) async-start(f32[32,256,16]{1,2,0:T(8,128)} %broadcast_in_dim.40), calls=%async_computation | async-start | bytes 1048576 | tf_op jit(solution)/shard_map/all_to_all | solution.py:88
  21.7 0.7 copy.70
  22.4 1.3 copy.71
  23.7 26.6 %all-to-all-done = f32[32,256,16]{1,2,0:T(8,128)S(1)} async-done(((f32[32,256,16]{1,2,0:T(8,128)}), f32[32,256,16]{1,2,0:T(8,128)S(1)}, u32[]{:S(2)}, u32[]{:S(2)}) %all-to-all-start) | async-done | bytes 524320 | tf_op jit(solution)/shard_map/all_to_all | solution.py:88
  50.3 10.8 %all-to-all-start.1 = ((bf16[128,16,256]{2,0,1:T(8,128)(2,1)}), bf16[128,16,256]{2,0,1:T(8,128)(2,1)S(1)}, u32[]{:S(2)}, u32[]{:S(2)}) async-start(bf16[128,16,256]{2,0,1:T(8,128)(2,1)} %copy.71), calls=%async_computation.1 | async-start | bytes 2097152 | tf_op jit(solution)/shard_map/all_to_all | solution.py:96
  61.2 27.0 %all-to-all-done.1 = bf16[128,16,256]{2,0,1:T(8,128)(2,1)S(1)} async-done(((bf16[128,16,256]{2,0,1:T(8,128)(2,1)}), bf16[128,16,256]{2,0,1:T(8,128)(2,1)S(1)}, u32[]{:S(2)}, u32[]{:S(2)}) %all-to-all-start.1) | async-done | bytes 1048608 | tf_op jit(solution)/shard_map/all_to_all | solution.py:96
  88.2 2.0 convolution_convert_fusion.1
  90.2 4.6 %all-to-all-start.2 = ((bf16[16,128,512]{2,1,0:T(8,128)(2,1)}), bf16[16,128,512]{2,1,0:T(8,128)(2,1)}, u32[]{:S(2)}, u32[]{:S(2)}) async-start(bf16[16,128,512]{2,1,0:T(8,128)(2,1)} %bitcast.12), calls=%async_computation.2 | async-start | bytes 4194304 | tf_op jit(solution)/shard_map/all_to_all | solution.py:111
  95.1 1.2 copy.99
  96.4 3.5 fusion.59
  100.0 1.8 divide_convert_fusion
  101.8 1.7 copy.77
  103.5 41.1 %all-to-all-done.2 = bf16[16,128,512]{2,1,0:T(8,128)(2,1)} async-done(((bf16[16,128,512]{2,1,0:T(8,128)(2,1)}), bf16[16,128,512]{2,1,0:T(8,128)(2,1)}, u32[]{:S(2)}, u32[]{:S(2)}) %all-to-all-start.2) | async-done | bytes 2097184 | tf_op jit(solution)/shard_map/all_to_all | solution.py:111
  144.6 1.9 convert_reduce_fusion.1
  146.7 1.8 fusion.64
  148.4 2.9 copy.76
  151.4 2.2 fusion.12
  153.5 0.2 copy.100
  153.8 1.0 copy-done.6
  154.7 0.5 fusion.9
  155.2 1.9 collective-permute-start
  157.2 5.2 %collective-permute-start.1 = (bf16[128,512]{0,1:T(8,128)(2,1)S(1)}, bf16[128,512]{0,1:T(8,128)(2,1)S(1)}, u32[]{:S(2)}, u32[]{:S(2)}) collective-permute-start(bf16[128,512]{0,1:T(8,128)(2,1)S(1)} %bitcast.124), channel_id=1, source_target_pairs={{0,3},{1,0},{2,1},{3,2},{4,7},{5,4},{6,5},{7,6},{8,11},{9,8},{10,9... | collective-permute-start | bytes 393224 | tf_op jit(solution)/shard_map/ppermute | solution.py:55
  162.4 0.5 collective-permute-done
  162.9 1.9 collective-permute-start.2
  164.9 1.0 copy.86
  165.9 0.6 gather_fusion
  166.5 0.5 collective-permute-done.1
  167.0 3.6 %collective-permute-done.2 = bf16[128,512]{0,1:T(8,128)(2,1)} collective-permute-done((bf16[128,512]{0,1:T(8,128)(2,1)S(1)}, bf16[128,512]{0,1:T(8,128)(2,1)}, u32[]{:S(2)}, u32[]{:S(2)}) %collective-permute-start.2) | collective-permute-done | bytes 131104 | tf_op jit(solution)/shard_map/ppermute | solution.py:56
  170.5 1.0 pad_maximum_fusion
  171.5 1.9 collective-permute-start.3
  173.4 0.5 bitcast_select_fusion.2
  174.0 4.6 %collective-permute-start.4 = (bf16[512,512]{0,1:T(8,128)(2,1)S(1)}, bf16[512,512]{0,1:T(8,128)(2,1)S(1)}, u32[]{:S(2)}, u32[]{:S(2)}) collective-permute-start(bf16[512,512]{0,1:T(8,128)(2,1)S(1)} %pad_maximum_fusion), channel_id=1, source_target_pairs={{0,12},{1,13},{2,14},{3,15},{4,0},{5,1},{6,2},{7,3},{8,4},{9,5},{1... | collective-permute-start | bytes 1572872 | tf_op jit(solution)/shard_map/ppermute | solution.py:55
  178.6 4.7 %collective-permute-done.3 = bf16[512,512]{0,1:T(8,128)(2,1)S(1)} collective-permute-done((bf16[512,512]{0,1:T(8,128)(2,1)S(1)}, bf16[512,512]{0,1:T(8,128)(2,1)S(1)}, u32[]{:S(2)}, u32[]{:S(2)}) %collective-permute-start.3) | collective-permute-done | bytes 524320 | tf_op jit(solution)/shard_map/ppermute | solution.py:54
  183.3 1.9 collective-permute-start.5
  185.3 0.9 constant_dynamic-update-slice_fusion.3
  186.4 8.0 %collective-permute-done.5 = bf16[512,512]{0,1:T(8,128)(2,1)S(1)} collective-permute-done((bf16[512,512]{0,1:T(8,128)(2,1)S(1)}, bf16[512,512]{0,1:T(8,128)(2,1)S(1)}, u32[]{:S(2)}, u32[]{:S(2)}) %collective-permute-start.5) | collective-permute-done | bytes 524320 | tf_op jit(solution)/shard_map/ppermute | solution.py:56
  194.6 0.8 fusion.65
  195.3 0.8 copy-done.12
  196.1 1.1 fusion.6
  197.2 0.5 copy.123
  197.8 56.4 %all_to_all.43 = bf16[16,128,512]{1,2,0:T(8,128)(2,1)S(1)} all-to-all(bf16[16,128,512]{1,2,0:T(8,128)(2,1)S(1)} %bitcast.112), channel_id=1, replica_groups=mesh['island'=32,'fsdp'=16] {'fsdp'}, dimensions={0} | all-to-all | bytes 4194304 | tf_op jit(solution)/shard_map/all_to_all | solution.py:111
  254.2 0.3 convert_reduce_fusion
  254.5 0.1 copy.81
  254.7 1.8 fusion.66
  256.5 1.9 copy.84
  258.4 1.5 fusion.11
  260.0 0.2 copy.101
  260.2 1.0 copy-done.7
  261.2 0.5 fusion.10
  261.7 1.9 collective-permute-start.6
  263.6 5.2 %collective-permute-start.7 = (bf16[128,512]{0,1:T(8,128)(2,1)S(1)}, bf16[128,512]{0,1:T(8,128)(2,1)S(1)}, u32[]{:S(2)}, u32[]{:S(2)}) collective-permute-start(bf16[128,512]{0,1:T(8,128)(2,1)S(1)} %bitcast.128), channel_id=1, source_target_pairs={{0,3},{1,0},{2,1},{3,2},{4,7},{5,4},{6,5},{7,6},{8,11},{9,8},{10,9... | collective-permute-start | bytes 393224 | tf_op jit(solution)/shard_map/ppermute | solution.py:55
  268.8 0.6 collective-permute-done.6
  269.4 1.9 collective-permute-start.8
  271.3 5.6 %collective-permute-done.8 = bf16[128,512]{0,1:T(8,128)(2,1)S(1)} collective-permute-done((bf16[128,512]{0,1:T(8,128)(2,1)S(1)}, bf16[128,512]{0,1:T(8,128)(2,1)S(1)}, u32[]{:S(2)}, u32[]{:S(2)}) %collective-permute-start.8) | collective-permute-done | bytes 131104 | tf_op jit(solution)/shard_map/ppermute | solution.py:56
  277.0 1.9 collective-permute-start.9
  279.6 4.8 %collective-permute-start.10 = (bf16[512,512]{0,1:T(8,128)(2,1)S(1)}, bf16[512,512]{0,1:T(8,128)(2,1)S(1)}, u32[]{:S(2)}, u32[]{:S(2)}) collective-permute-start(bf16[512,512]{0,1:T(8,128)(2,1)S(1)} %pad_maximum_fusion.1), channel_id=1, source_target_pairs={{0,12},{1,13},{2,14},{3,15},{4,0},{5,1},{6,2},{7,3},{8,4},{9,5},{1... | collective-permute-start | bytes 1572872 | tf_op jit(solution)/shard_map/ppermute | solution.py:55
  284.5 4.0 %collective-permute-done.9 = bf16[512,512]{0,1:T(8,128)(2,1)S(1)} collective-permute-done((bf16[512,512]{0,1:T(8,128)(2,1)S(1)}, bf16[512,512]{0,1:T(8,128)(2,1)S(1)}, u32[]{:S(2)}, u32[]{:S(2)}) %collective-permute-start.9) | collective-permute-done | bytes 524320 | tf_op jit(solution)/shard_map/ppermute | solution.py:54
  288.5 1.9 collective-permute-start.11
  290.7 8.9 %collective-permute-done.11 = bf16[512,512]{0,1:T(8,128)(2,1)S(1)} collective-permute-done((bf16[512,512]{0,1:T(8,128)(2,1)S(1)}, bf16[512,512]{0,1:T(8,128)(2,1)S(1)}, u32[]{:S(2)}, u32[]{:S(2)}) %collective-permute-start.11) | collective-permute-done | bytes 524320 | tf_op jit(solution)/shard_map/ppermute | solution.py:56
  299.7 1.4 fusion.27
  301.1 0.2 copy.97
  301.4 53.9 %all_to_all.44 = f32[257,32,16]{0,2,1:T(8,128)S(1)} all-to-all(f32[257,32,16]{0,2,1:T(8,128)S(1)} %bitcast.115), channel_id=1, replica_groups=mesh['island'=32,'fsdp'=16] {'island'}, dimensions={1} | all-to-all | bytes 1052672 | tf_op jit(solution)/shard_map/all_to_all | solution.py:147
  355.5 0.7 multiply_subtract_fusion.1
  (70 shorter events, 1.8 us)
Async XLA Ops:
  0.6 21.1 %copy-start.4 = (bf16[128,4096]{1,0:T(8,128)(2,1)S(1)}, bf16[128,4096]{1,0:T(8,128)(2,1)}, u32[]{:S(2)}) copy-start(bf16[128,4096]{1,0:T(8,128)(2,1)} %param.12) | copy-start | bytes 3145732
  2.3 48.0 %all-to-all-start = ((f32[32,256,16]{1,2,0:T(8,128)}), f32[32,256,16]{1,2,0:T(8,128)S(1)}, u32[]{:S(2)}, u32[]{:S(2)}) async-start(f32[32,256,16]{1,2,0:T(8,128)} %broadcast_in_dim.40), calls=%async_computation | async-start | bytes 1048576 | tf_op jit(solution)/shard_map/all_to_all | solution.py:88
  50.3 37.9 %all-to-all-start.1 = ((bf16[128,16,256]{2,0,1:T(8,128)(2,1)}), bf16[128,16,256]{2,0,1:T(8,128)(2,1)S(1)}, u32[]{:S(2)}, u32[]{:S(2)}) async-start(bf16[128,16,256]{2,0,1:T(8,128)(2,1)} %copy.71), calls=%async_computation.1 | async-start | bytes 2097152 | tf_op jit(solution)/shard_map/all_to_all | solution.py:96
  90.2 4.6 %copy-start.18 = (s32[4]{0:T(128)S(1)}, s32[4]{0:T(128)}, u32[]{:S(2)}) copy-start(s32[4]{0:T(128)} %constant.86.clone) | copy-start | bytes 52
  90.2 4.9 %copy-start.5 = (bf16[128,4096]{1,0:T(8,128)(2,1)S(1)}, bf16[128,4096]{1,0:T(8,128)(2,1)}, u32[]{:S(2)}) copy-start(bf16[128,4096]{1,0:T(8,128)(2,1)} %param.13) | copy-start | bytes 3145732
  90.2 54.4 %all-to-all-start.2 = ((bf16[16,128,512]{2,1,0:T(8,128)(2,1)}), bf16[16,128,512]{2,1,0:T(8,128)(2,1)}, u32[]{:S(2)}, u32[]{:S(2)}) async-start(bf16[16,128,512]{2,1,0:T(8,128)(2,1)} %bitcast.12), calls=%async_computation.2 | async-start | bytes 4194304 | tf_op jit(solution)/shard_map/all_to_all | solution.py:111
  94.8 1.5 copy-start.14
  94.8 1.6 copy-start.17
  153.5 1.2 copy-start.6
  155.2 7.7 %collective-permute-start = (bf16[128,512]{0,1:T(8,128)(2,1)S(1)}, bf16[128,512]{0,1:T(8,128)(2,1)S(1)}, u32[]{:S(2)}, u32[]{:S(2)}) collective-permute-start(bf16[128,512]{0,1:T(8,128)(2,1)S(1)} %bitcast.123), channel_id=1, source_target_pairs={{0,1},{1,2},{2,3},{3,0},{4,5},{5,6},{6,7},{7,4},{8,9},{9,10},{10,1... | collective-permute-start | bytes 393224 | tf_op jit(solution)/shard_map/ppermute | solution.py:54
  157.2 9.7 %collective-permute-start.1 = (bf16[128,512]{0,1:T(8,128)(2,1)S(1)}, bf16[128,512]{0,1:T(8,128)(2,1)S(1)}, u32[]{:S(2)}, u32[]{:S(2)}) collective-permute-start(bf16[128,512]{0,1:T(8,128)(2,1)S(1)} %bitcast.124), channel_id=1, source_target_pairs={{0,3},{1,0},{2,1},{3,2},{4,7},{5,4},{6,5},{7,6},{8,11},{9,8},{10,9... | collective-permute-start | bytes 393224 | tf_op jit(solution)/shard_map/ppermute | solution.py:55
  162.9 7.6 %collective-permute-start.2 = (bf16[128,512]{0,1:T(8,128)(2,1)S(1)}, bf16[128,512]{0,1:T(8,128)(2,1)}, u32[]{:S(2)}, u32[]{:S(2)}) collective-permute-start(bf16[128,512]{0,1:T(8,128)(2,1)S(1)} %collective-permute-done), channel_id=1, source_target_pairs={{0,1},{1,2},{2,3},{3,0},{4,5},{5,6},{6,7},{7,4},{8,9},{9,10},{10,1... | collective-permute-start | bytes 393224 | tf_op jit(solution)/shard_map/ppermute | solution.py:56
  171.5 11.8 %collective-permute-start.3 = (bf16[512,512]{0,1:T(8,128)(2,1)S(1)}, bf16[512,512]{0,1:T(8,128)(2,1)S(1)}, u32[]{:S(2)}, u32[]{:S(2)}) collective-permute-start(bf16[512,512]{0,1:T(8,128)(2,1)S(1)} %pad_maximum_fusion), channel_id=1, source_target_pairs={{0,4},{1,5},{2,6},{3,7},{4,8},{5,9},{6,10},{7,11},{8,12},{9,13},{1... | collective-permute-start | bytes 1572872 | tf_op jit(solution)/shard_map/ppermute | solution.py:54
  174.0 20.5 %copy-start.2 = (bf16[2048,256]{1,0:T(8,128)(2,1)}, bf16[2048,256]{1,0:T(8,128)(2,1)S(1)}, u32[]{:S(2)}) copy-start(bf16[2048,256]{1,0:T(8,128)(2,1)S(1)} %bitcast_select_fusion.2) | copy-start | bytes 3145732
  174.0 12.4 %collective-permute-start.4 = (bf16[512,512]{0,1:T(8,128)(2,1)S(1)}, bf16[512,512]{0,1:T(8,128)(2,1)S(1)}, u32[]{:S(2)}, u32[]{:S(2)}) collective-permute-start(bf16[512,512]{0,1:T(8,128)(2,1)S(1)} %pad_maximum_fusion), channel_id=1, source_target_pairs={{0,12},{1,13},{2,14},{3,15},{4,0},{5,1},{6,2},{7,3},{8,4},{9,5},{1... | collective-permute-start | bytes 1572872 | tf_op jit(solution)/shard_map/ppermute | solution.py:55
  183.3 11.1 %collective-permute-start.5 = (bf16[512,512]{0,1:T(8,128)(2,1)S(1)}, bf16[512,512]{0,1:T(8,128)(2,1)S(1)}, u32[]{:S(2)}, u32[]{:S(2)}) collective-permute-start(bf16[512,512]{0,1:T(8,128)(2,1)S(1)} %collective-permute-done.3), channel_id=1, source_target_pairs={{0,4},{1,5},{2,6},{3,7},{4,8},{5,9},{6,10},{7,11},{8,12},{9,13},{1... | collective-permute-start | bytes 1572872 | tf_op jit(solution)/shard_map/ppermute | solution.py:56
  194.5 1.6 copy-start
  194.6 1.6 copy-start.8
  194.6 1.6 copy-start.10
  195.3 0.8 copy-start.12
  260.0 1.2 copy-start.7
  261.7 7.7 %collective-permute-start.6 = (bf16[128,512]{0,1:T(8,128)(2,1)S(1)}, bf16[128,512]{0,1:T(8,128)(2,1)S(1)}, u32[]{:S(2)}, u32[]{:S(2)}) collective-permute-start(bf16[128,512]{0,1:T(8,128)(2,1)S(1)} %bitcast.127), channel_id=1, source_target_pairs={{0,1},{1,2},{2,3},{3,0},{4,5},{5,6},{6,7},{7,4},{8,9},{9,10},{10,1... | collective-permute-start | bytes 393224 | tf_op jit(solution)/shard_map/ppermute | solution.py:54
  263.6 7.7 %collective-permute-start.7 = (bf16[128,512]{0,1:T(8,128)(2,1)S(1)}, bf16[128,512]{0,1:T(8,128)(2,1)S(1)}, u32[]{:S(2)}, u32[]{:S(2)}) collective-permute-start(bf16[128,512]{0,1:T(8,128)(2,1)S(1)} %bitcast.128), channel_id=1, source_target_pairs={{0,3},{1,0},{2,1},{3,2},{4,7},{5,4},{6,5},{7,6},{8,11},{9,8},{10,9... | collective-permute-start | bytes 393224 | tf_op jit(solution)/shard_map/ppermute | solution.py:55
  269.4 7.5 %collective-permute-start.8 = (bf16[128,512]{0,1:T(8,128)(2,1)S(1)}, bf16[128,512]{0,1:T(8,128)(2,1)S(1)}, u32[]{:S(2)}, u32[]{:S(2)}) collective-permute-start(bf16[128,512]{0,1:T(8,128)(2,1)S(1)} %collective-permute-done.6), channel_id=1, source_target_pairs={{0,1},{1,2},{2,3},{3,0},{4,5},{5,6},{6,7},{7,4},{8,9},{9,10},{10,1... | collective-permute-start | bytes 393224 | tf_op jit(solution)/shard_map/ppermute | solution.py:56
  277.0 11.5 %collective-permute-start.9 = (bf16[512,512]{0,1:T(8,128)(2,1)S(1)}, bf16[512,512]{0,1:T(8,128)(2,1)S(1)}, u32[]{:S(2)}, u32[]{:S(2)}) collective-permute-start(bf16[512,512]{0,1:T(8,128)(2,1)S(1)} %pad_maximum_fusion.1), channel_id=1, source_target_pairs={{0,4},{1,5},{2,6},{3,7},{4,8},{5,9},{6,10},{7,11},{8,12},{9,13},{1... | collective-permute-start | bytes 1572872 | tf_op jit(solution)/shard_map/ppermute | solution.py:54
  279.5 20.1 %copy-start.1 = (f32[256,512]{1,0:T(8,128)S(1)}, f32[256,512]{1,0:T(8,128)}, u32[]{:S(2)}) copy-start(f32[256,512]{1,0:T(8,128)} %copy.86) | copy-start | bytes 1572868
  279.5 20.1 %copy-start.3 = (bf16[2048,256]{1,0:T(8,128)(2,1)S(1)}, bf16[2048,256]{1,0:T(8,128)(2,1)}, u32[]{:S(2)}) copy-start(bf16[2048,256]{1,0:T(8,128)(2,1)} %copy-done.2) | copy-start | bytes 3145732
  279.6 20.1 %copy-start.9 = (f32[1,256,512]{2,1,0:T(8,128)S(1)}, f32[1,256,512]{2,1,0:T(8,128)}, u32[]{:S(2)}) copy-start(f32[1,256,512]{2,1,0:T(8,128)} %param.17) | copy-start | bytes 1572868
  279.6 20.1 %copy-start.11 = (f32[1,256,512]{2,1,0:T(8,128)S(1)}, f32[1,256,512]{2,1,0:T(8,128)}, u32[]{:S(2)}) copy-start(f32[1,256,512]{2,1,0:T(8,128)} %param.18) | copy-start | bytes 1572868
  279.6 20.1 %copy-start.13 = (f32[256,512]{1,0:T(8,128)S(1)}, f32[256,512]{1,0:T(8,128)}, u32[]{:S(2)}) copy-start(f32[256,512]{1,0:T(8,128)} %copy-done.12) | copy-start | bytes 1572868
  279.6 11.0 %collective-permute-start.10 = (bf16[512,512]{0,1:T(8,128)(2,1)S(1)}, bf16[512,512]{0,1:T(8,128)(2,1)S(1)}, u32[]{:S(2)}, u32[]{:S(2)}) collective-permute-start(bf16[512,512]{0,1:T(8,128)(2,1)S(1)} %pad_maximum_fusion.1), channel_id=1, source_target_pairs={{0,12},{1,13},{2,14},{3,15},{4,0},{5,1},{6,2},{7,3},{8,4},{9,5},{1... | collective-permute-start | bytes 1572872 | tf_op jit(solution)/shard_map/ppermute | solution.py:55
  288.5 11.1 %collective-permute-start.11 = (bf16[512,512]{0,1:T(8,128)(2,1)S(1)}, bf16[512,512]{0,1:T(8,128)(2,1)S(1)}, u32[]{:S(2)}, u32[]{:S(2)}) collective-permute-start(bf16[512,512]{0,1:T(8,128)(2,1)S(1)} %collective-permute-done.9), channel_id=1, source_target_pairs={{0,4},{1,5},{2,6},{3,7},{4,8},{5,9},{6,10},{7,11},{8,12},{9,13},{1... | collective-permute-start | bytes 1572872 | tf_op jit(solution)/shard_map/ppermute | solution.py:56
  301.3 54.2 %copy-start.15 = (f32[256,16]{0,1:T(8,128)S(1)}, f32[256,16]{0,1:T(8,128)}, u32[]{:S(2)}) copy-start(f32[256,16]{0,1:T(8,128)} %param.19) | copy-start | bytes 49156
  301.3 54.2 %copy-start.16 = (f32[256,16]{0,1:T(8,128)S(1)}, f32[256,16]{0,1:T(8,128)}, u32[]{:S(2)}) copy-start(f32[256,16]{0,1:T(8,128)} %param.20) | copy-start | bytes 49156

commit v3 on v2

--- a/solution.py
+++ b/solution.py
@@ -8,6 +8,7 @@
 KVH = 4
 QPK = 8
 HD = 128
+CHUNKS = 2
 
 
 beta_one = 0.9
@@ -104,40 +105,55 @@
     ring_rows = jnp.take(
         feature_rows.reshape(members, rows, block), order, axis=0
     ).reshape(group_rows, block)
+    heads = KVH // CHUNKS
+    span = heads * HD
+    wide = heads * QPK * HD
+    weights = [master[:, c * span : (c + 1) * span] for c in range(CHUNKS)]
+    firsts = [first[:, c * span : (c + 1) * span] for c in range(CHUNKS)]
+    seconds = [second[:, c * span : (c + 1) * span] for c in range(CHUNKS)]
     for inner_step in range(2):
-        partial = jnp.dot(
-            feature_rows, master.astype(jnp.bfloat16), preferred_element_type=jnp.float32
-        ).astype(jnp.bfloat16)
-        pieces = lax.all_to_all(
-            partial.reshape(members, rows, width), "fsdp", split_axis=0, concat_axis=0, tiled=True
-        )
-        projected = jnp.sum(pieces.astype(jnp.float32), axis=0)
-        values = (projected * scale_in).astype(jnp.bfloat16)
-        mixed = jnp.einsum(
-            "gjts,sgd->tgjd",
-            attention,
-            values.reshape(rows, KVH, HD),
-            preferred_element_type=jnp.float32,
-        )
-        error = (
-            (mixed.reshape(rows, KVH * QPK * HD) - targets.astype(jnp.float32)) / group_rows
-        ).astype(jnp.bfloat16)
-        back = jnp.einsum(
-            "gjts,tgjd->sgd",
-            attention,
-            error.reshape(rows, KVH, QPK, HD),
-            preferred_element_type=jnp.float32,
-        )
-        value_grad = (back.reshape(rows, width) * scale_in).astype(jnp.bfloat16)
-        grad = lax.dot_general(
-            ring_rows,
-            ring_gather(value_grad, grid_rows, grid_cols),
-            (((0,), (0,)), ((), ())),
-            preferred_element_type=jnp.float32,
-        )
-        first = beta_one * first + (1.0 - beta_one) * grad
-        second = beta_two * second + (1.0 - beta_two) * grad * grad
-        master = master - inner_rate * (first / (jnp.sqrt(second) + epsilon) + decay * master)
+        for c in range(CHUNKS):
+            partial = jnp.dot(
+                feature_rows, weights[c].astype(jnp.bfloat16), preferred_element_type=jnp.float32
+            ).astype(jnp.bfloat16)
+            pieces = lax.all_to_all(
+                partial.reshape(members, rows, span), "fsdp", split_axis=0, concat_axis=0, tiled=True
+            )
+            projected = jnp.sum(pieces.astype(jnp.float32), axis=0)
+            values = (projected * scale_in).astype(jnp.bfloat16)
+            own_attention = attention[c * heads : (c + 1) * heads]
+            mixed = jnp.einsum(
+                "gjts,sgd->tgjd",
+                own_attention,
+                values.reshape(rows, heads, HD),
+                preferred_element_type=jnp.float32,
+            )
+            error = (
+                (
+                    mixed.reshape(rows, wide)
+                    - targets[:, c * wide : (c + 1) * wide].astype(jnp.float32)
+                )
+                / group_rows
+            ).astype(jnp.bfloat16)
+            back = jnp.einsum(
+                "gjts,tgjd->sgd",
+                own_attention,
+                error.reshape(rows, heads, QPK, HD),
+                preferred_element_type=jnp.float32,
+            )
+            value_grad = (back.reshape(rows, span) * scale_in).astype(jnp.bfloat16)
+            grad = lax.dot_general(
+                ring_rows,
+                ring_gather(value_grad, grid_rows, grid_cols),
+                (((0,), (0,)), ((), ())),
+                preferred_element_type=jnp.float32,
+            )
+            firsts[c] = beta_one * firsts[c] + (1.0 - beta_one) * grad
+            seconds[c] = beta_two * seconds[c] + (1.0 - beta_two) * grad * grad
+            weights[c] = weights[c] - inner_rate * (
+                firsts[c] / (jnp.sqrt(seconds[c]) + epsilon) + decay * weights[c]
+            )
+    master = jnp.concatenate(weights, axis=1)
     delta = start_point - master
     cols = anchor.shape[1]
     own_count = token_counts[0].astype(jnp.float32)

time: 357 us -> 384 us (1.076)
  starting transfers between devices: 69.8 us -> 115 us
  blocking collectives: 110 us -> 90 us
  waiting for transfers between devices: 131 us -> 116 us
  local copies, waits for them, and re-layouts: 19.3 us -> 29.8 us
    all_to_all x1, blocking collectives: 56.4 us -> 37.6 us  [on_device(): lax.all_to_all(hidden, 'fsdp', split_axis=1, concat_axis=0, tiled=True)]
    all_to_all x2 -> x4, waiting for transfers between devices: 68.1 us -> 49.4 us  [on_device(): lax.all_to_all(partial.reshape(members, rows, span), 'fsdp', split_axis=0...]
    ppermute x4 -> x8, starting transfers between devices: 19.7 us -> 36.8 us  [along(): down = lax.ppermute(part, 'fsdp', _shift(cols, rows, -dx, -dz))]
    ppermute x4 -> x8, starting transfers between devices: 7.64 us -> 23.5 us  [along(): far = lax.ppermute(up, 'fsdp', _shift(cols, rows, dx, dz))]
    ppermute x4 -> x8, starting transfers between devices: 7.68 us -> 17.8 us  [along(): up = lax.ppermute(part, 'fsdp', _shift(cols, rows, dx, dz))]
    slice x0 -> x3, local copies, waits for them, and re-layouts: none -> 5.52 us  [on_device(): own_attention = attention[c * heads:(c + 1) * heads]]
    reshape x4 -> x6, local copies, waits for them, and re-layouts: 6.34 us -> 9.3 us  [the longest x4 6.78 us: on_device(): mixed.reshape(rows, wide)]
    all_to_all x2 -> x4, starting transfers between devices: 15.4 us -> 18 us  [on_device(): lax.all_to_all(partial.reshape(members, rows, span), 'fsdp', split_axis=0...]
  transfers between devices with their start and end apart: 15 -> 29, of which waited for: 12 -> 16; matrix products, arithmetic and copies ran while one was open for 4% -> 11% of each run, Pallas kernels for 0% -> 0%
where the time goes in v3:
time: 384 us; the launch traced here: 382 us
  waiting for transfers between devices  116 us (30%)
  starting transfers between devices  115 us (30%)
  blocking collectives  90 us (23%)
  local copies, waits for them, and re-layouts  29.8 us (8%)
  matrix products  15.7 us (4%)
  other arithmetic  13.5 us (4%)
    all_to_all x1, blocking collectives, on_device(): lax.all_to_all(weighted.reshape(block + 1, groups, cols), 'island', split...  52.4 us
    all_to_all x4, waiting for transfers between devices, on_device(): lax.all_to_all(partial.reshape(members, rows, span), 'fsdp', split_axis=0...  49.4 us
    all_to_all x1, blocking collectives, on_device(): lax.all_to_all(hidden, 'fsdp', split_axis=1, concat_axis=0, tiled=True)  37.6 us
    ppermute x8, starting transfers between devices, along(): down = lax.ppermute(part, 'fsdp', _shift(cols, rows, -dx, -dz))  36.8 us
    ppermute x8, waiting for transfers between devices, along(): far = lax.ppermute(up, 'fsdp', _shift(cols, rows, dx, dz))  28.6 us
    all_to_all x1, waiting for transfers between devices, on_device(): lax.all_to_all(copies, 'island', split_axis=0, concat_axis=0, tiled=True)  27.4 us
    ppermute x8, starting transfers between devices, along(): far = lax.ppermute(up, 'fsdp', _shift(cols, rows, dx, dz))  23.5 us
    all_to_all x1, starting transfers between devices, on_device(): lax.all_to_all(copies, 'island', split_axis=0, concat_axis=0, tiled=True)  19.4 us
  transfers between devices with their start and end apart: 29, of which 16 were waited for; matrix products, arithmetic and copies ran while one was open for 11% of the time, Pallas kernels for 0%

profile of v3, /device:TPU:1, one launch (start us, length us, event | category | flops | bytes accessed | tf_op | source)
XLA Modules:
  0.0 382.5 jit_solution(15498123248586259649)
XLA Ops:
  0.6 1.7 broadcast_in_dim.40
  2.3 19.4 %all-to-all-start = ((f32[32,256,16]{1,2,0:T(8,128)}), f32[32,256,16]{1,2,0:T(8,128)S(1)}, u32[]{:S(2)}, u32[]{:S(2)}) async-start(f32[32,256,16]{1,2,0:T(8,128)} %broadcast_in_dim.40), calls=%async_computation | async-start | bytes 1048576 | tf_op jit(solution)/shard_map/all_to_all | solution.py:89
  22.9 27.4 %all-to-all-done = f32[32,256,16]{1,2,0:T(8,128)S(1)} async-done(((f32[32,256,16]{1,2,0:T(8,128)}), f32[32,256,16]{1,2,0:T(8,128)S(1)}, u32[]{:S(2)}, u32[]{:S(2)}) %all-to-all-start) | async-done | bytes 524320 | tf_op jit(solution)/shard_map/all_to_all | solution.py:89
  50.3 37.6 %all_to_all.53 = bf16[128,16,256]{2,0,1:T(8,128)(2,1)S(1)} all-to-all(bf16[128,16,256]{2,0,1:T(8,128)(2,1)S(1)} %copy.98), channel_id=1, replica_groups=mesh['island'=32,'fsdp'=16] {'fsdp'}, dimensions={1} | all-to-all | bytes 2097152 | tf_op jit(solution)/shard_map/all_to_all | solution.py:97
  87.9 1.5 convolution_convert_fusion.3
  89.4 3.7 all-to-all-start.2
  93.1 1.5 convolution_convert_fusion.1
  94.6 25.5 %all-to-all-done.2 = bf16[16,128,256]{2,1,0:T(8,128)(2,1)S(1)} async-done(((bf16[16,128,256]{2,1,0:T(8,128)(2,1)}), bf16[16,128,256]{2,1,0:T(8,128)(2,1)S(1)}, u32[]{:S(2)}, u32[]{:S(2)}) %all-to-all-start.2) | async-done | bytes 1048608 | tf_op jit(solution)/shard_map/all_to_all | solution.py:119
  120.1 4.5 %all-to-all-start.4 = ((bf16[16,128,256]{2,1,0:T(8,128)(2,1)}), bf16[16,128,256]{2,1,0:T(8,128)(2,1)S(1)}, u32[]{:S(2)}, u32[]{:S(2)}) async-start(bf16[16,128,256]{2,1,0:T(8,128)(2,1)} %bitcast.36), calls=%async_computation.4 | async-start | bytes 2097152 | tf_op jit(solution)/shard_map/all_to_all | solution.py:119
  124.8 2.5 copy.139
  127.4 3.5 fusion.79
  130.9 1.8 divide_convert_fusion
  133.9 2.2 copy.104
  136.1 2.0 copy.96
  138.1 2.0 copy.105
  140.3 1.4 convert_reduce_fusion.3
  143.1 2.5 copy.103
  145.6 6.0 %all-to-all-done.4 = bf16[16,128,256]{2,1,0:T(8,128)(2,1)S(1)} async-done(((bf16[16,128,256]{2,1,0:T(8,128)(2,1)}), bf16[16,128,256]{2,1,0:T(8,128)(2,1)S(1)}, u32[]{:S(2)}, u32[]{:S(2)}) %all-to-all-start.4) | async-done | bytes 1048608 | tf_op jit(solution)/shard_map/all_to_all | solution.py:119
  153.5 3.1 fusion.28
  157.1 1.9 collective-permute-start
  159.0 1.6 gather_fusion
  160.6 5.1 %collective-permute-start.1 = (bf16[128,256]{0,1:T(8,128)(2,1)S(1)}, bf16[128,256]{0,1:T(8,128)(2,1)S(1)}, u32[]{:S(2)}, u32[]{:S(2)}) collective-permute-start(bf16[128,256]{0,1:T(8,128)(2,1)S(1)} %bitcast.195), channel_id=1, source_target_pairs={{0,3},{1,0},{2,1},{3,2},{4,7},{5,4},{6,5},{7,6},{8,11},{9,8},{10,9... | collective-permute-start | bytes 196616 | tf_op jit(solution)/shard_map/ppermute | solution.py:56
  165.8 1.9 collective-permute-start.2
  167.7 1.5 bitcast_select_fusion.2
  169.2 3.4 collective-permute-done.2
  172.6 1.9 collective-permute-start.3
  174.6 4.7 %collective-permute-start.4 = (bf16[512,256]{0,1:T(8,128)(2,1)S(1)}, bf16[512,256]{0,1:T(8,128)(2,1)S(1)}, u32[]{:S(2)}, u32[]{:S(2)}) collective-permute-start(bf16[512,256]{0,1:T(8,128)(2,1)S(1)} %pad_maximum_fusion), channel_id=1, source_target_pairs={{0,12},{1,13},{2,14},{3,15},{4,0},{5,1},{6,2},{7,3},{8,4},{9,5},{1... | collective-permute-start | bytes 786440 | tf_op jit(solution)/shard_map/ppermute | solution.py:56
  179.3 1.6 collective-permute-done.3
  180.9 1.9 collective-permute-start.5
  182.9 6.3 %collective-permute-done.5 = bf16[512,256]{0,1:T(8,128)(2,1)S(1)} collective-permute-done((bf16[512,256]{0,1:T(8,128)(2,1)S(1)}, bf16[512,256]{0,1:T(8,128)(2,1)S(1)}, u32[]{:S(2)}, u32[]{:S(2)}) %collective-permute-start.5) | collective-permute-done | bytes 262176 | tf_op jit(solution)/shard_map/ppermute | solution.py:57
  191.6 4.3 %all-to-all-start.3 = ((bf16[16,128,256]{1,2,0:T(8,128)(2,1)}), bf16[16,128,256]{1,2,0:T(8,128)(2,1)}, u32[]{:S(2)}, u32[]{:S(2)}) async-start(bf16[16,128,256]{1,2,0:T(8,128)(2,1)} %bitcast.162), calls=%async_computation.3 | async-start | bytes 2097152 | tf_op jit(solution)/shard_map/all_to_all | solution.py:119
  196.0 2.2 copy.115
  199.4 1.4 fusion.10
  200.8 3.1 collective-permute-start.12
  203.8 4.0 %collective-permute-start.13 = (bf16[128,256]{0,1:T(8,128)(2,1)S(1)}, bf16[128,256]{0,1:T(8,128)(2,1)S(1)}, u32[]{:S(2)}, u32[]{:S(2)}) collective-permute-start(bf16[128,256]{0,1:T(8,128)(2,1)S(1)} %bitcast.199), channel_id=1, source_target_pairs={{0,3},{1,0},{2,1},{3,2},{4,7},{5,4},{6,5},{7,6},{8,11},{9,8},{10,9... | collective-permute-start | bytes 196616 | tf_op jit(solution)/shard_map/ppermute | solution.py:56
  207.8 4.8 %collective-permute-done.12 = bf16[128,256]{0,1:T(8,128)(2,1)S(1)} collective-permute-done((bf16[128,256]{0,1:T(8,128)(2,1)S(1)}, bf16[128,256]{0,1:T(8,128)(2,1)S(1)}, u32[]{:S(2)}, u32[]{:S(2)}) %collective-permute-start.12) | collective-permute-done | bytes 65568 | tf_op jit(solution)/shard_map/ppermute | solution.py:55
  212.7 10.0 %collective-permute-start.14 = (bf16[128,256]{0,1:T(8,128)(2,1)S(1)}, bf16[128,256]{0,1:T(8,128)(2,1)S(1)}, u32[]{:S(2)}, u32[]{:S(2)}) collective-permute-start(bf16[128,256]{0,1:T(8,128)(2,1)S(1)} %collective-permute-done.12), channel_id=1, source_target_pairs={{0,1},{1,2},{2,3},{3,0},{4,5},{5,6},{6,7},{7,4},{8,9},{9,10},{10,1... | collective-permute-start | bytes 196616 | tf_op jit(solution)/shard_map/ppermute | solution.py:57
  224.1 3.2 collective-permute-start.15
  227.4 3.4 collective-permute-start.16
  230.8 1.6 collective-permute-done.15
  232.4 2.0 collective-permute-start.17
  234.9 5.8 %collective-permute-done.17 = bf16[512,256]{0,1:T(8,128)(2,1)S(1)} collective-permute-done((bf16[512,256]{0,1:T(8,128)(2,1)S(1)}, bf16[512,256]{0,1:T(8,128)(2,1)S(1)}, u32[]{:S(2)}, u32[]{:S(2)}) %collective-permute-start.17) | collective-permute-done | bytes 262176 | tf_op jit(solution)/shard_map/ppermute | solution.py:57
  243.2 5.6 %all-to-all-start.5 = ((bf16[16,128,256]{1,2,0:T(8,128)(2,1)}), bf16[16,128,256]{1,2,0:T(8,128)(2,1)S(1)}, u32[]{:S(2)}, u32[]{:S(2)}) async-start(bf16[16,128,256]{1,2,0:T(8,128)(2,1)} %bitcast.150), calls=%async_computation.5 | async-start | bytes 2097152 | tf_op jit(solution)/shard_map/all_to_all | solution.py:119
  249.4 1.4 convert_reduce_fusion.2
  253.9 2.6 copy.110
  256.5 17.9 %all-to-all-done.5 = bf16[16,128,256]{1,2,0:T(8,128)(2,1)S(1)} async-done(((bf16[16,128,256]{1,2,0:T(8,128)(2,1)}), bf16[16,128,256]{1,2,0:T(8,128)(2,1)S(1)}, u32[]{:S(2)}, u32[]{:S(2)}) %all-to-all-start.5) | async-done | bytes 1048608 | tf_op jit(solution)/shard_map/all_to_all | solution.py:119
  275.4 1.9 fusion.27
  277.8 1.9 collective-permute-start.18
  279.7 5.2 %collective-permute-start.19 = (bf16[128,256]{0,1:T(8,128)(2,1)S(1)}, bf16[128,256]{0,1:T(8,128)(2,1)S(1)}, u32[]{:S(2)}, u32[]{:S(2)}) collective-permute-start(bf16[128,256]{0,1:T(8,128)(2,1)S(1)} %bitcast.188), channel_id=1, source_target_pairs={{0,3},{1,0},{2,1},{3,2},{4,7},{5,4},{6,5},{7,6},{8,11},{9,8},{10,9... | collective-permute-start | bytes 196616 | tf_op jit(solution)/shard_map/ppermute | solution.py:56
  285.4 1.9 collective-permute-start.6
  287.3 5.2 %collective-permute-start.7 = (bf16[128,256]{0,1:T(8,128)(2,1)S(1)}, bf16[128,256]{0,1:T(8,128)(2,1)S(1)}, u32[]{:S(2)}, u32[]{:S(2)}) collective-permute-start(bf16[128,256]{0,1:T(8,128)(2,1)S(1)} %bitcast.191), channel_id=1, source_target_pairs={{0,3},{1,0},{2,1},{3,2},{4,7},{5,4},{6,5},{7,6},{8,11},{9,8},{10,9... | collective-permute-start | bytes 196616 | tf_op jit(solution)/shard_map/ppermute | solution.py:56
  292.5 1.9 collective-permute-start.20
  294.5 1.9 collective-permute-start.8
  296.5 2.8 collective-permute-done.20
  299.4 1.9 collective-permute-start.21
  301.3 4.6 %collective-permute-start.22 = (bf16[512,256]{0,1:T(8,128)(2,1)S(1)}, bf16[512,256]{0,1:T(8,128)(2,1)S(1)}, u32[]{:S(2)}, u32[]{:S(2)}) collective-permute-start(bf16[512,256]{0,1:T(8,128)(2,1)S(1)} %pad_maximum_fusion.3), channel_id=1, source_target_pairs={{0,12},{1,13},{2,14},{3,15},{4,0},{5,1},{6,2},{7,3},{8,4},{9,5},{1... | collective-permute-start | bytes 786440 | tf_op jit(solution)/shard_map/ppermute | solution.py:56
  305.9 1.9 collective-permute-start.9
  307.8 4.6 %collective-permute-start.10 = (bf16[512,256]{0,1:T(8,128)(2,1)S(1)}, bf16[512,256]{0,1:T(8,128)(2,1)S(1)}, u32[]{:S(2)}, u32[]{:S(2)}) collective-permute-start(bf16[512,256]{0,1:T(8,128)(2,1)S(1)} %pad_maximum_fusion.1), channel_id=1, source_target_pairs={{0,12},{1,13},{2,14},{3,15},{4,0},{5,1},{6,2},{7,3},{8,4},{9,5},{1... | collective-permute-start | bytes 786440 | tf_op jit(solution)/shard_map/ppermute | solution.py:56
  312.5 1.9 collective-permute-start.23
  314.4 1.9 collective-permute-done.9
  316.4 1.9 collective-permute-start.11
  318.4 5.2 %collective-permute-done.23 = bf16[512,256]{0,1:T(8,128)(2,1)S(1)} collective-permute-done((bf16[512,256]{0,1:T(8,128)(2,1)S(1)}, bf16[512,256]{0,1:T(8,128)(2,1)S(1)}, u32[]{:S(2)}, u32[]{:S(2)}) %collective-permute-start.23) | collective-permute-done | bytes 262176 | tf_op jit(solution)/shard_map/ppermute | solution.py:57
  324.1 3.8 collective-permute-done.11
  329.2 52.4 %all_to_all.54 = f32[257,32,16]{0,2,1:T(8,128)S(1)} all-to-all(f32[257,32,16]{0,2,1:T(8,128)S(1)} %bitcast.169), channel_id=1, replica_groups=mesh['island'=32,'fsdp'=16] {'island'}, dimensions={1} | all-to-all | bytes 1052672 | tf_op jit(solution)/shard_map/all_to_all | solution.py:163
  (142 shorter events, 22.3 us)
Async XLA Ops:
  0.6 21.0 %copy-start.13 = (bf16[128,4096]{1,0:T(8,128)(2,1)S(1)}, bf16[128,4096]{1,0:T(8,128)(2,1)}, u32[]{:S(2)}) copy-start(bf16[128,4096]{1,0:T(8,128)(2,1)} %param.12) | copy-start | bytes 3145732
  2.3 48.0 %all-to-all-start = ((f32[32,256,16]{1,2,0:T(8,128)}), f32[32,256,16]{1,2,0:T(8,128)S(1)}, u32[]{:S(2)}, u32[]{:S(2)}) async-start(f32[32,256,16]{1,2,0:T(8,128)} %broadcast_in_dim.40), calls=%async_computation | async-start | bytes 1048576 | tf_op jit(solution)/shard_map/all_to_all | solution.py:89
  50.3 42.8 %copy-start = (f32[32,256,16]{1,2,0:T(8,128)}, f32[32,256,16]{1,2,0:T(8,128)S(1)}, u32[]{:S(2)}) copy-start(f32[32,256,16]{1,2,0:T(8,128)S(1)} %all-to-all-done) | copy-start | bytes 1572868
  89.4 30.7 %all-to-all-start.2 = ((bf16[16,128,256]{2,1,0:T(8,128)(2,1)}), bf16[16,128,256]{2,1,0:T(8,128)(2,1)S(1)}, u32[]{:S(2)}, u32[]{:S(2)}) async-start(bf16[16,128,256]{2,1,0:T(8,128)(2,1)} %bitcast.163), calls=%async_computation.2 | async-start | bytes 2097152 | tf_op jit(solution)/shard_map/all_to_all | solution.py:119
  93.1 31.5 %copy-start.21 = (s32[4]{0:T(128)S(1)}, s32[4]{0:T(128)}, u32[]{:S(2)}) copy-start(s32[4]{0:T(128)} %constant.88.clone) | copy-start | bytes 52
  120.1 7.2 %copy-start.4 = (bf16[16,128,256]{2,1,0:T(8,128)(2,1)}, bf16[16,128,256]{2,1,0:T(8,128)(2,1)S(1)}, u32[]{:S(2)}) copy-start(bf16[16,128,256]{2,1,0:T(8,128)(2,1)S(1)} %all-to-all-done.2) | copy-start | bytes 3145732
  120.1 7.2 %copy-start.17 = (bf16[128,512]{1,0:T(8,128)(2,1)S(1)}, bf16[128,512]{1,0:T(8,128)(2,1)}, u32[]{:S(2)}) copy-start(bf16[128,512]{1,0:T(8,128)(2,1)} %param.14) | copy-start | bytes 393220
  120.1 7.3 %copy-start.20 = (s32[1,128]{1,0:T(1,128)S(1)}, s32[1,128]{1,0:T(1,128)}, u32[]{:S(2)}) copy-start(s32[1,128]{1,0:T(1,128)} %param.16) | copy-start | bytes 1540
  120.1 31.5 %all-to-all-start.4 = ((bf16[16,128,256]{2,1,0:T(8,128)(2,1)}), bf16[16,128,256]{2,1,0:T(8,128)(2,1)S(1)}, u32[]{:S(2)}, u32[]{:S(2)}) async-start(bf16[16,128,256]{2,1,0:T(8,128)(2,1)} %bitcast.36), calls=%async_computation.4 | async-start | bytes 2097152 | tf_op jit(solution)/shard_map/all_to_all | solution.py:119
  153.5 3.2 copy-start.14
  157.1 8.7 %collective-permute-start = (bf16[128,256]{0,1:T(8,128)(2,1)S(1)}, bf16[128,256]{0,1:T(8,128)(2,1)S(1)}, u32[]{:S(2)}, u32[]{:S(2)}) collective-permute-start(bf16[128,256]{0,1:T(8,128)(2,1)S(1)} %bitcast.194), channel_id=1, source_target_pairs={{0,1},{1,2},{2,3},{3,0},{4,5},{5,6},{6,7},{7,4},{8,9},{9,10},{10,1... | collective-permute-start | bytes 196616 | tf_op jit(solution)/shard_map/ppermute | solution.py:55
  160.6 8.6 %collective-permute-start.1 = (bf16[128,256]{0,1:T(8,128)(2,1)S(1)}, bf16[128,256]{0,1:T(8,128)(2,1)S(1)}, u32[]{:S(2)}, u32[]{:S(2)}) collective-permute-start(bf16[128,256]{0,1:T(8,128)(2,1)S(1)} %bitcast.195), channel_id=1, source_target_pairs={{0,3},{1,0},{2,1},{3,2},{4,7},{5,4},{6,5},{7,6},{8,11},{9,8},{10,9... | collective-permute-start | bytes 196616 | tf_op jit(solution)/shard_map/ppermute | solution.py:56
  165.8 6.8 %collective-permute-start.2 = (bf16[128,256]{0,1:T(8,128)(2,1)S(1)}, bf16[128,256]{0,1:T(8,128)(2,1)S(1)}, u32[]{:S(2)}, u32[]{:S(2)}) collective-permute-start(bf16[128,256]{0,1:T(8,128)(2,1)S(1)} %collective-permute-done), channel_id=1, source_target_pairs={{0,1},{1,2},{2,3},{3,0},{4,5},{5,6},{6,7},{7,4},{8,9},{9,10},{10,1... | collective-permute-start | bytes 196616 | tf_op jit(solution)/shard_map/ppermute | solution.py:57
  172.6 8.3 %collective-permute-start.3 = (bf16[512,256]{0,1:T(8,128)(2,1)S(1)}, bf16[512,256]{0,1:T(8,128)(2,1)S(1)}, u32[]{:S(2)}, u32[]{:S(2)}) collective-permute-start(bf16[512,256]{0,1:T(8,128)(2,1)S(1)} %pad_maximum_fusion), channel_id=1, source_target_pairs={{0,4},{1,5},{2,6},{3,7},{4,8},{5,9},{6,10},{7,11},{8,12},{9,13},{1... | collective-permute-start | bytes 786440 | tf_op jit(solution)/shard_map/ppermute | solution.py:55
  174.6 15.2 %copy-start.1 = (f32[32,256,16]{1,2,0:T(8,128)S(1)}, f32[32,256,16]{1,2,0:T(8,128)}, u32[]{:S(2)}) copy-start(f32[32,256,16]{1,2,0:T(8,128)} %copy-done) | copy-start | bytes 1572868
  174.6 15.2 %copy-start.5 = (f32[1,256,512]{1,2,0:T(8,128)S(1)}, f32[1,256,512]{1,2,0:T(8,128)}, u32[]{:S(2)}) copy-start(f32[1,256,512]{1,2,0:T(8,128)} %copy.96) | copy-start | bytes 1572868
  174.6 15.2 %copy-start.8 = (f32[1,256,512]{1,2,0:T(8,128)S(1)}, f32[1,256,512]{1,2,0:T(8,128)}, u32[]{:S(2)}) copy-start(f32[1,256,512]{1,2,0:T(8,128)} %copy.105) | copy-start | bytes 1572868
  174.6 8.3 %collective-permute-start.4 = (bf16[512,256]{0,1:T(8,128)(2,1)S(1)}, bf16[512,256]{0,1:T(8,128)(2,1)S(1)}, u32[]{:S(2)}, u32[]{:S(2)}) collective-permute-start(bf16[512,256]{0,1:T(8,128)(2,1)S(1)} %pad_maximum_fusion), channel_id=1, source_target_pairs={{0,12},{1,13},{2,14},{3,15},{4,0},{5,1},{6,2},{7,3},{8,4},{9,5},{1... | collective-permute-start | bytes 786440 | tf_op jit(solution)/shard_map/ppermute | solution.py:56
  180.9 8.3 %collective-permute-start.5 = (bf16[512,256]{0,1:T(8,128)(2,1)S(1)}, bf16[512,256]{0,1:T(8,128)(2,1)S(1)}, u32[]{:S(2)}, u32[]{:S(2)}) collective-permute-start(bf16[512,256]{0,1:T(8,128)(2,1)S(1)} %collective-permute-done.3), channel_id=1, source_target_pairs={{0,4},{1,5},{2,6},{3,7},{4,8},{5,9},{6,10},{7,11},{8,12},{9,13},{1... | collective-permute-start | bytes 786440 | tf_op jit(solution)/shard_map/ppermute | solution.py:57
  191.6 51.6 %all-to-all-start.3 = ((bf16[16,128,256]{1,2,0:T(8,128)(2,1)}), bf16[16,128,256]{1,2,0:T(8,128)(2,1)}, u32[]{:S(2)}, u32[]{:S(2)}) async-start(bf16[16,128,256]{1,2,0:T(8,128)(2,1)} %bitcast.162), calls=%async_computation.3 | async-start | bytes 2097152 | tf_op jit(solution)/shard_map/all_to_all | solution.py:119
  200.8 11.9 %collective-permute-start.12 = (bf16[128,256]{0,1:T(8,128)(2,1)S(1)}, bf16[128,256]{0,1:T(8,128)(2,1)S(1)}, u32[]{:S(2)}, u32[]{:S(2)}) collective-permute-start(bf16[128,256]{0,1:T(8,128)(2,1)S(1)} %bitcast.198), channel_id=1, source_target_pairs={{0,1},{1,2},{2,3},{3,0},{4,5},{5,6},{6,7},{7,4},{8,9},{9,10},{10,1... | collective-permute-start | bytes 196616 | tf_op jit(solution)/shard_map/ppermute | solution.py:55
  203.8 18.9 %collective-permute-start.13 = (bf16[128,256]{0,1:T(8,128)(2,1)S(1)}, bf16[128,256]{0,1:T(8,128)(2,1)S(1)}, u32[]{:S(2)}, u32[]{:S(2)}) collective-permute-start(bf16[128,256]{0,1:T(8,128)(2,1)S(1)} %bitcast.199), channel_id=1, source_target_pairs={{0,3},{1,0},{2,1},{3,2},{4,7},{5,4},{6,5},{7,6},{8,11},{9,8},{10,9... | collective-permute-start | bytes 196616 | tf_op jit(solution)/shard_map/ppermute | solution.py:56
  212.7 11.4 %collective-permute-start.14 = (bf16[128,256]{0,1:T(8,128)(2,1)S(1)}, bf16[128,256]{0,1:T(8,128)(2,1)S(1)}, u32[]{:S(2)}, u32[]{:S(2)}) collective-permute-start(bf16[128,256]{0,1:T(8,128)(2,1)S(1)} %collective-permute-done.12), channel_id=1, source_target_pairs={{0,1},{1,2},{2,3},{3,0},{4,5},{5,6},{6,7},{7,4},{8,9},{9,10},{10,1... | collective-permute-start | bytes 196616 | tf_op jit(solution)/shard_map/ppermute | solution.py:57
  224.1 8.3 %collective-permute-start.15 = (bf16[512,256]{0,1:T(8,128)(2,1)S(1)}, bf16[512,256]{0,1:T(8,128)(2,1)S(1)}, u32[]{:S(2)}, u32[]{:S(2)}) collective-permute-start(bf16[512,256]{0,1:T(8,128)(2,1)S(1)} %pad_maximum_fusion.2), channel_id=1, source_target_pairs={{0,4},{1,5},{2,6},{3,7},{4,8},{5,9},{6,10},{7,11},{8,12},{9,13},{1... | collective-permute-start | bytes 786440 | tf_op jit(solution)/shard_map/ppermute | solution.py:55
  227.3 13.9 %copy-start.2 = (f32[32,256,16]{1,2,0:T(8,128)S(1)}, f32[32,256,16]{1,2,0:T(8,128)}, u32[]{:S(2)}) copy-start(f32[32,256,16]{1,2,0:T(8,128)} %copy-done) | copy-start | bytes 1572868
  227.3 13.9 %copy-start.6 = (f32[1,256,512]{1,2,0:T(8,128)S(1)}, f32[1,256,512]{1,2,0:T(8,128)}, u32[]{:S(2)}) copy-start(f32[1,256,512]{1,2,0:T(8,128)} %copy.96) | copy-start | bytes 1572868
  227.3 13.9 %copy-start.9 = (f32[1,256,512]{1,2,0:T(8,128)S(1)}, f32[1,256,512]{1,2,0:T(8,128)}, u32[]{:S(2)}) copy-start(f32[1,256,512]{1,2,0:T(8,128)} %copy.105) | copy-start | bytes 1572868
  227.4 7.5 %collective-permute-start.16 = (bf16[512,256]{0,1:T(8,128)(2,1)S(1)}, bf16[512,256]{0,1:T(8,128)(2,1)S(1)}, u32[]{:S(2)}, u32[]{:S(2)}) collective-permute-start(bf16[512,256]{0,1:T(8,128)(2,1)S(1)} %pad_maximum_fusion.2), channel_id=1, source_target_pairs={{0,12},{1,13},{2,14},{3,15},{4,0},{5,1},{6,2},{7,3},{8,4},{9,5},{1... | collective-permute-start | bytes 786440 | tf_op jit(solution)/shard_map/ppermute | solution.py:56
  232.4 8.3 %collective-permute-start.17 = (bf16[512,256]{0,1:T(8,128)(2,1)S(1)}, bf16[512,256]{0,1:T(8,128)(2,1)S(1)}, u32[]{:S(2)}, u32[]{:S(2)}) collective-permute-start(bf16[512,256]{0,1:T(8,128)(2,1)S(1)} %collective-permute-done.15), channel_id=1, source_target_pairs={{0,4},{1,5},{2,6},{3,7},{4,8},{5,9},{6,10},{7,11},{8,12},{9,13},{1... | collective-permute-start | bytes 786440 | tf_op jit(solution)/shard_map/ppermute | solution.py:57
  241.2 0.7 copy-start.11
  243.2 31.1 %all-to-all-start.5 = ((bf16[16,128,256]{1,2,0:T(8,128)(2,1)}), bf16[16,128,256]{1,2,0:T(8,128)(2,1)S(1)}, u32[]{:S(2)}, u32[]{:S(2)}) async-start(bf16[16,128,256]{1,2,0:T(8,128)(2,1)} %bitcast.150), calls=%async_computation.5 | async-start | bytes 2097152 | tf_op jit(solution)/shard_map/all_to_all | solution.py:119
  275.3 2.1 copy-start.16
  277.4 7.6 %copy-start.15 = (bf16[2,8,128,128]{3,1,0,2:T(8,128)(2,1)S(1)}, bf16[2,8,128,128]{3,1,0,2:T(8,128)(2,1)}, u32[]{:S(2)}) copy-start(bf16[2,8,128,128]{3,1,0,2:T(8,128)(2,1)} %copy.104) | copy-start | bytes 1572868
  277.8 14.7 %collective-permute-start.18 = (bf16[128,256]{0,1:T(8,128)(2,1)S(1)}, bf16[128,256]{0,1:T(8,128)(2,1)S(1)}, u32[]{:S(2)}, u32[]{:S(2)}) collective-permute-start(bf16[128,256]{0,1:T(8,128)(2,1)S(1)} %bitcast.187), channel_id=1, source_target_pairs={{0,1},{1,2},{2,3},{3,0},{4,5},{5,6},{6,7},{7,4},{8,9},{9,10},{10,1... | collective-permute-start | bytes 196616 | tf_op jit(solution)/shard_map/ppermute | solution.py:55
  279.7 16.7 %collective-permute-start.19 = (bf16[128,256]{0,1:T(8,128)(2,1)S(1)}, bf16[128,256]{0,1:T(8,128)(2,1)S(1)}, u32[]{:S(2)}, u32[]{:S(2)}) collective-permute-start(bf16[128,256]{0,1:T(8,128)(2,1)S(1)} %bitcast.188), channel_id=1, source_target_pairs={{0,3},{1,0},{2,1},{3,2},{4,7},{5,4},{6,5},{7,6},{8,11},{9,8},{10,9... | collective-permute-start | bytes 196616 | tf_op jit(solution)/shard_map/ppermute | solution.py:56
  285.4 9.1 %collective-permute-start.6 = (bf16[128,256]{0,1:T(8,128)(2,1)S(1)}, bf16[128,256]{0,1:T(8,128)(2,1)S(1)}, u32[]{:S(2)}, u32[]{:S(2)}) collective-permute-start(bf16[128,256]{0,1:T(8,128)(2,1)S(1)} %bitcast.190), channel_id=1, source_target_pairs={{0,1},{1,2},{2,3},{3,0},{4,5},{5,6},{6,7},{7,4},{8,9},{9,10},{10,1... | collective-permute-start | bytes 196616 | tf_op jit(solution)/shard_map/ppermute | solution.py:55
  287.3 9.2 %collective-permute-start.7 = (bf16[128,256]{0,1:T(8,128)(2,1)S(1)}, bf16[128,256]{0,1:T(8,128)(2,1)S(1)}, u32[]{:S(2)}, u32[]{:S(2)}) collective-permute-start(bf16[128,256]{0,1:T(8,128)(2,1)S(1)} %bitcast.191), channel_id=1, source_target_pairs={{0,3},{1,0},{2,1},{3,2},{4,7},{5,4},{6,5},{7,6},{8,11},{9,8},{10,9... | collective-permute-start | bytes 196616 | tf_op jit(solution)/shard_map/ppermute | solution.py:56
  292.5 6.8 %collective-permute-start.20 = (bf16[128,256]{0,1:T(8,128)(2,1)S(1)}, bf16[128,256]{0,1:T(8,128)(2,1)S(1)}, u32[]{:S(2)}, u32[]{:S(2)}) collective-permute-start(bf16[128,256]{0,1:T(8,128)(2,1)S(1)} %collective-permute-done.18), channel_id=1, source_target_pairs={{0,1},{1,2},{2,3},{3,0},{4,5},{5,6},{6,7},{7,4},{8,9},{9,10},{10,1... | collective-permute-start | bytes 196616 | tf_op jit(solution)/shard_map/ppermute | solution.py:57
  294.5 11.4 %collective-permute-start.8 = (bf16[128,256]{0,1:T(8,128)(2,1)S(1)}, bf16[128,256]{0,1:T(8,128)(2,1)S(1)}, u32[]{:S(2)}, u32[]{:S(2)}) collective-permute-start(bf16[128,256]{0,1:T(8,128)(2,1)S(1)} %collective-permute-done.6), channel_id=1, source_target_pairs={{0,1},{1,2},{2,3},{3,0},{4,5},{5,6},{6,7},{7,4},{8,9},{9,10},{10,1... | collective-permute-start | bytes 196616 | tf_op jit(solution)/shard_map/ppermute | solution.py:57
  299.4 13.1 %collective-permute-start.21 = (bf16[512,256]{0,1:T(8,128)(2,1)S(1)}, bf16[512,256]{0,1:T(8,128)(2,1)S(1)}, u32[]{:S(2)}, u32[]{:S(2)}) collective-permute-start(bf16[512,256]{0,1:T(8,128)(2,1)S(1)} %pad_maximum_fusion.3), channel_id=1, source_target_pairs={{0,4},{1,5},{2,6},{3,7},{4,8},{5,9},{6,10},{7,11},{8,12},{9,13},{1... | collective-permute-start | bytes 786440 | tf_op jit(solution)/shard_map/ppermute | solution.py:55
  301.3 17.0 %collective-permute-start.22 = (bf16[512,256]{0,1:T(8,128)(2,1)S(1)}, bf16[512,256]{0,1:T(8,128)(2,1)S(1)}, u32[]{:S(2)}, u32[]{:S(2)}) collective-permute-start(bf16[512,256]{0,1:T(8,128)(2,1)S(1)} %pad_maximum_fusion.3), channel_id=1, source_target_pairs={{0,12},{1,13},{2,14},{3,15},{4,0},{5,1},{6,2},{7,3},{8,4},{9,5},{1... | collective-permute-start | bytes 786440 | tf_op jit(solution)/shard_map/ppermute | solution.py:56
  305.9 10.4 %collective-permute-start.9 = (bf16[512,256]{0,1:T(8,128)(2,1)S(1)}, bf16[512,256]{0,1:T(8,128)(2,1)S(1)}, u32[]{:S(2)}, u32[]{:S(2)}) collective-permute-start(bf16[512,256]{0,1:T(8,128)(2,1)S(1)} %pad_maximum_fusion.1), channel_id=1, source_target_pairs={{0,4},{1,5},{2,6},{3,7},{4,8},{5,9},{6,10},{7,11},{8,12},{9,13},{1... | collective-permute-start | bytes 786440 | tf_op jit(solution)/shard_map/ppermute | solution.py:55
  307.8 10.5 %collective-permute-start.10 = (bf16[512,256]{0,1:T(8,128)(2,1)S(1)}, bf16[512,256]{0,1:T(8,128)(2,1)S(1)}, u32[]{:S(2)}, u32[]{:S(2)}) collective-permute-start(bf16[512,256]{0,1:T(8,128)(2,1)S(1)} %pad_maximum_fusion.1), channel_id=1, source_target_pairs={{0,12},{1,13},{2,14},{3,15},{4,0},{5,1},{6,2},{7,3},{8,4},{9,5},{1... | collective-permute-start | bytes 786440 | tf_op jit(solution)/shard_map/ppermute | solution.py:56
  312.5 11.1 %collective-permute-start.23 = (bf16[512,256]{0,1:T(8,128)(2,1)S(1)}, bf16[512,256]{0,1:T(8,128)(2,1)S(1)}, u32[]{:S(2)}, u32[]{:S(2)}) collective-permute-start(bf16[512,256]{0,1:T(8,128)(2,1)S(1)} %collective-permute-done.21), channel_id=1, source_target_pairs={{0,4},{1,5},{2,6},{3,7},{4,8},{5,9},{6,10},{7,11},{8,12},{9,13},{1... | collective-permute-start | bytes 786440 | tf_op jit(solution)/shard_map/ppermute | solution.py:57
  316.4 11.5 %collective-permute-start.11 = (bf16[512,256]{0,1:T(8,128)(2,1)S(1)}, bf16[512,256]{0,1:T(8,128)(2,1)S(1)}, u32[]{:S(2)}, u32[]{:S(2)}) collective-permute-start(bf16[512,256]{0,1:T(8,128)(2,1)S(1)} %collective-permute-done.9), channel_id=1, source_target_pairs={{0,4},{1,5},{2,6},{3,7},{4,8},{5,9},{6,10},{7,11},{8,12},{9,13},{1... | collective-permute-start | bytes 786440 | tf_op jit(solution)/shard_map/ppermute | solution.py:57
  318.3 9.6 %copy-start.3 = (f32[32,256,16]{1,2,0:T(8,128)S(1)}, f32[32,256,16]{1,2,0:T(8,128)}, u32[]{:S(2)}) copy-start(f32[32,256,16]{1,2,0:T(8,128)} %copy-done) | copy-start | bytes 1572868
  318.4 9.6 %copy-start.7 = (f32[1,256,512]{1,2,0:T(8,128)S(1)}, f32[1,256,512]{1,2,0:T(8,128)}, u32[]{:S(2)}) copy-start(f32[1,256,512]{1,2,0:T(8,128)} %copy.96) | copy-start | bytes 1572868
  318.4 9.6 %copy-start.10 = (f32[1,256,512]{1,2,0:T(8,128)S(1)}, f32[1,256,512]{1,2,0:T(8,128)}, u32[]{:S(2)}) copy-start(f32[1,256,512]{1,2,0:T(8,128)} %copy.105) | copy-start | bytes 1572868
  318.4 9.6 %copy-start.12 = (f32[256,256]{0,1:T(8,128)S(1)}, f32[256,256]{0,1:T(8,128)}, u32[]{:S(2)}) copy-start(f32[256,256]{0,1:T(8,128)} %copy-done.11) | copy-start | bytes 786436
  329.1 52.7 %copy-start.18 = (f32[256,16]{0,1:T(8,128)S(1)}, f32[256,16]{0,1:T(8,128)}, u32[]{:S(2)}) copy-start(f32[256,16]{0,1:T(8,128)} %param.19) | copy-start | bytes 49156
  329.1 52.7 %copy-start.19 = (f32[256,16]{0,1:T(8,128)S(1)}, f32[256,16]{0,1:T(8,128)}, u32[]{:S(2)}) copy-start(f32[256,16]{0,1:T(8,128)} %param.20) | copy-start | bytes 49156

commit v4 on v2

--- a/solution.py
+++ b/solution.py
@@ -83,12 +83,7 @@
     scale_in = 1.0 / math.sqrt(hidden.shape[1])
     attention = attention_weights(query_rows, key_rows, segment_ids[0])
     groups = lax.axis_size("island")
-    copies = jnp.broadcast_to(anchor[None], (groups,) + anchor.shape)
-    master = (
-        lax.all_to_all(copies, "island", split_axis=0, concat_axis=0, tiled=True)
-        .transpose(1, 0, 2)
-        .reshape(anchor.shape[0], groups * anchor.shape[1])
-    )
+    master = lax.all_gather(anchor, "island", axis=1, tiled=True)
     start_point = master
     block = master.shape[0]
     first = first_moment[0]
@@ -141,14 +136,22 @@
     delta = start_point - master
     cols = anchor.shape[1]
     own_count = token_counts[0].astype(jnp.float32)
-    weighted = jnp.concatenate(
-        [own_count * delta, jnp.full((1, delta.shape[1]), own_count, jnp.float32)], axis=0
+    count_high = own_count.astype(jnp.bfloat16)
+    count_low = (own_count - count_high.astype(jnp.float32)).astype(jnp.bfloat16)
+    sent = jnp.concatenate(
+        [
+            delta.astype(jnp.bfloat16),
+            jnp.full((1, delta.shape[1]), count_high, jnp.bfloat16),
+            jnp.full((1, delta.shape[1]), count_low, jnp.bfloat16),
+        ],
+        axis=0,
     )
     received = lax.all_to_all(
-        weighted.reshape(block + 1, groups, cols), "island", split_axis=1, concat_axis=0, tiled=True
-    )
-    summed = jnp.sum(received.reshape(groups, block + 1, cols), axis=0)
-    average = summed[:block] / summed[block:]
+        sent.reshape(block + 2, groups, cols), "island", split_axis=1, concat_axis=0, tiled=True
+    ).reshape(groups, block + 2, cols).astype(jnp.float32)
+    counts = received[:, block] + received[:, block + 1]
+    total = jnp.sum(counts, axis=0)
+    average = jnp.sum(counts[:, None, :] * received[:, :block], axis=0) / total
     new_momentum = outer_beta * outer_momentum + average
     new_anchor = anchor - outer_rate * (average + outer_beta * new_momentum)
     return (new_anchor, new_momentum)

time: 357 us -> 347 us (0.972)
  blocking collectives: 110 us -> 166 us
  waiting for transfers between devices: 131 us -> 76.9 us
  starting transfers between devices: 69.8 us -> 56.6 us
    all_gather x0 -> x1, blocking collectives: none -> 71 us  [on_device(): master = lax.all_gather(anchor, 'island', axis=1, tiled=True)]
    all_to_all x1, waiting for transfers between devices: 27 us -> 0.01 us  [on_device(): lax.all_to_all(hidden, 'fsdp', split_axis=1, concat_axis=0, tiled=True)]
    all_to_all x1 -> x0, waiting for transfers between devices: 26.6 us -> none  [on_device(): lax.all_to_all(copies, 'island', split_axis=0, concat_axis=0, tiled=True)]
    all_to_all x1 -> x0, starting transfers between devices: 19.4 us -> none  [on_device(): lax.all_to_all(copies, 'island', split_axis=0, concat_axis=0, tiled=True)]
    all_to_all x1, blocking collectives: 53.9 us -> 37.4 us  [on_device(): lax.all_to_all(sent.reshape(block + 2, groups, cols), 'island', split_axi...]
    all_to_all x1, starting transfers between devices: 4.56 us -> 12.3 us  [on_device(): lax.all_to_all(partial.reshape(members, rows, width), 'fsdp', split_axis=...]
    unnamed x55 -> x52, local copies, waits for them, and re-layouts: 6.76 us -> 7.53 us
  transfers between devices with their start and end apart: 15 -> 14, of which waited for: 12 -> 9; matrix products, arithmetic and copies ran while one was open for 4% -> 4% of each run, Pallas kernels for 0% -> 0%
where the time goes in v4:
time: 347 us; the launch traced here: 346 us
  blocking collectives  166 us (48%)
  waiting for transfers between devices  76.9 us (22%)
  starting transfers between devices  56.6 us (16%)
  local copies, waits for them, and re-layouts  19.5 us (6%)
  matrix products  13.3 us (4%)
  other arithmetic  12 us (3%)
    all_gather x1, blocking collectives, on_device(): master = lax.all_gather(anchor, 'island', axis=1, tiled=True)  71 us
    all_to_all x1, blocking collectives, on_device(): lax.all_to_all(partial.reshape(members, rows, width), 'fsdp', split_axis=...  57.2 us
    all_to_all x1, waiting for transfers between devices, on_device(): lax.all_to_all(partial.reshape(members, rows, width), 'fsdp', split_axis=...  41.2 us
    all_to_all x1, blocking collectives, on_device(): lax.all_to_all(sent.reshape(block + 2, groups, cols), 'island', split_axi...  37.4 us
    ppermute x4, waiting for transfers between devices, along(): far = lax.ppermute(up, 'fsdp', _shift(cols, rows, dx, dz))  26.3 us
    ppermute x4, starting transfers between devices, along(): down = lax.ppermute(part, 'fsdp', _shift(cols, rows, -dx, -dz))  19.9 us
    all_to_all x1, starting transfers between devices, on_device(): lax.all_to_all(partial.reshape(members, rows, width), 'fsdp', split_axis=...  12.3 us
    all_to_all x1, starting transfers between devices, on_device(): lax.all_to_all(hidden, 'fsdp', split_axis=1, concat_axis=0, tiled=True)  9 us
  transfers between devices with their start and end apart: 14, of which 9 were waited for; matrix products, arithmetic and copies ran while one was open for 4% of the time, Pallas kernels for 0%

profile of v4, /device:TPU:1, one launch (start us, length us, event | category | flops | bytes accessed | tf_op | source)
XLA Modules:
  0.0 345.8 jit_solution(5157409917700478423)
XLA Ops:
  0.6 1.6 copy.70
  2.3 1.3 copy.71
  3.6 9.0 %all-to-all-start = ((bf16[128,16,256]{2,0,1:T(8,128)(2,1)}), bf16[128,16,256]{2,0,1:T(8,128)(2,1)S(1)}, u32[]{:S(2)}, u32[]{:S(2)}) async-start(bf16[128,16,256]{2,0,1:T(8,128)(2,1)} %copy.71), calls=%async_computation | async-start | bytes 2097152 | tf_op jit(solution)/shard_map/all_to_all | solution.py:91
  12.6 71.0 %all_gather.3 = f32[256,512]{0,1:T(8,128)S(1)} all-gather(f32[256,16]{0,1:T(8,128)S(1)} %copy-done.14), channel_id=1, replica_groups=mesh['island'=32,'fsdp'=16] {'island'}, dimensions={1}, use_global_device_ids=true | all-gather | bytes 540672 | tf_op jit(solution)/shard_map/all_gather | solution.py:86
  83.6 2.1 convolution_convert_fusion.1
  85.6 12.3 %all-to-all-start.1 = ((bf16[16,128,512]{2,1,0:T(8,128)(2,1)}), bf16[16,128,512]{2,1,0:T(8,128)(2,1)}, u32[]{:S(2)}, u32[]{:S(2)}) async-start(bf16[16,128,512]{2,1,0:T(8,128)(2,1)} %bitcast.7), calls=%async_computation.1 | async-start | bytes 4194304 | tf_op jit(solution)/shard_map/all_to_all | solution.py:106
  98.3 1.2 copy.101
  99.6 3.5 %fusion.62 = (f32[4,8,128]{2,1,0:T(8,128)S(1)}, f32[4,8,128,128]{2,3,1,0:T(8,128)}) fusion(pred[128,128]{0,1:T(8,128)(4,1)S(1)} %fusion.45, bf16[128,4,8,128]{3,2,1,0:T(8,128)(2,1)} %bitcast.121, bf16[128,4,128,1]{2,1,0,3:T(4,128)(2,1)S(1)} %bitcast.134), kind=kOutput, calls=%fused_computation.104 | convolution fusion | flops 136315008 | bytes 3309568 | tf_op jit(solution)/shard_map/sub | solution.py:33
  103.2 1.8 divide_convert_fusion
  105.0 1.7 copy.77
  106.7 41.2 %all-to-all-done.1 = bf16[16,128,512]{2,1,0:T(8,128)(2,1)} async-done(((bf16[16,128,512]{2,1,0:T(8,128)(2,1)}), bf16[16,128,512]{2,1,0:T(8,128)(2,1)}, u32[]{:S(2)}, u32[]{:S(2)}) %all-to-all-start.1) | async-done | bytes 2097184 | tf_op jit(solution)/shard_map/all_to_all | solution.py:106
  147.9 1.9 convert_reduce_fusion.1
  150.0 1.8 fusion.67
  151.8 2.9 copy.76
  154.7 2.2 fusion.12
  156.9 0.2 copy.102
  157.1 1.0 copy-done.5
  158.1 0.5 fusion.9
  158.6 1.9 collective-permute-start
  160.5 0.7 broadcast_bitcast_fusion
  161.2 5.1 %collective-permute-start.1 = (bf16[128,512]{0,1:T(8,128)(2,1)S(1)}, bf16[128,512]{0,1:T(8,128)(2,1)S(1)}, u32[]{:S(2)}, u32[]{:S(2)}) collective-permute-start(bf16[128,512]{0,1:T(8,128)(2,1)S(1)} %bitcast.127), channel_id=1, source_target_pairs={{0,3},{1,0},{2,1},{3,2},{4,7},{5,4},{6,5},{7,6},{8,11},{9,8},{10,9... | collective-permute-start | bytes 393224 | tf_op jit(solution)/shard_map/ppermute | solution.py:55
  166.3 1.9 collective-permute-start.2
  168.3 1.0 copy.86
  169.3 0.6 pad_clamp_fusion
  169.9 0.7 gather_fusion
  170.6 3.3 collective-permute-done.2
  173.9 1.0 pad_maximum_fusion
  174.9 1.9 collective-permute-start.3
  176.8 1.1 bitcast_select_fusion.2
  178.0 4.6 %collective-permute-start.4 = (bf16[512,512]{0,1:T(8,128)(2,1)S(1)}, bf16[512,512]{0,1:T(8,128)(2,1)S(1)}, u32[]{:S(2)}, u32[]{:S(2)}) collective-permute-start(bf16[512,512]{0,1:T(8,128)(2,1)S(1)} %pad_maximum_fusion), channel_id=1, source_target_pairs={{0,12},{1,13},{2,14},{3,15},{4,0},{5,1},{6,2},{7,3},{8,4},{9,5},{1... | collective-permute-start | bytes 1572872 | tf_op jit(solution)/shard_map/ppermute | solution.py:55
  182.6 5.0 %collective-permute-done.3 = bf16[512,512]{0,1:T(8,128)(2,1)S(1)} collective-permute-done((bf16[512,512]{0,1:T(8,128)(2,1)S(1)}, bf16[512,512]{0,1:T(8,128)(2,1)S(1)}, u32[]{:S(2)}, u32[]{:S(2)}) %collective-permute-start.3) | collective-permute-done | bytes 524320 | tf_op jit(solution)/shard_map/ppermute | solution.py:54
  187.6 1.9 collective-permute-start.5
  189.6 0.9 constant_dynamic-update-slice_fusion.3
  190.7 8.7 %collective-permute-done.5 = bf16[512,512]{0,1:T(8,128)(2,1)S(1)} collective-permute-done((bf16[512,512]{0,1:T(8,128)(2,1)S(1)}, bf16[512,512]{0,1:T(8,128)(2,1)S(1)}, u32[]{:S(2)}, u32[]{:S(2)}) %collective-permute-start.5) | collective-permute-done | bytes 524320 | tf_op jit(solution)/shard_map/ppermute | solution.py:56
  199.5 0.8 fusion.68
  200.2 0.8 copy-done.11
  201.0 1.1 fusion.6
  202.1 0.5 copy.125
  202.7 57.2 %all_to_all.38 = bf16[16,128,512]{1,2,0:T(8,128)(2,1)S(1)} all-to-all(bf16[16,128,512]{1,2,0:T(8,128)(2,1)S(1)} %bitcast.117), channel_id=1, replica_groups=mesh['island'=32,'fsdp'=16] {'fsdp'}, dimensions={0} | all-to-all | bytes 4194304 | tf_op jit(solution)/shard_map/all_to_all | solution.py:106
  259.9 0.3 convert_reduce_fusion
  260.5 1.8 fusion.69
  262.2 1.9 copy.84
  264.2 1.5 fusion.11
  265.7 0.2 copy.103
  266.0 1.0 copy-done.6
  266.9 0.5 fusion.10
  267.4 1.9 collective-permute-start.6
  269.3 5.3 %collective-permute-start.7 = (bf16[128,512]{0,1:T(8,128)(2,1)S(1)}, bf16[128,512]{0,1:T(8,128)(2,1)S(1)}, u32[]{:S(2)}, u32[]{:S(2)}) collective-permute-start(bf16[128,512]{0,1:T(8,128)(2,1)S(1)} %bitcast.131), channel_id=1, source_target_pairs={{0,3},{1,0},{2,1},{3,2},{4,7},{5,4},{6,5},{7,6},{8,11},{9,8},{10,9... | collective-permute-start | bytes 393224 | tf_op jit(solution)/shard_map/ppermute | solution.py:55
  274.7 0.4 collective-permute-done.6
  275.1 1.9 collective-permute-start.8
  277.0 5.6 %collective-permute-done.8 = bf16[128,512]{0,1:T(8,128)(2,1)S(1)} collective-permute-done((bf16[128,512]{0,1:T(8,128)(2,1)S(1)}, bf16[128,512]{0,1:T(8,128)(2,1)S(1)}, u32[]{:S(2)}, u32[]{:S(2)}) %collective-permute-start.8) | collective-permute-done | bytes 131104 | tf_op jit(solution)/shard_map/ppermute | solution.py:56
  282.7 1.9 collective-permute-start.9
  285.4 4.8 %collective-permute-start.10 = (bf16[512,512]{0,1:T(8,128)(2,1)S(1)}, bf16[512,512]{0,1:T(8,128)(2,1)S(1)}, u32[]{:S(2)}, u32[]{:S(2)}) collective-permute-start(bf16[512,512]{0,1:T(8,128)(2,1)S(1)} %pad_maximum_fusion.1), channel_id=1, source_target_pairs={{0,12},{1,13},{2,14},{3,15},{4,0},{5,1},{6,2},{7,3},{8,4},{9,5},{1... | collective-permute-start | bytes 1572872 | tf_op jit(solution)/shard_map/ppermute | solution.py:55
  290.3 3.5 %collective-permute-done.9 = bf16[512,512]{0,1:T(8,128)(2,1)S(1)} collective-permute-done((bf16[512,512]{0,1:T(8,128)(2,1)S(1)}, bf16[512,512]{0,1:T(8,128)(2,1)S(1)}, u32[]{:S(2)}, u32[]{:S(2)}) %collective-permute-start.9) | collective-permute-done | bytes 524320 | tf_op jit(solution)/shard_map/ppermute | solution.py:54
  293.8 1.9 collective-permute-start.11
  295.9 0.4 collective-permute-done.10
  296.4 8.7 %collective-permute-done.11 = bf16[512,512]{0,1:T(8,128)(2,1)S(1)} collective-permute-done((bf16[512,512]{0,1:T(8,128)(2,1)S(1)}, bf16[512,512]{0,1:T(8,128)(2,1)S(1)}, u32[]{:S(2)}, u32[]{:S(2)}) %collective-permute-start.11) | collective-permute-done | bytes 524320 | tf_op jit(solution)/shard_map/ppermute | solution.py:56
  305.3 1.4 fusion.28
  306.8 0.2 copy.87
  307.0 37.4 %all_to_all.39 = bf16[258,32,16]{0,2,1:T(8,128)(2,1)S(1)} all-to-all(bf16[258,32,16]{0,2,1:T(8,128)(2,1)S(1)} %bitcast.119), channel_id=1, replica_groups=mesh['island'=32,'fsdp'=16] {'island'}, dimensions={1} | all-to-all | bytes 528384 | tf_op jit(solution)/shard_map/all_to_all | solution.py:149
  344.5 0.2 fusion.61
  344.7 0.2 copy.99
  345.0 0.2 fusion.27
  345.1 0.7 multiply_subtract_fusion.1
  (69 shorter events, 1.8 us)
Async XLA Ops:
  2.3 10.3 %copy-start.14 = (f32[256,16]{0,1:T(8,128)S(1)}, f32[256,16]{0,1:T(8,128)}, u32[]{:S(2)}) copy-start(f32[256,16]{0,1:T(8,128)} %param.19) | copy-start | bytes 49156
  3.6 80.0 %all-to-all-start = ((bf16[128,16,256]{2,0,1:T(8,128)(2,1)}), bf16[128,16,256]{2,0,1:T(8,128)(2,1)S(1)}, u32[]{:S(2)}, u32[]{:S(2)}) async-start(bf16[128,16,256]{2,0,1:T(8,128)(2,1)} %copy.71), calls=%async_computation | async-start | bytes 2097152 | tf_op jit(solution)/shard_map/all_to_all | solution.py:91
  85.6 12.4 %copy-start.17 = (s32[4]{0:T(128)S(1)}, s32[4]{0:T(128)}, u32[]{:S(2)}) copy-start(s32[4]{0:T(128)} %constant.86.clone) | copy-start | bytes 52
  85.6 12.7 %copy-start.4 = (bf16[128,4096]{1,0:T(8,128)(2,1)S(1)}, bf16[128,4096]{1,0:T(8,128)(2,1)}, u32[]{:S(2)}) copy-start(bf16[128,4096]{1,0:T(8,128)(2,1)} %param.13) | copy-start | bytes 3145732
  85.6 62.3 %all-to-all-start.1 = ((bf16[16,128,512]{2,1,0:T(8,128)(2,1)}), bf16[16,128,512]{2,1,0:T(8,128)(2,1)}, u32[]{:S(2)}, u32[]{:S(2)}) async-start(bf16[16,128,512]{2,1,0:T(8,128)(2,1)} %bitcast.7), calls=%async_computation.1 | async-start | bytes 4194304 | tf_op jit(solution)/shard_map/all_to_all | solution.py:106
  98.0 1.5 copy-start.13
  98.0 1.6 copy-start.16
  156.9 1.2 copy-start.5
  158.6 7.7 %collective-permute-start = (bf16[128,512]{0,1:T(8,128)(2,1)S(1)}, bf16[128,512]{0,1:T(8,128)(2,1)S(1)}, u32[]{:S(2)}, u32[]{:S(2)}) collective-permute-start(bf16[128,512]{0,1:T(8,128)(2,1)S(1)} %bitcast.126), channel_id=1, source_target_pairs={{0,1},{1,2},{2,3},{3,0},{4,5},{5,6},{6,7},{7,4},{8,9},{9,10},{10,1... | collective-permute-start | bytes 393224 | tf_op jit(solution)/shard_map/ppermute | solution.py:54
  161.2 9.4 %collective-permute-start.1 = (bf16[128,512]{0,1:T(8,128)(2,1)S(1)}, bf16[128,512]{0,1:T(8,128)(2,1)S(1)}, u32[]{:S(2)}, u32[]{:S(2)}) collective-permute-start(bf16[128,512]{0,1:T(8,128)(2,1)S(1)} %bitcast.127), channel_id=1, source_target_pairs={{0,3},{1,0},{2,1},{3,2},{4,7},{5,4},{6,5},{7,6},{8,11},{9,8},{10,9... | collective-permute-start | bytes 393224 | tf_op jit(solution)/shard_map/ppermute | solution.py:55
  166.3 7.6 %collective-permute-start.2 = (bf16[128,512]{0,1:T(8,128)(2,1)S(1)}, bf16[128,512]{0,1:T(8,128)(2,1)}, u32[]{:S(2)}, u32[]{:S(2)}) collective-permute-start(bf16[128,512]{0,1:T(8,128)(2,1)S(1)} %collective-permute-done), channel_id=1, source_target_pairs={{0,1},{1,2},{2,3},{3,0},{4,5},{5,6},{6,7},{7,4},{8,9},{9,10},{10,1... | collective-permute-start | bytes 393224 | tf_op jit(solution)/shard_map/ppermute | solution.py:56
  174.9 12.7 %collective-permute-start.3 = (bf16[512,512]{0,1:T(8,128)(2,1)S(1)}, bf16[512,512]{0,1:T(8,128)(2,1)S(1)}, u32[]{:S(2)}, u32[]{:S(2)}) collective-permute-start(bf16[512,512]{0,1:T(8,128)(2,1)S(1)} %pad_maximum_fusion), channel_id=1, source_target_pairs={{0,4},{1,5},{2,6},{3,7},{4,8},{5,9},{6,10},{7,11},{8,12},{9,13},{1... | collective-permute-start | bytes 1572872 | tf_op jit(solution)/shard_map/ppermute | solution.py:54
  178.0 21.5 %copy-start.2 = (bf16[2048,256]{1,0:T(8,128)(2,1)}, bf16[2048,256]{1,0:T(8,128)(2,1)S(1)}, u32[]{:S(2)}) copy-start(bf16[2048,256]{1,0:T(8,128)(2,1)S(1)} %bitcast_select_fusion.2) | copy-start | bytes 3145732
  178.0 12.6 %collective-permute-start.4 = (bf16[512,512]{0,1:T(8,128)(2,1)S(1)}, bf16[512,512]{0,1:T(8,128)(2,1)S(1)}, u32[]{:S(2)}, u32[]{:S(2)}) collective-permute-start(bf16[512,512]{0,1:T(8,128)(2,1)S(1)} %pad_maximum_fusion), channel_id=1, source_target_pairs={{0,12},{1,13},{2,14},{3,15},{4,0},{5,1},{6,2},{7,3},{8,4},{9,5},{1... | collective-permute-start | bytes 1572872 | tf_op jit(solution)/shard_map/ppermute | solution.py:55
  187.6 11.8 %collective-permute-start.5 = (bf16[512,512]{0,1:T(8,128)(2,1)S(1)}, bf16[512,512]{0,1:T(8,128)(2,1)S(1)}, u32[]{:S(2)}, u32[]{:S(2)}) collective-permute-start(bf16[512,512]{0,1:T(8,128)(2,1)S(1)} %collective-permute-done.3), channel_id=1, source_target_pairs={{0,4},{1,5},{2,6},{3,7},{4,8},{5,9},{6,10},{7,11},{8,12},{9,13},{1... | collective-permute-start | bytes 1572872 | tf_op jit(solution)/shard_map/ppermute | solution.py:56
  199.4 1.6 copy-start
  199.5 1.6 copy-start.7
  199.5 1.6 copy-start.9
  200.2 0.8 copy-start.11
  265.7 1.2 copy-start.6
  267.4 7.7 %collective-permute-start.6 = (bf16[128,512]{0,1:T(8,128)(2,1)S(1)}, bf16[128,512]{0,1:T(8,128)(2,1)S(1)}, u32[]{:S(2)}, u32[]{:S(2)}) collective-permute-start(bf16[128,512]{0,1:T(8,128)(2,1)S(1)} %bitcast.130), channel_id=1, source_target_pairs={{0,1},{1,2},{2,3},{3,0},{4,5},{5,6},{6,7},{7,4},{8,9},{9,10},{10,1... | collective-permute-start | bytes 393224 | tf_op jit(solution)/shard_map/ppermute | solution.py:54
  269.3 7.7 %collective-permute-start.7 = (bf16[128,512]{0,1:T(8,128)(2,1)S(1)}, bf16[128,512]{0,1:T(8,128)(2,1)S(1)}, u32[]{:S(2)}, u32[]{:S(2)}) collective-permute-start(bf16[128,512]{0,1:T(8,128)(2,1)S(1)} %bitcast.131), channel_id=1, source_target_pairs={{0,3},{1,0},{2,1},{3,2},{4,7},{5,4},{6,5},{7,6},{8,11},{9,8},{10,9... | collective-permute-start | bytes 393224 | tf_op jit(solution)/shard_map/ppermute | solution.py:55
  275.1 7.5 %collective-permute-start.8 = (bf16[128,512]{0,1:T(8,128)(2,1)S(1)}, bf16[128,512]{0,1:T(8,128)(2,1)S(1)}, u32[]{:S(2)}, u32[]{:S(2)}) collective-permute-start(bf16[128,512]{0,1:T(8,128)(2,1)S(1)} %collective-permute-done.6), channel_id=1, source_target_pairs={{0,1},{1,2},{2,3},{3,0},{4,5},{5,6},{6,7},{7,4},{8,9},{9,10},{10,1... | collective-permute-start | bytes 393224 | tf_op jit(solution)/shard_map/ppermute | solution.py:56
  282.7 11.1 %collective-permute-start.9 = (bf16[512,512]{0,1:T(8,128)(2,1)S(1)}, bf16[512,512]{0,1:T(8,128)(2,1)S(1)}, u32[]{:S(2)}, u32[]{:S(2)}) collective-permute-start(bf16[512,512]{0,1:T(8,128)(2,1)S(1)} %pad_maximum_fusion.1), channel_id=1, source_target_pairs={{0,4},{1,5},{2,6},{3,7},{4,8},{5,9},{6,10},{7,11},{8,12},{9,13},{1... | collective-permute-start | bytes 1572872 | tf_op jit(solution)/shard_map/ppermute | solution.py:54
  285.4 19.9 %copy-start.1 = (f32[256,512]{1,0:T(8,128)S(1)}, f32[256,512]{1,0:T(8,128)}, u32[]{:S(2)}) copy-start(f32[256,512]{1,0:T(8,128)} %copy.86) | copy-start | bytes 1572868
  285.4 19.9 %copy-start.3 = (bf16[2048,256]{1,0:T(8,128)(2,1)S(1)}, bf16[2048,256]{1,0:T(8,128)(2,1)}, u32[]{:S(2)}) copy-start(bf16[2048,256]{1,0:T(8,128)(2,1)} %copy-done.2) | copy-start | bytes 3145732
  285.4 19.9 %copy-start.8 = (f32[1,256,512]{2,1,0:T(8,128)S(1)}, f32[1,256,512]{2,1,0:T(8,128)}, u32[]{:S(2)}) copy-start(f32[1,256,512]{2,1,0:T(8,128)} %param.17) | copy-start | bytes 1572868
  285.4 19.9 %copy-start.10 = (f32[1,256,512]{2,1,0:T(8,128)S(1)}, f32[1,256,512]{2,1,0:T(8,128)}, u32[]{:S(2)}) copy-start(f32[1,256,512]{2,1,0:T(8,128)} %param.18) | copy-start | bytes 1572868
  285.4 19.9 %copy-start.12 = (f32[256,512]{1,0:T(8,128)S(1)}, f32[256,512]{1,0:T(8,128)}, u32[]{:S(2)}) copy-start(f32[256,512]{1,0:T(8,128)} %copy-done.11) | copy-start | bytes 1572868
  285.4 10.9 %collective-permute-start.10 = (bf16[512,512]{0,1:T(8,128)(2,1)S(1)}, bf16[512,512]{0,1:T(8,128)(2,1)S(1)}, u32[]{:S(2)}, u32[]{:S(2)}) collective-permute-start(bf16[512,512]{0,1:T(8,128)(2,1)S(1)} %pad_maximum_fusion.1), channel_id=1, source_target_pairs={{0,12},{1,13},{2,14},{3,15},{4,0},{5,1},{6,2},{7,3},{8,4},{9,5},{1... | collective-permute-start | bytes 1572872 | tf_op jit(solution)/shard_map/ppermute | solution.py:55
  293.8 11.3 %collective-permute-start.11 = (bf16[512,512]{0,1:T(8,128)(2,1)S(1)}, bf16[512,512]{0,1:T(8,128)(2,1)S(1)}, u32[]{:S(2)}, u32[]{:S(2)}) collective-permute-start(bf16[512,512]{0,1:T(8,128)(2,1)S(1)} %collective-permute-done.9), channel_id=1, source_target_pairs={{0,4},{1,5},{2,6},{3,7},{4,8},{5,9},{6,10},{7,11},{8,12},{9,13},{1... | collective-permute-start | bytes 1572872 | tf_op jit(solution)/shard_map/ppermute | solution.py:56
  306.8 38.3 %copy-start.15 = (f32[256,16]{0,1:T(8,128)S(1)}, f32[256,16]{0,1:T(8,128)}, u32[]{:S(2)}) copy-start(f32[256,16]{0,1:T(8,128)} %param.20) | copy-start | bytes 49156

commit v5 on v4

--- a/solution.py
+++ b/solution.py
@@ -62,6 +62,27 @@
 
     row = jnp.concatenate(along(piece, cols, 0, 1), axis=0)
     return jnp.concatenate(along(row, rows, 1, 0), axis=0)
+
+
+def ring_exchange(hidden, rows, cols, block):
+    me = lax.axis_index("fsdp")
+    me_x, me_z = me // cols, me % cols
+    tokens = hidden.shape[0]
+    mine = hidden.reshape(tokens, rows, cols, block).transpose(1, 2, 0, 3)
+    stage = []
+    for dz in [0, 1, -1, 2]:
+        part = lax.dynamic_index_in_dim(mine, (me_z + dz) % cols, axis=1, keepdims=False)
+        if dz:
+            part = lax.ppermute(part, "fsdp", _shift(cols, rows, 0, dz))
+        stage.append(part)
+    gathered = jnp.stack(stage, axis=1)
+    out = []
+    for dx in [0, 1, -1, 2]:
+        part = lax.dynamic_index_in_dim(gathered, (me_x + dx) % rows, axis=0, keepdims=False)
+        if dx:
+            part = lax.ppermute(part, "fsdp", _shift(cols, rows, dx, 0))
+        out.append(part)
+    return jnp.stack(out, axis=0).reshape(rows * cols * tokens, block)
 
 
 def on_device(
@@ -83,12 +104,16 @@
     scale_in = 1.0 / math.sqrt(hidden.shape[1])
     attention = attention_weights(query_rows, key_rows, segment_ids[0])
     groups = lax.axis_size("island")
-    master = lax.all_gather(anchor, "island", axis=1, tiled=True)
+    copies = jnp.broadcast_to(anchor[None], (groups,) + anchor.shape)
+    master = (
+        lax.all_to_all(copies, "island", split_axis=0, concat_axis=0, tiled=True)
+        .transpose(1, 0, 2)
+        .reshape(anchor.shape[0], groups * anchor.shape[1])
+    )
     start_point = master
     block = master.shape[0]
     first = first_moment[0]
     second = second_moment[0]
-    feature_rows = lax.all_to_all(hidden, "fsdp", split_axis=1, concat_axis=0, tiled=True)
     grid_cols = 4 if members % 4 == 0 else 1
     grid_rows = members // grid_cols
     me = lax.axis_index("fsdp")
@@ -96,9 +121,16 @@
     take_x = (me_x + jnp.array(ring_offsets(grid_rows))) % grid_rows
     take_z = (me_z + jnp.array(ring_offsets(grid_cols))) % grid_cols
     order = (take_x[:, None] * grid_cols + take_z[None, :]).reshape(-1)
-    ring_rows = jnp.take(
-        feature_rows.reshape(members, rows, block), order, axis=0
-    ).reshape(group_rows, block)
+    if grid_rows == 4 and grid_cols == 4:
+        ring_rows = ring_exchange(hidden, grid_rows, grid_cols, block)
+        feature_rows = jnp.take(
+            ring_rows.reshape(members, rows, block), jnp.argsort(order), axis=0
+        ).reshape(group_rows, block)
+    else:
+        feature_rows = lax.all_to_all(hidden, "fsdp", split_axis=1, concat_axis=0, tiled=True)
+        ring_rows = jnp.take(
+            feature_rows.reshape(members, rows, block), order, axis=0
+        ).reshape(group_rows, block)
     for inner_step in range(2):
         partial = jnp.dot(
             feature_rows, master.astype(jnp.bfloat16), preferred_element_type=jnp.float32

time: 347 us -> 350 us (level)
  blocking collectives: 166 us -> 102 us
  waiting for transfers between devices: 76.9 us -> 116 us
  starting transfers between devices: 56.6 us -> 82.6 us
    all_gather x1 -> x0, blocking collectives: 71 us -> none  [on_device(): master = lax.all_gather(anchor, 'island', axis=1, tiled=True)]
    ppermute x0 -> x6, waiting for transfers between devices: none -> 38 us  [the longest x3 31.3 us: ring_exchange(): part = lax.ppermute(part, 'fsdp', _shift(cols, rows, 0, dz))]
    ppermute x0 -> x6, starting transfers between devices: none -> 18.5 us  [the longest x3 9.93 us: ring_exchange(): part = lax.ppermute(part, 'fsdp', _shift(cols, rows, dx, 0))]
    all_to_all x1, starting transfers between devices: 9 us -> 19.4 us  [on_device(): lax.all_to_all(copies, 'island', split_axis=0, concat_axis=0, tiled=True)]
    all_to_all x1, blocking collectives: 37.4 us -> 45.4 us  [on_device(): lax.all_to_all(sent.reshape(block + 2, groups, cols), 'island', split_axi...]
    unnamed x52 -> x64, local copies, waits for them, and re-layouts: 7.53 us -> 7.06 us
  transfers between devices with their start and end apart: 14 -> 20, of which waited for: 9 -> 15; matrix products, arithmetic and copies ran while one was open for 4% -> 5% of each run, Pallas kernels for 0% -> 0%
where the time goes in v5:
time: 350 us; the launch traced here: 349 us
  waiting for transfers between devices  116 us (33%)
  blocking collectives  102 us (29%)
  starting transfers between devices  82.6 us (24%)
  local copies, waits for them, and re-layouts  20.7 us (6%)
  other arithmetic  13.5 us (4%)
  matrix products  12.1 us (3%)
    all_to_all x1, blocking collectives, on_device(): lax.all_to_all(partial.reshape(members, rows, width), 'fsdp', split_axis=...  56.3 us
    all_to_all x1, blocking collectives, on_device(): lax.all_to_all(sent.reshape(block + 2, groups, cols), 'island', split_axi...  45.4 us
    all_to_all x1, waiting for transfers between devices, on_device(): lax.all_to_all(partial.reshape(members, rows, width), 'fsdp', split_axis=...  43.1 us
    ppermute x3, waiting for transfers between devices, ring_exchange(): part = lax.ppermute(part, 'fsdp', _shift(cols, rows, 0, dz))  31.3 us
    ppermute x4, waiting for transfers between devices, along(): far = lax.ppermute(up, 'fsdp', _shift(cols, rows, dx, dz))  25.2 us
    ppermute x4, starting transfers between devices, along(): down = lax.ppermute(part, 'fsdp', _shift(cols, rows, -dx, -dz))  19.8 us
    all_to_all x1, starting transfers between devices, on_device(): lax.all_to_all(copies, 'island', split_axis=0, concat_axis=0, tiled=True)  19.4 us
    ppermute x3, starting transfers between devices, ring_exchange(): part = lax.ppermute(part, 'fsdp', _shift(cols, rows, dx, 0))  9.93 us
  transfers between devices with their start and end apart: 20, of which 15 were waited for; matrix products, arithmetic and copies ran while one was open for 5% of the time, Pallas kernels for 0%

profile of v5, /device:TPU:1, one launch (start us, length us, event | category | flops | bytes accessed | tf_op | source)
XLA Modules:
  0.0 349.1 jit_solution(9564387474928417520)
XLA Ops:
  0.6 1.7 broadcast_in_dim.53
  2.3 19.4 %all-to-all-start = ((f32[32,256,16]{1,2,0:T(8,128)}), f32[32,256,16]{1,2,0:T(8,128)S(1)}, u32[]{:S(2)}, u32[]{:S(2)}) async-start(f32[32,256,16]{1,2,0:T(8,128)} %broadcast_in_dim.53), calls=%async_computation | async-start | bytes 1048576 | tf_op jit(solution)/shard_map/all_to_all | solution.py:109
  21.8 0.7 copy.74
  22.6 3.1 collective-permute-start.2
  25.7 3.5 %collective-permute-start.1 = (bf16[4,128,256]{1,2,0:T(8,128)(2,1)S(1)}, bf16[4,128,256]{1,2,0:T(8,128)(2,1)S(1)}, u32[]{:S(2)}, u32[]{:S(2)}) collective-permute-start(bf16[4,128,256]{1,2,0:T(8,128)(2,1)S(1)} %get-tuple-element.13), channel_id=1, source_target_pairs={{0,3},{1,0},{2,1},{3,2},{4,7},{5,4},{6,5},{7,6},{8,11},{9,8},{10,9... | collective-permute-start | bytes 786440 | tf_op jit(solution)/shard_map/ppermute | solution.py:76
  29.2 1.9 collective-permute-start
  31.4 1.2 sort.17
  32.6 25.1 %collective-permute-done.2 = bf16[4,128,256]{1,2,0:T(8,128)(2,1)S(1)} collective-permute-done((bf16[4,128,256]{1,2,0:T(8,128)(2,1)S(1)}, bf16[4,128,256]{1,2,0:T(8,128)(2,1)S(1)}, u32[]{:S(2)}, u32[]{:S(2)}) %collective-permute-start.2) | collective-permute-done | bytes 262176 | tf_op jit(solution)/shard_map/ppermute | solution.py:76
  57.7 6.2 %collective-permute-done = bf16[4,128,256]{1,2,0:T(8,128)(2,1)S(1)} collective-permute-done((bf16[4,128,256]{1,2,0:T(8,128)(2,1)S(1)}, bf16[4,128,256]{1,2,0:T(8,128)(2,1)S(1)}, u32[]{:S(2)}, u32[]{:S(2)}) %collective-permute-start) | collective-permute-done | bytes 262176 | tf_op jit(solution)/shard_map/ppermute | solution.py:76
  64.3 4.7 %collective-permute-start.5 = (bf16[4,128,256]{2,1,0:T(8,128)(2,1)S(1)}, bf16[4,128,256]{2,1,0:T(8,128)(2,1)S(1)}, u32[]{:S(2)}, u32[]{:S(2)}) collective-permute-start(bf16[4,128,256]{2,1,0:T(8,128)(2,1)S(1)} %bitcast.164), channel_id=1, source_target_pairs={{0,8},{1,9},{2,10},{3,11},{4,12},{5,13},{6,14},{7,15},{8,0},{9,1},... | collective-permute-start | bytes 786440 | tf_op jit(solution)/shard_map/ppermute | solution.py:83
  69.1 2.8 collective-permute-start.4
  72.1 2.5 collective-permute-start.3
  75.0 5.6 %collective-permute-done.4 = bf16[4,128,256]{2,1,0:T(8,128)(2,1)S(1)} collective-permute-done((bf16[4,128,256]{2,1,0:T(8,128)(2,1)S(1)}, bf16[4,128,256]{2,1,0:T(8,128)(2,1)S(1)}, u32[]{:S(2)}, u32[]{:S(2)}) %collective-permute-start.4) | collective-permute-done | bytes 262176 | tf_op jit(solution)/shard_map/ppermute | solution.py:83
  80.8 0.9 collective-permute-done.3
  82.0 0.5 copy.85
  82.6 0.6 gather_fusion
  83.2 1.2 broadcast_select_fusion
  84.4 3.5 convolution_convert_fusion.1
  87.9 9.6 %all-to-all-start.1 = ((bf16[16,128,512]{2,1,0:T(8,128)(2,1)}), bf16[16,128,512]{2,1,0:T(8,128)(2,1)}, u32[]{:S(2)}, u32[]{:S(2)}) async-start(bf16[16,128,512]{2,1,0:T(8,128)(2,1)} %bitcast.139), calls=%async_computation.1 | async-start | bytes 4194304 | tf_op jit(solution)/shard_map/all_to_all | solution.py:138
  97.7 0.6 copy-done.19
  98.5 2.3 fusion.59
  100.8 1.8 divide_convert_fusion
  102.6 1.7 copy.92
  104.3 43.1 %all-to-all-done.1 = bf16[16,128,512]{2,1,0:T(8,128)(2,1)} async-done(((bf16[16,128,512]{2,1,0:T(8,128)(2,1)}), bf16[16,128,512]{2,1,0:T(8,128)(2,1)}, u32[]{:S(2)}, u32[]{:S(2)}) %all-to-all-start.1) | async-done | bytes 2097184 | tf_op jit(solution)/shard_map/all_to_all | solution.py:138
  147.4 1.9 convert_reduce_fusion.1
  149.5 1.8 fusion.64
  151.2 3.0 copy.91
  154.2 1.9 fusion.11
  156.4 1.0 copy-done.10
  157.8 1.9 collective-permute-start.6
  159.8 5.2 %collective-permute-start.7 = (bf16[128,512]{0,1:T(8,128)(2,1)S(1)}, bf16[128,512]{0,1:T(8,128)(2,1)S(1)}, u32[]{:S(2)}, u32[]{:S(2)}) collective-permute-start(bf16[128,512]{0,1:T(8,128)(2,1)S(1)} %bitcast.161), channel_id=1, source_target_pairs={{0,3},{1,0},{2,1},{3,2},{4,7},{5,4},{6,5},{7,6},{8,11},{9,8},{10,9... | collective-permute-start | bytes 393224 | tf_op jit(solution)/shard_map/ppermute | solution.py:55
  164.9 0.6 collective-permute-done.6
  165.6 1.9 collective-permute-start.8
  167.5 2.0 collective-permute-done.7
  169.6 3.5 collective-permute-done.8
  173.1 0.9 pad_maximum_fusion.2
  173.9 1.9 collective-permute-start.9
  175.8 0.5 bitcast_select_fusion.2
  176.4 2.0 copy.99
  178.4 4.7 %collective-permute-start.10 = (bf16[512,512]{0,1:T(8,128)(2,1)}, bf16[512,512]{0,1:T(8,128)(2,1)S(1)}, u32[]{:S(2)}, u32[]{:S(2)}) collective-permute-start(bf16[512,512]{0,1:T(8,128)(2,1)} %pad_maximum_fusion.2), channel_id=1, source_target_pairs={{0,12},{1,13},{2,14},{3,15},{4,0},{5,1},{6,2},{7,3},{8,4},{9,5},{1... | collective-permute-start | bytes 1572872 | tf_op jit(solution)/shard_map/ppermute | solution.py:55
  183.2 2.8 collective-permute-done.9
  186.0 1.9 collective-permute-start.11
  188.0 0.9 constant_dynamic-update-slice_fusion.3
  188.9 1.1 constant_dynamic-update-slice_fusion.2
  190.1 7.2 %collective-permute-done.11 = bf16[512,512]{0,1:T(8,128)(2,1)S(1)} collective-permute-done((bf16[512,512]{0,1:T(8,128)(2,1)}, bf16[512,512]{0,1:T(8,128)(2,1)S(1)}, u32[]{:S(2)}, u32[]{:S(2)}) %collective-permute-start.11) | collective-permute-done | bytes 524320 | tf_op jit(solution)/shard_map/ppermute | solution.py:56
  197.4 0.8 fusion.65
  198.8 1.0 convolution_convert_fusion
  199.8 56.3 %all_to_all.24 = bf16[16,128,512]{2,1,0:T(8,128)(2,1)S(1)} all-to-all(bf16[16,128,512]{2,1,0:T(8,128)(2,1)S(1)} %bitcast.138), channel_id=1, replica_groups=mesh['island'=32,'fsdp'=16] {'fsdp'}, dimensions={0} | all-to-all | bytes 4194304 | tf_op jit(solution)/shard_map/all_to_all | solution.py:138
  257.0 1.8 copy.97
  258.9 1.9 fusion.10
  261.0 1.0 copy-done.11
  262.5 1.9 collective-permute-start.12
  264.4 5.2 %collective-permute-start.13 = (bf16[128,512]{0,1:T(8,128)(2,1)S(1)}, bf16[128,512]{0,1:T(8,128)(2,1)S(1)}, u32[]{:S(2)}, u32[]{:S(2)}) collective-permute-start(bf16[128,512]{0,1:T(8,128)(2,1)S(1)} %bitcast.157), channel_id=1, source_target_pairs={{0,3},{1,0},{2,1},{3,2},{4,7},{5,4},{6,5},{7,6},{8,11},{9,8},{10,9... | collective-permute-start | bytes 393224 | tf_op jit(solution)/shard_map/ppermute | solution.py:55
  269.6 0.6 collective-permute-done.12
  270.2 1.9 collective-permute-start.14
  272.1 5.6 %collective-permute-done.14 = bf16[128,512]{0,1:T(8,128)(2,1)S(1)} collective-permute-done((bf16[128,512]{0,1:T(8,128)(2,1)S(1)}, bf16[128,512]{0,1:T(8,128)(2,1)S(1)}, u32[]{:S(2)}, u32[]{:S(2)}) %collective-permute-start.14) | collective-permute-done | bytes 131104 | tf_op jit(solution)/shard_map/ppermute | solution.py:56
  277.7 1.9 collective-permute-start.15
  280.5 4.8 %collective-permute-start.16 = (bf16[512,512]{0,1:T(8,128)(2,1)S(1)}, bf16[512,512]{0,1:T(8,128)(2,1)S(1)}, u32[]{:S(2)}, u32[]{:S(2)}) collective-permute-start(bf16[512,512]{0,1:T(8,128)(2,1)S(1)} %pad_maximum_fusion.3), channel_id=1, source_target_pairs={{0,12},{1,13},{2,14},{3,15},{4,0},{5,1},{6,2},{7,3},{8,4},{9,5},{1... | collective-permute-start | bytes 1572872 | tf_op jit(solution)/shard_map/ppermute | solution.py:55
  285.3 3.9 %collective-permute-done.15 = bf16[512,512]{0,1:T(8,128)(2,1)S(1)} collective-permute-done((bf16[512,512]{0,1:T(8,128)(2,1)S(1)}, bf16[512,512]{0,1:T(8,128)(2,1)S(1)}, u32[]{:S(2)}, u32[]{:S(2)}) %collective-permute-start.15) | collective-permute-done | bytes 524320 | tf_op jit(solution)/shard_map/ppermute | solution.py:54
  289.3 1.9 collective-permute-start.17
  291.5 8.9 %collective-permute-done.17 = bf16[512,512]{0,1:T(8,128)(2,1)S(1)} collective-permute-done((bf16[512,512]{0,1:T(8,128)(2,1)S(1)}, bf16[512,512]{0,1:T(8,128)(2,1)S(1)}, u32[]{:S(2)}, u32[]{:S(2)}) %collective-permute-start.17) | collective-permute-done | bytes 524320 | tf_op jit(solution)/shard_map/ppermute | solution.py:56
  300.5 1.4 fusion.27
  302.3 45.4 %all_to_all.25 = bf16[258,32,16]{0,2,1:T(8,128)(2,1)S(1)} all-to-all(bf16[258,32,16]{0,2,1:T(8,128)(2,1)S(1)} %bitcast.148), channel_id=1, replica_groups=mesh['island'=32,'fsdp'=16] {'island'}, dimensions={1} | all-to-all | bytes 528384 | tf_op jit(solution)/shard_map/all_to_all | solution.py:181
  348.4 0.7 multiply_subtract_fusion.1
  (104 shorter events, 7.1 us)
Async XLA Ops:
  0.6 21.1 %copy-start.8 = (bf16[128,4096]{1,0:T(8,128)(2,1)S(1)}, bf16[128,4096]{1,0:T(8,128)(2,1)}, u32[]{:S(2)}) copy-start(bf16[128,4096]{1,0:T(8,128)(2,1)} %param.12) | copy-start | bytes 3145732
  2.3 82.1 %all-to-all-start = ((f32[32,256,16]{1,2,0:T(8,128)}), f32[32,256,16]{1,2,0:T(8,128)S(1)}, u32[]{:S(2)}, u32[]{:S(2)}) async-start(f32[32,256,16]{1,2,0:T(8,128)} %broadcast_in_dim.53), calls=%async_computation | async-start | bytes 1048576 | tf_op jit(solution)/shard_map/all_to_all | solution.py:109
  21.8 9.4 %copy-start.23 = (s32[4]{0:T(128)S(1)}, s32[4]{0:T(128)}, u32[]{:S(2)}) copy-start(s32[4]{0:T(128)} %constant.145.clone) | copy-start | bytes 52
  22.6 35.1 %collective-permute-start.2 = (bf16[4,128,256]{1,2,0:T(8,128)(2,1)S(1)}, bf16[4,128,256]{1,2,0:T(8,128)(2,1)S(1)}, u32[]{:S(2)}, u32[]{:S(2)}) collective-permute-start(bf16[4,128,256]{1,2,0:T(8,128)(2,1)S(1)} %get-tuple-element.14), channel_id=1, source_target_pairs={{0,2},{1,3},{2,0},{3,1},{4,6},{5,7},{6,4},{7,5},{8,10},{9,11},{10,... | collective-permute-start | bytes 786440 | tf_op jit(solution)/shard_map/ppermute | solution.py:76
  25.7 32.0 %collective-permute-start.1 = (bf16[4,128,256]{1,2,0:T(8,128)(2,1)S(1)}, bf16[4,128,256]{1,2,0:T(8,128)(2,1)S(1)}, u32[]{:S(2)}, u32[]{:S(2)}) collective-permute-start(bf16[4,128,256]{1,2,0:T(8,128)(2,1)S(1)} %get-tuple-element.13), channel_id=1, source_target_pairs={{0,3},{1,0},{2,1},{3,2},{4,7},{5,4},{6,5},{7,6},{8,11},{9,8},{10,9... | collective-permute-start | bytes 786440 | tf_op jit(solution)/shard_map/ppermute | solution.py:76
  29.2 34.7 %collective-permute-start = (bf16[4,128,256]{1,2,0:T(8,128)(2,1)S(1)}, bf16[4,128,256]{1,2,0:T(8,128)(2,1)S(1)}, u32[]{:S(2)}, u32[]{:S(2)}) collective-permute-start(bf16[4,128,256]{1,2,0:T(8,128)(2,1)S(1)} %get-tuple-element.15), channel_id=1, source_target_pairs={{0,1},{1,2},{2,3},{3,0},{4,5},{5,6},{6,7},{7,4},{8,9},{9,10},{10,1... | collective-permute-start | bytes 786440 | tf_op jit(solution)/shard_map/ppermute | solution.py:76
  64.3 10.5 %collective-permute-start.5 = (bf16[4,128,256]{2,1,0:T(8,128)(2,1)S(1)}, bf16[4,128,256]{2,1,0:T(8,128)(2,1)S(1)}, u32[]{:S(2)}, u32[]{:S(2)}) collective-permute-start(bf16[4,128,256]{2,1,0:T(8,128)(2,1)S(1)} %bitcast.164), channel_id=1, source_target_pairs={{0,8},{1,9},{2,10},{3,11},{4,12},{5,13},{6,14},{7,15},{8,0},{9,1},... | collective-permute-start | bytes 786440 | tf_op jit(solution)/shard_map/ppermute | solution.py:83
  69.1 11.5 %collective-permute-start.4 = (bf16[4,128,256]{2,1,0:T(8,128)(2,1)S(1)}, bf16[4,128,256]{2,1,0:T(8,128)(2,1)S(1)}, u32[]{:S(2)}, u32[]{:S(2)}) collective-permute-start(bf16[4,128,256]{2,1,0:T(8,128)(2,1)S(1)} %bitcast.166), channel_id=1, source_target_pairs={{0,12},{1,13},{2,14},{3,15},{4,0},{5,1},{6,2},{7,3},{8,4},{9,5},{1... | collective-permute-start | bytes 786440 | tf_op jit(solution)/shard_map/ppermute | solution.py:83
  72.1 9.7 %collective-permute-start.3 = (bf16[4,128,256]{2,1,0:T(8,128)(2,1)S(1)}, bf16[4,128,256]{2,1,0:T(8,128)(2,1)S(1)}, u32[]{:S(2)}, u32[]{:S(2)}) collective-permute-start(bf16[4,128,256]{2,1,0:T(8,128)(2,1)S(1)} %bitcast.168), channel_id=1, source_target_pairs={{0,4},{1,5},{2,6},{3,7},{4,8},{5,9},{6,10},{7,11},{8,12},{9,13},{1... | collective-permute-start | bytes 786440 | tf_op jit(solution)/shard_map/ppermute | solution.py:83
  82.6 1.8 copy-start.1
  84.4 3.5 %copy-start = (f32[32,256,16]{1,2,0:T(8,128)}, f32[32,256,16]{1,2,0:T(8,128)S(1)}, u32[]{:S(2)}) copy-start(f32[32,256,16]{1,2,0:T(8,128)S(1)} %all-to-all-done) | copy-start | bytes 1572868
  87.9 9.6 %copy-start.9 = (bf16[128,4096]{1,0:T(8,128)(2,1)S(1)}, bf16[128,4096]{1,0:T(8,128)(2,1)}, u32[]{:S(2)}) copy-start(bf16[128,4096]{1,0:T(8,128)(2,1)} %param.13) | copy-start | bytes 3145732
  87.9 59.5 %all-to-all-start.1 = ((bf16[16,128,512]{2,1,0:T(8,128)(2,1)}), bf16[16,128,512]{2,1,0:T(8,128)(2,1)}, u32[]{:S(2)}, u32[]{:S(2)}) async-start(bf16[16,128,512]{2,1,0:T(8,128)(2,1)} %bitcast.139), calls=%async_computation.1 | async-start | bytes 4194304 | tf_op jit(solution)/shard_map/all_to_all | solution.py:138
  97.4 0.9 copy-start.19
  97.4 0.9 copy-start.22
  151.2 3.0 copy-start.4
  156.1 1.2 copy-start.10
  157.8 7.7 %collective-permute-start.6 = (bf16[128,512]{0,1:T(8,128)(2,1)S(1)}, bf16[128,512]{0,1:T(8,128)(2,1)S(1)}, u32[]{:S(2)}, u32[]{:S(2)}) collective-permute-start(bf16[128,512]{0,1:T(8,128)(2,1)S(1)} %bitcast.160), channel_id=1, source_target_pairs={{0,1},{1,2},{2,3},{3,0},{4,5},{5,6},{6,7},{7,4},{8,9},{9,10},{10,1... | collective-permute-start | bytes 393224 | tf_op jit(solution)/shard_map/ppermute | solution.py:54
  159.8 9.8 %collective-permute-start.7 = (bf16[128,512]{0,1:T(8,128)(2,1)S(1)}, bf16[128,512]{0,1:T(8,128)(2,1)S(1)}, u32[]{:S(2)}, u32[]{:S(2)}) collective-permute-start(bf16[128,512]{0,1:T(8,128)(2,1)S(1)} %bitcast.161), channel_id=1, source_target_pairs={{0,3},{1,0},{2,1},{3,2},{4,7},{5,4},{6,5},{7,6},{8,11},{9,8},{10,9... | collective-permute-start | bytes 393224 | tf_op jit(solution)/shard_map/ppermute | solution.py:55
  165.6 7.5 %collective-permute-start.8 = (bf16[128,512]{0,1:T(8,128)(2,1)S(1)}, bf16[128,512]{0,1:T(8,128)(2,1)S(1)}, u32[]{:S(2)}, u32[]{:S(2)}) collective-permute-start(bf16[128,512]{0,1:T(8,128)(2,1)S(1)} %collective-permute-done.6), channel_id=1, source_target_pairs={{0,1},{1,2},{2,3},{3,0},{4,5},{5,6},{6,7},{7,4},{8,9},{9,10},{10,1... | collective-permute-start | bytes 393224 | tf_op jit(solution)/shard_map/ppermute | solution.py:56
  173.1 0.9 copy-start.12
  173.9 12.1 %collective-permute-start.9 = (bf16[512,512]{0,1:T(8,128)(2,1)}, bf16[512,512]{0,1:T(8,128)(2,1)}, u32[]{:S(2)}, u32[]{:S(2)}) collective-permute-start(bf16[512,512]{0,1:T(8,128)(2,1)} %pad_maximum_fusion.2), channel_id=1, source_target_pairs={{0,4},{1,5},{2,6},{3,7},{4,8},{5,9},{6,10},{7,11},{8,12},{9,13},{1... | collective-permute-start | bytes 1572872 | tf_op jit(solution)/shard_map/ppermute | solution.py:54
  178.4 19.0 %copy-start.2 = (bf16[4,4,128,256]{3,2,1,0:T(8,128)(2,1)S(1)}, bf16[4,4,128,256]{3,2,1,0:T(8,128)(2,1)}, u32[]{:S(2)}) copy-start(bf16[4,4,128,256]{3,2,1,0:T(8,128)(2,1)} %copy-done.1) | copy-start | bytes 3145732
  178.4 11.6 %collective-permute-start.10 = (bf16[512,512]{0,1:T(8,128)(2,1)}, bf16[512,512]{0,1:T(8,128)(2,1)S(1)}, u32[]{:S(2)}, u32[]{:S(2)}) collective-permute-start(bf16[512,512]{0,1:T(8,128)(2,1)} %pad_maximum_fusion.2), channel_id=1, source_target_pairs={{0,12},{1,13},{2,14},{3,15},{4,0},{5,1},{6,2},{7,3},{8,4},{9,5},{1... | collective-permute-start | bytes 1572872 | tf_op jit(solution)/shard_map/ppermute | solution.py:55
  186.0 11.3 %collective-permute-start.11 = (bf16[512,512]{0,1:T(8,128)(2,1)}, bf16[512,512]{0,1:T(8,128)(2,1)S(1)}, u32[]{:S(2)}, u32[]{:S(2)}) collective-permute-start(bf16[512,512]{0,1:T(8,128)(2,1)} %collective-permute-done.9), channel_id=1, source_target_pairs={{0,4},{1,5},{2,6},{3,7},{4,8},{5,9},{6,10},{7,11},{8,12},{9,13},{1... | collective-permute-start | bytes 1572872 | tf_op jit(solution)/shard_map/ppermute | solution.py:56
  197.4 1.1 copy-start.6
  197.4 1.2 copy-start.13
  197.4 1.3 copy-start.15
  198.8 1.1 copy-start.17
  257.0 1.8 copy-start.5
  260.8 1.2 copy-start.11
  262.5 7.7 %collective-permute-start.12 = (bf16[128,512]{0,1:T(8,128)(2,1)S(1)}, bf16[128,512]{0,1:T(8,128)(2,1)S(1)}, u32[]{:S(2)}, u32[]{:S(2)}) collective-permute-start(bf16[128,512]{0,1:T(8,128)(2,1)S(1)} %bitcast.156), channel_id=1, source_target_pairs={{0,1},{1,2},{2,3},{3,0},{4,5},{5,6},{6,7},{7,4},{8,9},{9,10},{10,1... | collective-permute-start | bytes 393224 | tf_op jit(solution)/shard_map/ppermute | solution.py:54
  264.4 7.7 %collective-permute-start.13 = (bf16[128,512]{0,1:T(8,128)(2,1)S(1)}, bf16[128,512]{0,1:T(8,128)(2,1)S(1)}, u32[]{:S(2)}, u32[]{:S(2)}) collective-permute-start(bf16[128,512]{0,1:T(8,128)(2,1)S(1)} %bitcast.157), channel_id=1, source_target_pairs={{0,3},{1,0},{2,1},{3,2},{4,7},{5,4},{6,5},{7,6},{8,11},{9,8},{10,9... | collective-permute-start | bytes 393224 | tf_op jit(solution)/shard_map/ppermute | solution.py:55
  270.2 7.5 %collective-permute-start.14 = (bf16[128,512]{0,1:T(8,128)(2,1)S(1)}, bf16[128,512]{0,1:T(8,128)(2,1)S(1)}, u32[]{:S(2)}, u32[]{:S(2)}) collective-permute-start(bf16[128,512]{0,1:T(8,128)(2,1)S(1)} %collective-permute-done.12), channel_id=1, source_target_pairs={{0,1},{1,2},{2,3},{3,0},{4,5},{5,6},{6,7},{7,4},{8,9},{9,10},{10,1... | collective-permute-start | bytes 393224 | tf_op jit(solution)/shard_map/ppermute | solution.py:56
  277.7 11.5 %collective-permute-start.15 = (bf16[512,512]{0,1:T(8,128)(2,1)S(1)}, bf16[512,512]{0,1:T(8,128)(2,1)S(1)}, u32[]{:S(2)}, u32[]{:S(2)}) collective-permute-start(bf16[512,512]{0,1:T(8,128)(2,1)S(1)} %pad_maximum_fusion.3), channel_id=1, source_target_pairs={{0,4},{1,5},{2,6},{3,7},{4,8},{5,9},{6,10},{7,11},{8,12},{9,13},{1... | collective-permute-start | bytes 1572872 | tf_op jit(solution)/shard_map/ppermute | solution.py:54
  280.4 20.0 %copy-start.3 = (bf16[4,4,128,256]{3,2,1,0:T(8,128)(2,1)S(1)}, bf16[4,4,128,256]{3,2,1,0:T(8,128)(2,1)}, u32[]{:S(2)}) copy-start(bf16[4,4,128,256]{3,2,1,0:T(8,128)(2,1)} %copy-done.1) | copy-start | bytes 3145732
  280.4 20.0 %copy-start.7 = (f32[256,512]{1,0:T(8,128)S(1)}, f32[256,512]{1,0:T(8,128)}, u32[]{:S(2)}) copy-start(f32[256,512]{1,0:T(8,128)} %copy.99) | copy-start | bytes 1572868
  280.4 20.0 %copy-start.14 = (f32[1,256,512]{2,1,0:T(8,128)S(1)}, f32[1,256,512]{2,1,0:T(8,128)}, u32[]{:S(2)}) copy-start(f32[1,256,512]{2,1,0:T(8,128)} %param.17) | copy-start | bytes 1572868
  280.4 20.0 %copy-start.16 = (f32[1,256,512]{2,1,0:T(8,128)S(1)}, f32[1,256,512]{2,1,0:T(8,128)}, u32[]{:S(2)}) copy-start(f32[1,256,512]{2,1,0:T(8,128)} %param.18) | copy-start | bytes 1572868
  280.4 20.0 %copy-start.18 = (f32[256,512]{1,0:T(8,128)S(1)}, f32[256,512]{1,0:T(8,128)}, u32[]{:S(2)}) copy-start(f32[256,512]{1,0:T(8,128)} %copy-done.17) | copy-start | bytes 1572868
  280.5 10.9 %collective-permute-start.16 = (bf16[512,512]{0,1:T(8,128)(2,1)S(1)}, bf16[512,512]{0,1:T(8,128)(2,1)S(1)}, u32[]{:S(2)}, u32[]{:S(2)}) collective-permute-start(bf16[512,512]{0,1:T(8,128)(2,1)S(1)} %pad_maximum_fusion.3), channel_id=1, source_target_pairs={{0,12},{1,13},{2,14},{3,15},{4,0},{5,1},{6,2},{7,3},{8,4},{9,5},{1... | collective-permute-start | bytes 1572872 | tf_op jit(solution)/shard_map/ppermute | solution.py:55
  289.3 11.1 %collective-permute-start.17 = (bf16[512,512]{0,1:T(8,128)(2,1)S(1)}, bf16[512,512]{0,1:T(8,128)(2,1)S(1)}, u32[]{:S(2)}, u32[]{:S(2)}) collective-permute-start(bf16[512,512]{0,1:T(8,128)(2,1)S(1)} %collective-permute-done.15), channel_id=1, source_target_pairs={{0,4},{1,5},{2,6},{3,7},{4,8},{5,9},{6,10},{7,11},{8,12},{9,13},{1... | collective-permute-start | bytes 1572872 | tf_op jit(solution)/shard_map/ppermute | solution.py:56
  302.0 46.4 %copy-start.20 = (f32[256,16]{0,1:T(8,128)S(1)}, f32[256,16]{0,1:T(8,128)}, u32[]{:S(2)}) copy-start(f32[256,16]{0,1:T(8,128)} %param.19) | copy-start | bytes 49156
  302.0 46.4 %copy-start.21 = (f32[256,16]{0,1:T(8,128)S(1)}, f32[256,16]{0,1:T(8,128)}, u32[]{:S(2)}) copy-start(f32[256,16]{0,1:T(8,128)} %param.20) | copy-start | bytes 49156

commit v6 on v4

--- a/solution.py
+++ b/solution.py
@@ -62,6 +62,27 @@
 
     row = jnp.concatenate(along(piece, cols, 0, 1), axis=0)
     return jnp.concatenate(along(row, rows, 1, 0), axis=0)
+
+
+def block_sum(partial, rows, cols):
+    me = lax.axis_index("fsdp")
+    me_x, me_z = me // cols, me % cols
+    tokens = partial.shape[0] // (rows * cols)
+    mine = partial.reshape(rows, cols, tokens, partial.shape[1])
+    got = []
+    for dx in [0, 1, -1, 2]:
+        part = lax.dynamic_index_in_dim(mine, (me_x + dx) % rows, axis=0, keepdims=False)
+        if dx:
+            part = lax.ppermute(part, "fsdp", _shift(cols, rows, dx, 0))
+        got.append(part.astype(jnp.float32))
+    column = got[0] + got[1] + got[2] + got[3]
+    total = None
+    for dz in [0, 1, -1, 2]:
+        part = lax.dynamic_index_in_dim(column, (me_z + dz) % cols, axis=0, keepdims=False)
+        if dz:
+            part = lax.ppermute(part, "fsdp", _shift(cols, rows, 0, dz))
+        total = part if total is None else total + part
+    return total
 
 
 def on_device(
@@ -103,10 +124,13 @@
         partial = jnp.dot(
             feature_rows, master.astype(jnp.bfloat16), preferred_element_type=jnp.float32
         ).astype(jnp.bfloat16)
-        pieces = lax.all_to_all(
-            partial.reshape(members, rows, width), "fsdp", split_axis=0, concat_axis=0, tiled=True
-        )
-        projected = jnp.sum(pieces.astype(jnp.float32), axis=0)
+        if grid_rows == 4 and grid_cols == 4:
+            projected = block_sum(partial, grid_rows, grid_cols)
+        else:
+            pieces = lax.all_to_all(
+                partial.reshape(members, rows, width), "fsdp", split_axis=0, concat_axis=0, tiled=True
+            )
+            projected = jnp.sum(pieces.astype(jnp.float32), axis=0)
         values = (projected * scale_in).astype(jnp.bfloat16)
         mixed = jnp.einsum(
             "gjts,sgd->tgjd",

time: 347 us -> 355 us (1.023)
  blocking collectives: 166 us -> 108 us
  starting transfers between devices: 56.6 us -> 95.9 us
  waiting for transfers between devices: 76.9 us -> 100 us
  local copies, waits for them, and re-layouts: 19.5 us -> 24.8 us
    ppermute x0 -> x12, waiting for transfers between devices: none -> 61.3 us  [the longest x6 33.4 us: block_sum(): part = lax.ppermute(part, 'fsdp', _shift(cols, rows, dx, 0))]
    all_to_all x1 -> x0, blocking collectives: 57.2 us -> none  [on_device(): lax.all_to_all(partial.reshape(members, rows, width), 'fsdp', split_axis=...]
    ppermute x0 -> x12, starting transfers between devices: none -> 46.4 us  [the longest x6 27.3 us: block_sum(): part = lax.ppermute(part, 'fsdp', _shift(cols, rows, 0, dz))]
    all_to_all x1 -> x0, waiting for transfers between devices: 41.2 us -> none  [on_device(): lax.all_to_all(partial.reshape(members, rows, width), 'fsdp', split_axis=...]
    all_to_all x1 -> x0, starting transfers between devices: 12.3 us -> none  [on_device(): lax.all_to_all(partial.reshape(members, rows, width), 'fsdp', split_axis=...]
    ppermute x4, starting transfers between devices: 7.68 us -> 16.3 us  [along(): up = lax.ppermute(part, 'fsdp', _shift(cols, rows, dx, dz))]
    ppermute x4, starting transfers between devices: 19.9 us -> 16 us  [along(): down = lax.ppermute(part, 'fsdp', _shift(cols, rows, -dx, -dz))]
    unnamed x52 -> x60, local copies, waits for them, and re-layouts: 7.53 us -> 6.59 us
  transfers between devices with their start and end apart: 14 -> 25, of which waited for: 9 -> 19; matrix products, arithmetic and copies ran while one was open for 4% -> 3% of each run, Pallas kernels for 0% -> 0%
where the time goes in v6:
time: 355 us; the launch traced here: 354 us
  blocking collectives  108 us (30%)
  waiting for transfers between devices  100 us (28%)
  starting transfers between devices  95.9 us (27%)
  local copies, waits for them, and re-layouts  24.8 us (7%)
  other arithmetic  12.2 us (3%)
  matrix products  10.8 us (3%)
    all_gather x1, blocking collectives, on_device(): master = lax.all_gather(anchor, 'island', axis=1, tiled=True)  70.1 us
    all_to_all x1, blocking collectives, on_device(): lax.all_to_all(sent.reshape(block + 2, groups, cols), 'island', split_axi...  37.6 us
    ppermute x6, waiting for transfers between devices, block_sum(): part = lax.ppermute(part, 'fsdp', _shift(cols, rows, dx, 0))  33.4 us
    ppermute x6, waiting for transfers between devices, block_sum(): part = lax.ppermute(part, 'fsdp', _shift(cols, rows, 0, dz))  27.9 us
    ppermute x6, starting transfers between devices, block_sum(): part = lax.ppermute(part, 'fsdp', _shift(cols, rows, 0, dz))  27.3 us
    ppermute x4, waiting for transfers between devices, along(): far = lax.ppermute(up, 'fsdp', _shift(cols, rows, dx, dz))  26.5 us
    ppermute x6, starting transfers between devices, block_sum(): part = lax.ppermute(part, 'fsdp', _shift(cols, rows, dx, 0))  19.1 us
    ppermute x4, starting transfers between devices, along(): up = lax.ppermute(part, 'fsdp', _shift(cols, rows, dx, dz))  16.3 us
  transfers between devices with their start and end apart: 25, of which 19 were waited for; matrix products, arithmetic and copies ran while one was open for 3% of the time, Pallas kernels for 0%

profile of v6, /device:TPU:1, one launch (start us, length us, event | category | flops | bytes accessed | tf_op | source)
XLA Modules:
  0.0 353.7 jit_solution(5001300764268790554)
XLA Ops:
  0.6 1.6 copy.63
  2.3 1.3 copy.64
  3.6 9.1 %all-to-all-start = ((bf16[128,16,256]{2,0,1:T(8,128)(2,1)}), bf16[128,16,256]{2,0,1:T(8,128)(2,1)S(1)}, u32[]{:S(2)}, u32[]{:S(2)}) async-start(bf16[128,16,256]{2,0,1:T(8,128)(2,1)} %copy.64), calls=%async_computation | async-start | bytes 2097152 | tf_op jit(solution)/shard_map/all_to_all | solution.py:112
  13.4 70.1 %all_gather.3 = f32[256,512]{0,1:T(8,128)S(1)} all-gather(f32[256,16]{0,1:T(8,128)S(1)} %copy-done.10), channel_id=1, replica_groups=mesh['island'=32,'fsdp'=16] {'island'}, dimensions={1}, use_global_device_ids=true | all-gather | bytes 540672 | tf_op jit(solution)/shard_map/all_gather | solution.py:107
  83.4 2.3 fusion.74
  86.6 3.5 collective-permute-start
  90.1 3.1 collective-permute-start.1
  93.3 3.8 %collective-permute-start.2 = (bf16[4,128,512]{2,1,0:T(8,128)(2,1)S(1)}, bf16[4,128,512]{2,1,0:T(8,128)(2,1)S(1)}, u32[]{:S(2)}, u32[]{:S(2)}) collective-permute-start(bf16[4,128,512]{2,1,0:T(8,128)(2,1)S(1)} %get-tuple-element.10), channel_id=1, source_target_pairs={{0,8},{1,9},{2,10},{3,11},{4,12},{5,13},{6,14},{7,15},{8,0},{9,1},... | collective-permute-start | bytes 1572872 | tf_op jit(solution)/shard_map/ppermute | solution.py:76
  97.4 5.8 %collective-permute-done = bf16[4,128,512]{2,1,0:T(8,128)(2,1)S(1)} collective-permute-done((bf16[4,128,512]{2,1,0:T(8,128)(2,1)S(1)}, bf16[4,128,512]{2,1,0:T(8,128)(2,1)S(1)}, u32[]{:S(2)}, u32[]{:S(2)}) %collective-permute-start) | collective-permute-done | bytes 524320 | tf_op jit(solution)/shard_map/ppermute | solution.py:76
  103.2 1.8 collective-permute-done.1
  105.0 10.6 %collective-permute-done.2 = bf16[4,128,512]{2,1,0:T(8,128)(2,1)S(1)} collective-permute-done((bf16[4,128,512]{2,1,0:T(8,128)(2,1)S(1)}, bf16[4,128,512]{2,1,0:T(8,128)(2,1)S(1)}, u32[]{:S(2)}, u32[]{:S(2)}) %collective-permute-start.2) | collective-permute-done | bytes 524320 | tf_op jit(solution)/shard_map/ppermute | solution.py:76
  115.6 1.3 fusion.16
  116.9 1.2 dynamic-slice_bitcast_fusion.8
  118.0 10.1 %collective-permute-start.3 = (f32[128,512]{1,0:T(8,128)S(1)}, f32[128,512]{1,0:T(8,128)}, u32[]{:S(2)}, u32[]{:S(2)}) collective-permute-start(f32[128,512]{1,0:T(8,128)S(1)} %get-tuple-element.16), channel_id=1, source_target_pairs={{0,1},{1,2},{2,3},{3,0},{4,5},{5,6},{6,7},{7,4},{8,9},{9,10},{10,1... | collective-permute-start | bytes 786440 | tf_op jit(solution)/shard_map/ppermute | solution.py:83
  128.2 1.9 collective-permute-start.4
  130.1 3.1 collective-permute-start.5
  134.0 1.7 copy.70
  136.2 2.3 collective-permute-done.4
  138.5 9.5 %collective-permute-done.5 = f32[128,512]{1,0:T(8,128)} collective-permute-done((f32[128,512]{1,0:T(8,128)S(1)}, f32[128,512]{1,0:T(8,128)}, u32[]{:S(2)}, u32[]{:S(2)}) %collective-permute-start.5) | collective-permute-done | bytes 262176 | tf_op jit(solution)/shard_map/ppermute | solution.py:83
  148.0 1.3 fusion.42
  149.4 1.8 fusion.79
  151.2 2.9 copy.69
  154.1 2.2 fusion.12
  156.5 1.0 copy-done.5
  158.0 4.5 %collective-permute-start.6 = (bf16[128,512]{0,1:T(8,128)(2,1)S(1)}, bf16[128,512]{0,1:T(8,128)(2,1)S(1)}, u32[]{:S(2)}, u32[]{:S(2)}) collective-permute-start(bf16[128,512]{0,1:T(8,128)(2,1)S(1)} %bitcast.172), channel_id=1, source_target_pairs={{0,1},{1,2},{2,3},{3,0},{4,5},{5,6},{6,7},{7,4},{8,9},{9,10},{10,1... | collective-permute-start | bytes 393224 | tf_op jit(solution)/shard_map/ppermute | solution.py:54
  163.1 4.8 %collective-permute-start.7 = (bf16[128,512]{0,1:T(8,128)(2,1)S(1)}, bf16[128,512]{0,1:T(8,128)(2,1)S(1)}, u32[]{:S(2)}, u32[]{:S(2)}) collective-permute-start(bf16[128,512]{0,1:T(8,128)(2,1)S(1)} %bitcast.173), channel_id=1, source_target_pairs={{0,3},{1,0},{2,1},{3,2},{4,7},{5,4},{6,5},{7,6},{8,11},{9,8},{10,9... | collective-permute-start | bytes 393224 | tf_op jit(solution)/shard_map/ppermute | solution.py:55
  168.3 1.9 collective-permute-start.8
  170.2 1.0 copy.81
  172.6 3.3 collective-permute-done.8
  175.9 1.0 pad_maximum_fusion
  176.9 4.4 %collective-permute-start.9 = (bf16[512,512]{0,1:T(8,128)(2,1)S(1)}, bf16[512,512]{0,1:T(8,128)(2,1)S(1)}, u32[]{:S(2)}, u32[]{:S(2)}) collective-permute-start(bf16[512,512]{0,1:T(8,128)(2,1)S(1)} %pad_maximum_fusion), channel_id=1, source_target_pairs={{0,4},{1,5},{2,6},{3,7},{4,8},{5,9},{6,10},{7,11},{8,12},{9,13},{1... | collective-permute-start | bytes 1572872 | tf_op jit(solution)/shard_map/ppermute | solution.py:54
  181.3 1.1 bitcast_select_fusion.2
  182.4 2.6 collective-permute-start.10
  185.1 6.4 %collective-permute-done.9 = bf16[512,512]{0,1:T(8,128)(2,1)S(1)} collective-permute-done((bf16[512,512]{0,1:T(8,128)(2,1)S(1)}, bf16[512,512]{0,1:T(8,128)(2,1)S(1)}, u32[]{:S(2)}, u32[]{:S(2)}) %collective-permute-start.9) | collective-permute-done | bytes 524320 | tf_op jit(solution)/shard_map/ppermute | solution.py:54
  191.4 2.4 collective-permute-start.11
  193.9 0.9 constant_dynamic-update-slice_fusion.3
  195.0 9.6 %collective-permute-done.11 = bf16[512,512]{0,1:T(8,128)(2,1)S(1)} collective-permute-done((bf16[512,512]{0,1:T(8,128)(2,1)S(1)}, bf16[512,512]{0,1:T(8,128)(2,1)S(1)}, u32[]{:S(2)}, u32[]{:S(2)}) %collective-permute-start.11) | collective-permute-done | bytes 524320 | tf_op jit(solution)/shard_map/ppermute | solution.py:56
  206.3 2.4 fusion.1
  208.8 3.2 reshape.163
  212.6 1.9 collective-permute-start.12
  214.5 4.6 %collective-permute-start.13 = (bf16[4,128,512]{1,0,2:T(4,128)(2,1)S(1)}, bf16[4,128,512]{1,0,2:T(4,128)(2,1)S(1)}, u32[]{:S(2)}, u32[]{:S(2)}) collective-permute-start(bf16[4,128,512]{1,0,2:T(4,128)(2,1)S(1)} %get-tuple-element.8), channel_id=1, source_target_pairs={{0,12},{1,13},{2,14},{3,15},{4,0},{5,1},{6,2},{7,3},{8,4},{9,5},{1... | collective-permute-start | bytes 1572872 | tf_op jit(solution)/shard_map/ppermute | solution.py:76
  219.1 2.1 collective-permute-start.14
  221.2 3.7 %collective-permute-done.12 = bf16[4,128,512]{1,0,2:T(4,128)(2,1)S(1)} collective-permute-done((bf16[4,128,512]{1,0,2:T(4,128)(2,1)S(1)}, bf16[4,128,512]{1,0,2:T(4,128)(2,1)S(1)}, u32[]{:S(2)}, u32[]{:S(2)}) %collective-permute-start.12) | collective-permute-done | bytes 524320 | tf_op jit(solution)/shard_map/ppermute | solution.py:76
  224.9 1.6 collective-permute-done.13
  226.5 9.9 %collective-permute-done.14 = bf16[4,128,512]{1,0,2:T(4,128)(2,1)S(1)} collective-permute-done((bf16[4,128,512]{1,0,2:T(4,128)(2,1)S(1)}, bf16[4,128,512]{1,0,2:T(4,128)(2,1)S(1)}, u32[]{:S(2)}, u32[]{:S(2)}) %collective-permute-start.14) | collective-permute-done | bytes 524320 | tf_op jit(solution)/shard_map/ppermute | solution.py:76
  238.0 3.5 collective-permute-start.15
  241.7 4.2 %collective-permute-start.16 = (f32[128,512]{1,0:T(8,128)S(1)}, f32[128,512]{1,0:T(8,128)S(1)}, u32[]{:S(2)}, u32[]{:S(2)}) collective-permute-start(f32[128,512]{1,0:T(8,128)S(1)} %bitcast.181), channel_id=1, source_target_pairs={{0,3},{1,0},{2,1},{3,2},{4,7},{5,4},{6,5},{7,6},{8,11},{9,8},{10,9... | collective-permute-start | bytes 786440 | tf_op jit(solution)/shard_map/ppermute | solution.py:83
  246.1 4.4 %collective-permute-start.17 = (f32[128,512]{1,0:T(8,128)S(1)}, f32[128,512]{1,0:T(8,128)S(1)}, u32[]{:S(2)}, u32[]{:S(2)}) collective-permute-start(f32[128,512]{1,0:T(8,128)S(1)} %bitcast.182), channel_id=1, source_target_pairs={{0,2},{1,3},{2,0},{3,1},{4,6},{5,7},{6,4},{7,5},{8,10},{9,11},{10,... | collective-permute-start | bytes 786440 | tf_op jit(solution)/shard_map/ppermute | solution.py:83
  251.2 15.4 %collective-permute-done.17 = f32[128,512]{1,0:T(8,128)S(1)} collective-permute-done((f32[128,512]{1,0:T(8,128)S(1)}, f32[128,512]{1,0:T(8,128)S(1)}, u32[]{:S(2)}, u32[]{:S(2)}) %collective-permute-start.17) | collective-permute-done | bytes 262176 | tf_op jit(solution)/shard_map/ppermute | solution.py:83
  267.3 1.9 copy.79
  269.2 1.9 fusion.11
  271.3 1.0 copy-done.6
  272.8 1.9 collective-permute-start.18
  274.7 5.2 %collective-permute-start.19 = (bf16[128,512]{0,1:T(8,128)(2,1)S(1)}, bf16[128,512]{0,1:T(8,128)(2,1)S(1)}, u32[]{:S(2)}, u32[]{:S(2)}) collective-permute-start(bf16[128,512]{0,1:T(8,128)(2,1)S(1)} %bitcast.177), channel_id=1, source_target_pairs={{0,3},{1,0},{2,1},{3,2},{4,7},{5,4},{6,5},{7,6},{8,11},{9,8},{10,9... | collective-permute-start | bytes 393224 | tf_op jit(solution)/shard_map/ppermute | solution.py:55
  280.5 1.9 collective-permute-start.20
  282.4 5.6 %collective-permute-done.20 = bf16[128,512]{0,1:T(8,128)(2,1)S(1)} collective-permute-done((bf16[128,512]{0,1:T(8,128)(2,1)S(1)}, bf16[128,512]{0,1:T(8,128)(2,1)S(1)}, u32[]{:S(2)}, u32[]{:S(2)}) %collective-permute-start.20) | collective-permute-done | bytes 131104 | tf_op jit(solution)/shard_map/ppermute | solution.py:56
  288.0 5.4 %collective-permute-start.21 = (bf16[512,512]{0,1:T(8,128)(2,1)S(1)}, bf16[512,512]{0,1:T(8,128)(2,1)S(1)}, u32[]{:S(2)}, u32[]{:S(2)}) collective-permute-start(bf16[512,512]{0,1:T(8,128)(2,1)S(1)} %pad_maximum_fusion.1), channel_id=1, source_target_pairs={{0,4},{1,5},{2,6},{3,7},{4,8},{5,9},{6,10},{7,11},{8,12},{9,13},{1... | collective-permute-start | bytes 1572872 | tf_op jit(solution)/shard_map/ppermute | solution.py:54
  294.3 3.4 collective-permute-start.22
  297.7 3.9 %collective-permute-done.21 = bf16[512,512]{0,1:T(8,128)(2,1)S(1)} collective-permute-done((bf16[512,512]{0,1:T(8,128)(2,1)S(1)}, bf16[512,512]{0,1:T(8,128)(2,1)S(1)}, u32[]{:S(2)}, u32[]{:S(2)}) %collective-permute-start.21) | collective-permute-done | bytes 524320 | tf_op jit(solution)/shard_map/ppermute | solution.py:54
  301.7 1.9 collective-permute-start.23
  303.8 1.0 collective-permute-done.22
  304.8 8.0 %collective-permute-done.23 = bf16[512,512]{0,1:T(8,128)(2,1)S(1)} collective-permute-done((bf16[512,512]{0,1:T(8,128)(2,1)S(1)}, bf16[512,512]{0,1:T(8,128)(2,1)S(1)}, u32[]{:S(2)}, u32[]{:S(2)}) %collective-permute-start.23) | collective-permute-done | bytes 524320 | tf_op jit(solution)/shard_map/ppermute | solution.py:56
  312.9 1.4 fusion.32
  314.6 37.6 %all_to_all.28 = bf16[258,32,16]{0,2,1:T(8,128)(2,1)S(1)} all-to-all(bf16[258,32,16]{0,2,1:T(8,128)(2,1)S(1)} %bitcast.165), channel_id=1, replica_groups=mesh['island'=32,'fsdp'=16] {'island'}, dimensions={1} | all-to-all | bytes 528384 | tf_op jit(solution)/shard_map/all_to_all | solution.py:173
  (105 shorter events, 15.1 us)
Async XLA Ops:
  2.3 10.7 %copy-start.4 = (bf16[128,4096]{1,0:T(8,128)(2,1)S(1)}, bf16[128,4096]{1,0:T(8,128)(2,1)}, u32[]{:S(2)}) copy-start(bf16[128,4096]{1,0:T(8,128)(2,1)} %param.13) | copy-start | bytes 3145732
  3.6 9.6 %copy-start.9 = (bf16[128,512]{1,0:T(8,128)(2,1)S(1)}, bf16[128,512]{1,0:T(8,128)(2,1)}, u32[]{:S(2)}) copy-start(bf16[128,512]{1,0:T(8,128)(2,1)} %param.14) | copy-start | bytes 393220
  3.6 9.7 %copy-start.12 = (s32[1,128]{1,0:T(1,128)S(1)}, s32[1,128]{1,0:T(1,128)}, u32[]{:S(2)}) copy-start(s32[1,128]{1,0:T(1,128)} %param.16) | copy-start | bytes 1540
  3.6 9.8 %copy-start.10 = (f32[256,16]{0,1:T(8,128)S(1)}, f32[256,16]{0,1:T(8,128)}, u32[]{:S(2)}) copy-start(f32[256,16]{0,1:T(8,128)} %param.19) | copy-start | bytes 49156
  3.6 82.1 %all-to-all-start = ((bf16[128,16,256]{2,0,1:T(8,128)(2,1)}), bf16[128,16,256]{2,0,1:T(8,128)(2,1)S(1)}, u32[]{:S(2)}, u32[]{:S(2)}) async-start(bf16[128,16,256]{2,0,1:T(8,128)(2,1)} %copy.64), calls=%async_computation | async-start | bytes 2097152 | tf_op jit(solution)/shard_map/all_to_all | solution.py:112
  86.5 10.7 %copy-start.13 = (s32[4]{0:T(128)S(1)}, s32[4]{0:T(128)}, u32[]{:S(2)}) copy-start(s32[4]{0:T(128)} %constant.181.clone) | copy-start | bytes 52
  86.5 10.7 %copy-start.1 = (f32[4,8,128,128]{2,3,1,0:T(8,128)S(1)}, f32[4,8,128,128]{2,3,1,0:T(8,128)}, u32[]{:S(2)}) copy-start(f32[4,8,128,128]{2,3,1,0:T(8,128)} %get-tuple-element.22) | copy-start | bytes 6291460
  86.6 16.6 %collective-permute-start = (bf16[4,128,512]{2,1,0:T(8,128)(2,1)S(1)}, bf16[4,128,512]{2,1,0:T(8,128)(2,1)S(1)}, u32[]{:S(2)}, u32[]{:S(2)}) collective-permute-start(bf16[4,128,512]{2,1,0:T(8,128)(2,1)S(1)} %get-tuple-element.9), channel_id=1, source_target_pairs={{0,4},{1,5},{2,6},{3,7},{4,8},{5,9},{6,10},{7,11},{8,12},{9,13},{1... | collective-permute-start | bytes 1572872 | tf_op jit(solution)/shard_map/ppermute | solution.py:76
  90.1 14.9 %collective-permute-start.1 = (bf16[4,128,512]{2,1,0:T(8,128)(2,1)S(1)}, bf16[4,128,512]{2,1,0:T(8,128)(2,1)S(1)}, u32[]{:S(2)}, u32[]{:S(2)}) collective-permute-start(bf16[4,128,512]{2,1,0:T(8,128)(2,1)S(1)} %get-tuple-element.11), channel_id=1, source_target_pairs={{0,12},{1,13},{2,14},{3,15},{4,0},{5,1},{6,2},{7,3},{8,4},{9,5},{1... | collective-permute-start | bytes 1572872 | tf_op jit(solution)/shard_map/ppermute | solution.py:76
  93.3 22.3 %collective-permute-start.2 = (bf16[4,128,512]{2,1,0:T(8,128)(2,1)S(1)}, bf16[4,128,512]{2,1,0:T(8,128)(2,1)S(1)}, u32[]{:S(2)}, u32[]{:S(2)}) collective-permute-start(bf16[4,128,512]{2,1,0:T(8,128)(2,1)S(1)} %get-tuple-element.10), channel_id=1, source_target_pairs={{0,8},{1,9},{2,10},{3,11},{4,12},{5,13},{6,14},{7,15},{8,0},{9,1},... | collective-permute-start | bytes 1572872 | tf_op jit(solution)/shard_map/ppermute | solution.py:76
  118.0 18.1 %collective-permute-start.3 = (f32[128,512]{1,0:T(8,128)S(1)}, f32[128,512]{1,0:T(8,128)}, u32[]{:S(2)}, u32[]{:S(2)}) collective-permute-start(f32[128,512]{1,0:T(8,128)S(1)} %get-tuple-element.16), channel_id=1, source_target_pairs={{0,1},{1,2},{2,3},{3,0},{4,5},{5,6},{6,7},{7,4},{8,9},{9,10},{10,1... | collective-permute-start | bytes 786440 | tf_op jit(solution)/shard_map/ppermute | solution.py:83
  128.2 10.3 %collective-permute-start.4 = (f32[128,512]{1,0:T(8,128)S(1)}, f32[128,512]{1,0:T(8,128)}, u32[]{:S(2)}, u32[]{:S(2)}) collective-permute-start(f32[128,512]{1,0:T(8,128)S(1)} %get-tuple-element.18), channel_id=1, source_target_pairs={{0,3},{1,0},{2,1},{3,2},{4,7},{5,4},{6,5},{7,6},{8,11},{9,8},{10,9... | collective-permute-start | bytes 786440 | tf_op jit(solution)/shard_map/ppermute | solution.py:83
  130.1 17.9 %collective-permute-start.5 = (f32[128,512]{1,0:T(8,128)S(1)}, f32[128,512]{1,0:T(8,128)}, u32[]{:S(2)}, u32[]{:S(2)}) collective-permute-start(f32[128,512]{1,0:T(8,128)S(1)} %get-tuple-element.17), channel_id=1, source_target_pairs={{0,2},{1,3},{2,0},{3,1},{4,6},{5,7},{6,4},{7,5},{8,10},{9,11},{10,... | collective-permute-start | bytes 786440 | tf_op jit(solution)/shard_map/ppermute | solution.py:83
  156.3 1.2 copy-start.5
  157.5 5.0 %copy-start.15 = (pred[16]{0:T(512)(128)(4,1)S(1)}, pred[16]{0:T(512)(128)(4,1)}, u32[]{:S(2)}) copy-start(pred[16]{0:T(512)(128)(4,1)} %compare_and_fusion) | copy-start | bytes 52
  157.5 12.7 %copy-start.14 = (s32[16,1]{0,1:T(1,128)S(1)}, s32[16,1]{0,1:T(1,128)}, u32[]{:S(2)}) copy-start(s32[16,1]{0,1:T(1,128)} %add.246) | copy-start | bytes 196
  158.0 10.3 %collective-permute-start.6 = (bf16[128,512]{0,1:T(8,128)(2,1)S(1)}, bf16[128,512]{0,1:T(8,128)(2,1)S(1)}, u32[]{:S(2)}, u32[]{:S(2)}) collective-permute-start(bf16[128,512]{0,1:T(8,128)(2,1)S(1)} %bitcast.172), channel_id=1, source_target_pairs={{0,1},{1,2},{2,3},{3,0},{4,5},{5,6},{6,7},{7,4},{8,9},{9,10},{10,1... | collective-permute-start | bytes 393224 | tf_op jit(solution)/shard_map/ppermute | solution.py:54
  163.1 9.4 %collective-permute-start.7 = (bf16[128,512]{0,1:T(8,128)(2,1)S(1)}, bf16[128,512]{0,1:T(8,128)(2,1)S(1)}, u32[]{:S(2)}, u32[]{:S(2)}) collective-permute-start(bf16[128,512]{0,1:T(8,128)(2,1)S(1)} %bitcast.173), channel_id=1, source_target_pairs={{0,3},{1,0},{2,1},{3,2},{4,7},{5,4},{6,5},{7,6},{8,11},{9,8},{10,9... | collective-permute-start | bytes 393224 | tf_op jit(solution)/shard_map/ppermute | solution.py:55
  168.3 7.6 %collective-permute-start.8 = (bf16[128,512]{0,1:T(8,128)(2,1)S(1)}, bf16[128,512]{0,1:T(8,128)(2,1)}, u32[]{:S(2)}, u32[]{:S(2)}) collective-permute-start(bf16[128,512]{0,1:T(8,128)(2,1)S(1)} %collective-permute-done.6), channel_id=1, source_target_pairs={{0,1},{1,2},{2,3},{3,0},{4,5},{5,6},{6,7},{7,4},{8,9},{9,10},{10,1... | collective-permute-start | bytes 393224 | tf_op jit(solution)/shard_map/ppermute | solution.py:56
  176.9 14.6 %collective-permute-start.9 = (bf16[512,512]{0,1:T(8,128)(2,1)S(1)}, bf16[512,512]{0,1:T(8,128)(2,1)S(1)}, u32[]{:S(2)}, u32[]{:S(2)}) collective-permute-start(bf16[512,512]{0,1:T(8,128)(2,1)S(1)} %pad_maximum_fusion), channel_id=1, source_target_pairs={{0,4},{1,5},{2,6},{3,7},{4,8},{5,9},{6,10},{7,11},{8,12},{9,13},{1... | collective-permute-start | bytes 1572872 | tf_op jit(solution)/shard_map/ppermute | solution.py:54
  182.4 22.3 %copy-start.2 = (bf16[2048,256]{1,0:T(8,128)(2,1)}, bf16[2048,256]{1,0:T(8,128)(2,1)S(1)}, u32[]{:S(2)}) copy-start(bf16[2048,256]{1,0:T(8,128)(2,1)S(1)} %bitcast_select_fusion.2) | copy-start | bytes 3145732
  182.4 12.5 %collective-permute-start.10 = (bf16[512,512]{0,1:T(8,128)(2,1)S(1)}, bf16[512,512]{0,1:T(8,128)(2,1)S(1)}, u32[]{:S(2)}, u32[]{:S(2)}) collective-permute-start(bf16[512,512]{0,1:T(8,128)(2,1)S(1)} %pad_maximum_fusion), channel_id=1, source_target_pairs={{0,12},{1,13},{2,14},{3,15},{4,0},{5,1},{6,2},{7,3},{8,4},{9,5},{1... | collective-permute-start | bytes 1572872 | tf_op jit(solution)/shard_map/ppermute | solution.py:55
  191.4 13.2 %collective-permute-start.11 = (bf16[512,512]{0,1:T(8,128)(2,1)S(1)}, bf16[512,512]{0,1:T(8,128)(2,1)S(1)}, u32[]{:S(2)}, u32[]{:S(2)}) collective-permute-start(bf16[512,512]{0,1:T(8,128)(2,1)S(1)} %collective-permute-done.9), channel_id=1, source_target_pairs={{0,4},{1,5},{2,6},{3,7},{4,8},{5,9},{6,10},{7,11},{8,12},{9,13},{1... | collective-permute-start | bytes 1572872 | tf_op jit(solution)/shard_map/ppermute | solution.py:56
  204.7 1.6 copy-start.7
  204.7 1.6 copy-start.16
  204.7 1.6 copy-start.18
  205.5 0.8 copy-start.20
  212.6 12.4 %collective-permute-start.12 = (bf16[4,128,512]{1,0,2:T(4,128)(2,1)S(1)}, bf16[4,128,512]{1,0,2:T(4,128)(2,1)S(1)}, u32[]{:S(2)}, u32[]{:S(2)}) collective-permute-start(bf16[4,128,512]{1,0,2:T(4,128)(2,1)S(1)} %get-tuple-element.6), channel_id=1, source_target_pairs={{0,4},{1,5},{2,6},{3,7},{4,8},{5,9},{6,10},{7,11},{8,12},{9,13},{1... | collective-permute-start | bytes 1572872 | tf_op jit(solution)/shard_map/ppermute | solution.py:76
  214.5 12.0 %collective-permute-start.13 = (bf16[4,128,512]{1,0,2:T(4,128)(2,1)S(1)}, bf16[4,128,512]{1,0,2:T(4,128)(2,1)S(1)}, u32[]{:S(2)}, u32[]{:S(2)}) collective-permute-start(bf16[4,128,512]{1,0,2:T(4,128)(2,1)S(1)} %get-tuple-element.8), channel_id=1, source_target_pairs={{0,12},{1,13},{2,14},{3,15},{4,0},{5,1},{6,2},{7,3},{8,4},{9,5},{1... | collective-permute-start | bytes 1572872 | tf_op jit(solution)/shard_map/ppermute | solution.py:76
  219.1 17.4 %collective-permute-start.14 = (bf16[4,128,512]{1,0,2:T(4,128)(2,1)S(1)}, bf16[4,128,512]{1,0,2:T(4,128)(2,1)S(1)}, u32[]{:S(2)}, u32[]{:S(2)}) collective-permute-start(bf16[4,128,512]{1,0,2:T(4,128)(2,1)S(1)} %get-tuple-element.7), channel_id=1, source_target_pairs={{0,8},{1,9},{2,10},{3,11},{4,12},{5,13},{6,14},{7,15},{8,0},{9,1},... | collective-permute-start | bytes 1572872 | tf_op jit(solution)/shard_map/ppermute | solution.py:76
  238.0 12.6 %collective-permute-start.15 = (f32[128,512]{1,0:T(8,128)S(1)}, f32[128,512]{1,0:T(8,128)S(1)}, u32[]{:S(2)}, u32[]{:S(2)}) collective-permute-start(f32[128,512]{1,0:T(8,128)S(1)} %bitcast.180), channel_id=1, source_target_pairs={{0,1},{1,2},{2,3},{3,0},{4,5},{5,6},{6,7},{7,4},{8,9},{9,10},{10,1... | collective-permute-start | bytes 786440 | tf_op jit(solution)/shard_map/ppermute | solution.py:83
  241.7 9.6 %collective-permute-start.16 = (f32[128,512]{1,0:T(8,128)S(1)}, f32[128,512]{1,0:T(8,128)S(1)}, u32[]{:S(2)}, u32[]{:S(2)}) collective-permute-start(f32[128,512]{1,0:T(8,128)S(1)} %bitcast.181), channel_id=1, source_target_pairs={{0,3},{1,0},{2,1},{3,2},{4,7},{5,4},{6,5},{7,6},{8,11},{9,8},{10,9... | collective-permute-start | bytes 786440 | tf_op jit(solution)/shard_map/ppermute | solution.py:83
  246.1 20.6 %collective-permute-start.17 = (f32[128,512]{1,0:T(8,128)S(1)}, f32[128,512]{1,0:T(8,128)S(1)}, u32[]{:S(2)}, u32[]{:S(2)}) collective-permute-start(f32[128,512]{1,0:T(8,128)S(1)} %bitcast.182), channel_id=1, source_target_pairs={{0,2},{1,3},{2,0},{3,1},{4,6},{5,7},{6,4},{7,5},{8,10},{9,11},{10,... | collective-permute-start | bytes 786440 | tf_op jit(solution)/shard_map/ppermute | solution.py:83
  267.3 1.9 copy-start
  271.1 1.2 copy-start.6
  272.8 7.7 %collective-permute-start.18 = (bf16[128,512]{0,1:T(8,128)(2,1)S(1)}, bf16[128,512]{0,1:T(8,128)(2,1)S(1)}, u32[]{:S(2)}, u32[]{:S(2)}) collective-permute-start(bf16[128,512]{0,1:T(8,128)(2,1)S(1)} %bitcast.176), channel_id=1, source_target_pairs={{0,1},{1,2},{2,3},{3,0},{4,5},{5,6},{6,7},{7,4},{8,9},{9,10},{10,1... | collective-permute-start | bytes 393224 | tf_op jit(solution)/shard_map/ppermute | solution.py:54
  274.7 7.7 %collective-permute-start.19 = (bf16[128,512]{0,1:T(8,128)(2,1)S(1)}, bf16[128,512]{0,1:T(8,128)(2,1)S(1)}, u32[]{:S(2)}, u32[]{:S(2)}) collective-permute-start(bf16[128,512]{0,1:T(8,128)(2,1)S(1)} %bitcast.177), channel_id=1, source_target_pairs={{0,3},{1,0},{2,1},{3,2},{4,7},{5,4},{6,5},{7,6},{8,11},{9,8},{10,9... | collective-permute-start | bytes 393224 | tf_op jit(solution)/shard_map/ppermute | solution.py:55
  280.5 7.5 %collective-permute-start.20 = (bf16[128,512]{0,1:T(8,128)(2,1)S(1)}, bf16[128,512]{0,1:T(8,128)(2,1)S(1)}, u32[]{:S(2)}, u32[]{:S(2)}) collective-permute-start(bf16[128,512]{0,1:T(8,128)(2,1)S(1)} %collective-permute-done.18), channel_id=1, source_target_pairs={{0,1},{1,2},{2,3},{3,0},{4,5},{5,6},{6,7},{7,4},{8,9},{9,10},{10,1... | collective-permute-start | bytes 393224 | tf_op jit(solution)/shard_map/ppermute | solution.py:56
  288.0 13.6 %collective-permute-start.21 = (bf16[512,512]{0,1:T(8,128)(2,1)S(1)}, bf16[512,512]{0,1:T(8,128)(2,1)S(1)}, u32[]{:S(2)}, u32[]{:S(2)}) collective-permute-start(bf16[512,512]{0,1:T(8,128)(2,1)S(1)} %pad_maximum_fusion.1), channel_id=1, source_target_pairs={{0,4},{1,5},{2,6},{3,7},{4,8},{5,9},{6,10},{7,11},{8,12},{9,13},{1... | collective-permute-start | bytes 1572872 | tf_op jit(solution)/shard_map/ppermute | solution.py:54
  294.2 18.6 %copy-start.3 = (bf16[2048,256]{1,0:T(8,128)(2,1)S(1)}, bf16[2048,256]{1,0:T(8,128)(2,1)}, u32[]{:S(2)}) copy-start(bf16[2048,256]{1,0:T(8,128)(2,1)} %copy-done.2) | copy-start | bytes 3145732
  294.2 18.6 %copy-start.8 = (f32[256,512]{1,0:T(8,128)S(1)}, f32[256,512]{1,0:T(8,128)}, u32[]{:S(2)}) copy-start(f32[256,512]{1,0:T(8,128)} %copy.81) | copy-start | bytes 1572868
  294.2 18.6 %copy-start.17 = (f32[1,256,512]{2,1,0:T(8,128)S(1)}, f32[1,256,512]{2,1,0:T(8,128)}, u32[]{:S(2)}) copy-start(f32[1,256,512]{2,1,0:T(8,128)} %param.17) | copy-start | bytes 1572868
  294.2 18.6 %copy-start.19 = (f32[1,256,512]{2,1,0:T(8,128)S(1)}, f32[1,256,512]{2,1,0:T(8,128)}, u32[]{:S(2)}) copy-start(f32[1,256,512]{2,1,0:T(8,128)} %param.18) | copy-start | bytes 1572868
  294.2 18.6 %copy-start.21 = (f32[256,512]{1,0:T(8,128)S(1)}, f32[256,512]{1,0:T(8,128)}, u32[]{:S(2)}) copy-start(f32[256,512]{1,0:T(8,128)} %copy-done.20) | copy-start | bytes 1572868
  294.3 10.5 %collective-permute-start.22 = (bf16[512,512]{0,1:T(8,128)(2,1)S(1)}, bf16[512,512]{0,1:T(8,128)(2,1)S(1)}, u32[]{:S(2)}, u32[]{:S(2)}) collective-permute-start(bf16[512,512]{0,1:T(8,128)(2,1)S(1)} %pad_maximum_fusion.1), channel_id=1, source_target_pairs={{0,12},{1,13},{2,14},{3,15},{4,0},{5,1},{6,2},{7,3},{8,4},{9,5},{1... | collective-permute-start | bytes 1572872 | tf_op jit(solution)/shard_map/ppermute | solution.py:55
  301.7 11.1 %collective-permute-start.23 = (bf16[512,512]{0,1:T(8,128)(2,1)S(1)}, bf16[512,512]{0,1:T(8,128)(2,1)S(1)}, u32[]{:S(2)}, u32[]{:S(2)}) collective-permute-start(bf16[512,512]{0,1:T(8,128)(2,1)S(1)} %collective-permute-done.21), channel_id=1, source_target_pairs={{0,4},{1,5},{2,6},{3,7},{4,8},{5,9},{6,10},{7,11},{8,12},{9,13},{1... | collective-permute-start | bytes 1572872 | tf_op jit(solution)/shard_map/ppermute | solution.py:56
  314.4 38.6 %copy-start.11 = (f32[256,16]{0,1:T(8,128)S(1)}, f32[256,16]{0,1:T(8,128)}, u32[]{:S(2)}) copy-start(f32[256,16]{0,1:T(8,128)} %param.20) | copy-start | bytes 49156

commit v7 on v4

--- a/solution.py
+++ b/solution.py
@@ -62,6 +62,42 @@
 
     row = jnp.concatenate(along(piece, cols, 0, 1), axis=0)
     return jnp.concatenate(along(row, rows, 1, 0), axis=0)
+
+
+def island_gather(block, sizes):
+    strides = [math.prod(sizes[k + 1 :]) for k in range(len(sizes))]
+    total = math.prod(sizes)
+    me = lax.axis_index("island")
+    coords = [(me // strides[k]) % sizes[k] for k in range(len(sizes))]
+
+    def shift(axis, step):
+        pairs = []
+        for src in range(total):
+            at = (src // strides[axis]) % sizes[axis]
+            pairs.append((src, src + (((at + step) % sizes[axis]) - at) * strides[axis]))
+        return pairs
+
+    pieces = [block]
+    sources = [me]
+    for axis in reversed(range(len(sizes))):
+        size = sizes[axis]
+        steps = [0, -1, 1, -2] if size == 4 else list(range(0, -size, -1))
+        moved = {0: jnp.stack(pieces, axis=0)}
+        if size == 4:
+            moved[-1] = lax.ppermute(moved[0], "island", shift(axis, 1))
+            moved[1] = lax.ppermute(moved[0], "island", shift(axis, -1))
+            moved[-2] = lax.ppermute(moved[-1], "island", shift(axis, 1))
+        else:
+            for k in range(1, size):
+                moved[-k] = lax.ppermute(moved[-k + 1], "island", shift(axis, 1))
+        pieces = [moved[o][n] for o in steps for n in range(len(pieces))]
+        sources = [
+            src + ((coords[axis] + o) % size - coords[axis]) * strides[axis]
+            for o in steps
+            for src in sources
+        ]
+    got = jnp.take(jnp.stack(pieces, axis=0), jnp.argsort(jnp.stack(sources)), axis=0)
+    return jnp.moveaxis(got, 0, -2).reshape(block.shape[:-1] + (total * block.shape[-1],))
 
 
 def on_device(
@@ -83,7 +119,10 @@
     scale_in = 1.0 / math.sqrt(hidden.shape[1])
     attention = attention_weights(query_rows, key_rows, segment_ids[0])
     groups = lax.axis_size("island")
-    master = lax.all_gather(anchor, "island", axis=1, tiled=True)
+    if groups == 32:
+        master = island_gather(anchor, (4, 4, 2))
+    else:
+        master = lax.all_gather(anchor, "island", axis=1, tiled=True)
     start_point = master
     block = master.shape[0]
     first = first_moment[0]

time: 347 us -> 329 us (0.948)
  blocking collectives: 166 us -> 94.9 us
  starting transfers between devices: 56.6 us -> 83.5 us
  waiting for transfers between devices: 76.9 us -> 101 us
    all_gather x1 -> x0, blocking collectives: 71 us -> none  [on_device(): master = lax.all_gather(anchor, 'island', axis=1, tiled=True)]
    ppermute x0 -> x7, starting transfers between devices: none -> 24.9 us  [the longest x2 11.5 us: island_gather(): moved[-1] = lax.ppermute(moved[0], 'island', shift(axis, 1))]
    ppermute x0 -> x7, waiting for transfers between devices: none -> 22.2 us  [the longest x2 11.7 us: island_gather(): moved[-2] = lax.ppermute(moved[-1], 'island', shift(axis, 1))]
    unnamed x52 -> x64, local copies, waits for them, and re-layouts: 7.53 us -> 6.62 us
  transfers between devices with their start and end apart: 14 -> 21, of which waited for: 9 -> 13; matrix products, arithmetic and copies ran while one was open for 4% -> 5% of each run, Pallas kernels for 0% -> 0%
where the time goes in v7:
time: 329 us; the launch traced here: 328 us
  waiting for transfers between devices  101 us (31%)
  blocking collectives  94.9 us (29%)
  starting transfers between devices  83.5 us (25%)
  local copies, waits for them, and re-layouts  21.4 us (7%)
  other arithmetic  14.3 us (4%)
  matrix products  10.8 us (3%)
    all_to_all x1, blocking collectives, on_device(): lax.all_to_all(partial.reshape(members, rows, width), 'fsdp', split_axis=...  56.2 us
    all_to_all x1, waiting for transfers between devices, on_device(): lax.all_to_all(partial.reshape(members, rows, width), 'fsdp', split_axis=...  42.8 us
    all_to_all x1, blocking collectives, on_device(): lax.all_to_all(sent.reshape(block + 2, groups, cols), 'island', split_axi...  38.7 us
    ppermute x4, waiting for transfers between devices, along(): far = lax.ppermute(up, 'fsdp', _shift(cols, rows, dx, dz))  26.3 us
    ppermute x4, starting transfers between devices, along(): down = lax.ppermute(part, 'fsdp', _shift(cols, rows, -dx, -dz))  19.7 us
    all_to_all x1, starting transfers between devices, on_device(): lax.all_to_all(partial.reshape(members, rows, width), 'fsdp', split_axis=...  14.5 us
    ppermute x2, waiting for transfers between devices, island_gather(): moved[-2] = lax.ppermute(moved[-1], 'island', shift(axis, 1))  11.7 us
    ppermute x2, starting transfers between devices, island_gather(): moved[-1] = lax.ppermute(moved[0], 'island', shift(axis, 1))  11.5 us
  transfers between devices with their start and end apart: 21, of which 13 were waited for; matrix products, arithmetic and copies ran while one was open for 5% of the time, Pallas kernels for 0%

profile of v7, /device:TPU:1, one launch (start us, length us, event | category | flops | bytes accessed | tf_op | source)
XLA Modules:
  0.0 327.8 jit_solution(11881248643325062341)
XLA Ops:
  0.6 1.6 copy.55
  2.3 1.3 copy.56
  3.6 9.0 %all-to-all-start = ((bf16[128,16,256]{2,0,1:T(8,128)(2,1)}), bf16[128,16,256]{2,0,1:T(8,128)(2,1)S(1)}, u32[]{:S(2)}, u32[]{:S(2)}) async-start(bf16[128,16,256]{2,0,1:T(8,128)(2,1)} %copy.56), calls=%async_computation | async-start | bytes 2097152 | tf_op jit(solution)/shard_map/all_to_all | solution.py:130
  12.6 3.4 %collective-permute-start = (f32[1,256,16]{1,2,0:T(8,128)S(1)}, f32[1,256,16]{1,2,0:T(8,128)S(1)}, u32[]{:S(2)}, u32[]{:S(2)}) collective-permute-start(f32[1,256,16]{1,2,0:T(8,128)S(1)} %bitcast.182), channel_id=1, source_target_pairs={{0,16},{16,0},{32,48},{48,32},{64,80},{80,64},{96,112},{112,96},{1... | collective-permute-start | bytes 49160 | tf_op jit(solution)/shard_map/ppermute | solution.py:92
  16.4 1.6 sort.17
  18.0 8.3 %collective-permute-start.1 = (f32[2,256,16]{1,2,0:T(8,128)S(1)}, f32[2,256,16]{1,2,0:T(8,128)S(1)}, u32[]{:S(2)}, u32[]{:S(2)}) collective-permute-start(f32[2,256,16]{1,2,0:T(8,128)S(1)} %pad_maximum_fusion.2), channel_id=1, source_target_pairs={{0,32},{16,48},{32,64},{48,80},{64,96},{80,112},{96,0},{112,16},{1... | collective-permute-start | bytes 98312 | tf_op jit(solution)/shard_map/ppermute | solution.py:87
  26.3 2.9 collective-permute-start.2
  29.2 9.8 %collective-permute-done.1 = f32[2,256,16]{1,2,0:T(8,128)S(1)} collective-permute-done((f32[2,256,16]{1,2,0:T(8,128)S(1)}, f32[2,256,16]{1,2,0:T(8,128)S(1)}, u32[]{:S(2)}, u32[]{:S(2)}) %collective-permute-start.1) | collective-permute-done | bytes 32800 | tf_op jit(solution)/shard_map/ppermute | solution.py:87
  39.0 1.9 collective-permute-start.3
  41.0 7.1 %collective-permute-done.3 = f32[2,256,16]{1,2,0:T(8,128)S(1)} collective-permute-done((f32[2,256,16]{1,2,0:T(8,128)S(1)}, f32[2,256,16]{1,2,0:T(8,128)S(1)}, u32[]{:S(2)}, u32[]{:S(2)}) %collective-permute-start.3) | collective-permute-done | bytes 32800 | tf_op jit(solution)/shard_map/ppermute | solution.py:89
  48.0 3.2 collective-permute-start.4
  51.2 3.4 %collective-permute-start.5 = (f32[8,256,16]{1,2,0:T(8,128)S(1)}, f32[8,256,16]{1,2,0:T(8,128)S(1)}, u32[]{:S(2)}, u32[]{:S(2)}) collective-permute-start(f32[8,256,16]{1,2,0:T(8,128)S(1)} %get-tuple-element.10), channel_id=1, source_target_pairs={{0,384},{16,400},{32,416},{48,432},{64,448},{80,464},{96,480},{112... | collective-permute-start | bytes 393224 | tf_op jit(solution)/shard_map/ppermute | solution.py:88
  55.0 1.9 collective-permute-start.6
  57.3 4.7 %collective-permute-done.6 = f32[8,256,16]{1,2,0:T(8,128)S(1)} collective-permute-done((f32[8,256,16]{1,2,0:T(8,128)S(1)}, f32[8,256,16]{1,2,0:T(8,128)S(1)}, u32[]{:S(2)}, u32[]{:S(2)}) %collective-permute-start.6) | collective-permute-done | bytes 131104 | tf_op jit(solution)/shard_map/ppermute | solution.py:89
  62.5 0.9 bitcast_convert_fusion
  63.5 0.7 fusion.6
  64.2 1.8 copy.109
  66.0 14.5 %all-to-all-start.1 = ((bf16[16,128,512]{1,2,0:T(8,128)(2,1)}), bf16[16,128,512]{1,2,0:T(8,128)(2,1)}, u32[]{:S(2)}, u32[]{:S(2)}) async-start(bf16[16,128,512]{1,2,0:T(8,128)(2,1)} %bitcast.157), calls=%async_computation.1 | async-start | bytes 4194304 | tf_op jit(solution)/shard_map/all_to_all | solution.py:145
  81.8 2.3 fusion.62
  84.1 1.8 divide_convert_fusion
  86.0 1.7 copy.62
  87.7 42.8 %all-to-all-done.1 = bf16[16,128,512]{1,2,0:T(8,128)(2,1)} async-done(((bf16[16,128,512]{1,2,0:T(8,128)(2,1)}), bf16[16,128,512]{1,2,0:T(8,128)(2,1)}, u32[]{:S(2)}, u32[]{:S(2)}) %all-to-all-start.1) | async-done | bytes 2097184 | tf_op jit(solution)/shard_map/all_to_all | solution.py:145
  130.5 1.9 convert_reduce_fusion.1
  132.4 1.8 fusion.67
  134.1 3.0 copy.61
  137.2 1.9 fusion.13
  139.3 1.0 copy-done.7
  140.8 1.9 collective-permute-start.7
  142.7 0.7 broadcast_bitcast_fusion
  143.4 5.1 %collective-permute-start.8 = (bf16[128,512]{0,1:T(8,128)(2,1)S(1)}, bf16[128,512]{0,1:T(8,128)(2,1)S(1)}, u32[]{:S(2)}, u32[]{:S(2)}) collective-permute-start(bf16[128,512]{0,1:T(8,128)(2,1)S(1)} %bitcast.175), channel_id=1, source_target_pairs={{0,3},{1,0},{2,1},{3,2},{4,7},{5,4},{6,5},{7,6},{8,11},{9,8},{10,9... | collective-permute-start | bytes 393224 | tf_op jit(solution)/shard_map/ppermute | solution.py:55
  148.5 1.9 collective-permute-start.9
  150.5 0.6 pad_clamp_fusion
  151.1 1.0 copy.69
  152.1 0.7 gather_fusion.1
  152.8 3.3 %collective-permute-done.9 = bf16[128,512]{0,1:T(8,128)(2,1)} collective-permute-done((bf16[128,512]{0,1:T(8,128)(2,1)S(1)}, bf16[128,512]{0,1:T(8,128)(2,1)}, u32[]{:S(2)}, u32[]{:S(2)}) %collective-permute-start.9) | collective-permute-done | bytes 131104 | tf_op jit(solution)/shard_map/ppermute | solution.py:56
  156.1 1.0 pad_maximum_fusion
  157.1 1.9 collective-permute-start.10
  159.0 1.1 bitcast_select_fusion.2
  160.2 4.6 %collective-permute-start.11 = (bf16[512,512]{0,1:T(8,128)(2,1)S(1)}, bf16[512,512]{0,1:T(8,128)(2,1)S(1)}, u32[]{:S(2)}, u32[]{:S(2)}) collective-permute-start(bf16[512,512]{0,1:T(8,128)(2,1)S(1)} %pad_maximum_fusion), channel_id=1, source_target_pairs={{0,12},{1,13},{2,14},{3,15},{4,0},{5,1},{6,2},{7,3},{8,4},{9,5},{1... | collective-permute-start | bytes 1572872 | tf_op jit(solution)/shard_map/ppermute | solution.py:55
  164.8 4.7 %collective-permute-done.10 = bf16[512,512]{0,1:T(8,128)(2,1)S(1)} collective-permute-done((bf16[512,512]{0,1:T(8,128)(2,1)S(1)}, bf16[512,512]{0,1:T(8,128)(2,1)S(1)}, u32[]{:S(2)}, u32[]{:S(2)}) %collective-permute-start.10) | collective-permute-done | bytes 524320 | tf_op jit(solution)/shard_map/ppermute | solution.py:54
  169.6 1.9 collective-permute-start.12
  171.6 0.9 constant_dynamic-update-slice_fusion.16
  172.7 8.5 %collective-permute-done.12 = bf16[512,512]{0,1:T(8,128)(2,1)S(1)} collective-permute-done((bf16[512,512]{0,1:T(8,128)(2,1)S(1)}, bf16[512,512]{0,1:T(8,128)(2,1)S(1)}, u32[]{:S(2)}, u32[]{:S(2)}) %collective-permute-start.12) | collective-permute-done | bytes 524320 | tf_op jit(solution)/shard_map/ppermute | solution.py:56
  181.3 0.8 fusion.68
  182.0 0.8 copy-done.13
  182.8 1.1 fusion.7
  184.5 56.2 %all_to_all.38 = bf16[16,128,512]{1,2,0:T(8,128)(2,1)S(1)} all-to-all(bf16[16,128,512]{1,2,0:T(8,128)(2,1)S(1)} %bitcast.163), channel_id=1, replica_groups=mesh['island'=32,'fsdp'=16] {'fsdp'}, dimensions={0} | all-to-all | bytes 4194304 | tf_op jit(solution)/shard_map/all_to_all | solution.py:145
  241.0 1.8 fusion.69
  242.7 1.9 copy.67
  244.7 1.5 fusion.12
  246.5 1.0 copy-done.8
  247.9 1.9 collective-permute-start.13
  249.8 5.2 %collective-permute-start.14 = (bf16[128,512]{0,1:T(8,128)(2,1)S(1)}, bf16[128,512]{0,1:T(8,128)(2,1)S(1)}, u32[]{:S(2)}, u32[]{:S(2)}) collective-permute-start(bf16[128,512]{0,1:T(8,128)(2,1)S(1)} %bitcast.179), channel_id=1, source_target_pairs={{0,3},{1,0},{2,1},{3,2},{4,7},{5,4},{6,5},{7,6},{8,11},{9,8},{10,9... | collective-permute-start | bytes 393224 | tf_op jit(solution)/shard_map/ppermute | solution.py:55
  255.0 0.6 collective-permute-done.13
  255.6 1.9 collective-permute-start.15
  257.5 5.6 %collective-permute-done.15 = bf16[128,512]{0,1:T(8,128)(2,1)S(1)} collective-permute-done((bf16[128,512]{0,1:T(8,128)(2,1)S(1)}, bf16[128,512]{0,1:T(8,128)(2,1)S(1)}, u32[]{:S(2)}, u32[]{:S(2)}) %collective-permute-start.15) | collective-permute-done | bytes 131104 | tf_op jit(solution)/shard_map/ppermute | solution.py:56
  263.2 1.9 collective-permute-start.16
  265.9 4.8 %collective-permute-start.17 = (bf16[512,512]{0,1:T(8,128)(2,1)S(1)}, bf16[512,512]{0,1:T(8,128)(2,1)S(1)}, u32[]{:S(2)}, u32[]{:S(2)}) collective-permute-start(bf16[512,512]{0,1:T(8,128)(2,1)S(1)} %pad_maximum_fusion.1), channel_id=1, source_target_pairs={{0,12},{1,13},{2,14},{3,15},{4,0},{5,1},{6,2},{7,3},{8,4},{9,5},{1... | collective-permute-start | bytes 1572872 | tf_op jit(solution)/shard_map/ppermute | solution.py:55
  270.8 3.9 %collective-permute-done.16 = bf16[512,512]{0,1:T(8,128)(2,1)S(1)} collective-permute-done((bf16[512,512]{0,1:T(8,128)(2,1)S(1)}, bf16[512,512]{0,1:T(8,128)(2,1)S(1)}, u32[]{:S(2)}, u32[]{:S(2)}) %collective-permute-start.16) | collective-permute-done | bytes 524320 | tf_op jit(solution)/shard_map/ppermute | solution.py:54
  274.7 1.9 collective-permute-start.18
  276.9 8.9 %collective-permute-done.18 = bf16[512,512]{0,1:T(8,128)(2,1)S(1)} collective-permute-done((bf16[512,512]{0,1:T(8,128)(2,1)S(1)}, bf16[512,512]{0,1:T(8,128)(2,1)S(1)}, u32[]{:S(2)}, u32[]{:S(2)}) %collective-permute-start.18) | collective-permute-done | bytes 524320 | tf_op jit(solution)/shard_map/ppermute | solution.py:56
  285.9 1.4 fusion.29
  287.7 38.7 %all_to_all.39 = bf16[258,32,16]{0,2,1:T(8,128)(2,1)S(1)} all-to-all(bf16[258,32,16]{0,2,1:T(8,128)(2,1)S(1)} %bitcast.166), channel_id=1, replica_groups=mesh['island'=32,'fsdp'=16] {'island'}, dimensions={1} | all-to-all | bytes 528384 | tf_op jit(solution)/shard_map/all_to_all | solution.py:188
  327.1 0.7 multiply_subtract_fusion.1
  (103 shorter events, 6.8 us)
Async XLA Ops:
  2.3 10.4 %copy-start.15 = (f32[256,16]{0,1:T(8,128)S(1)}, f32[256,16]{0,1:T(8,128)}, u32[]{:S(2)}) copy-start(f32[256,16]{0,1:T(8,128)} %param.19) | copy-start | bytes 49156
  3.6 59.9 %all-to-all-start = ((bf16[128,16,256]{2,0,1:T(8,128)(2,1)}), bf16[128,16,256]{2,0,1:T(8,128)(2,1)S(1)}, u32[]{:S(2)}, u32[]{:S(2)}) async-start(bf16[128,16,256]{2,0,1:T(8,128)(2,1)} %copy.56), calls=%async_computation | async-start | bytes 2097152 | tf_op jit(solution)/shard_map/all_to_all | solution.py:130
  12.6 5.4 %collective-permute-start = (f32[1,256,16]{1,2,0:T(8,128)S(1)}, f32[1,256,16]{1,2,0:T(8,128)S(1)}, u32[]{:S(2)}, u32[]{:S(2)}) collective-permute-start(f32[1,256,16]{1,2,0:T(8,128)S(1)} %bitcast.182), channel_id=1, source_target_pairs={{0,16},{16,0},{32,48},{48,32},{64,80},{80,64},{96,112},{112,96},{1... | collective-permute-start | bytes 49160 | tf_op jit(solution)/shard_map/ppermute | solution.py:92
  18.0 21.0 %collective-permute-start.1 = (f32[2,256,16]{1,2,0:T(8,128)S(1)}, f32[2,256,16]{1,2,0:T(8,128)S(1)}, u32[]{:S(2)}, u32[]{:S(2)}) collective-permute-start(f32[2,256,16]{1,2,0:T(8,128)S(1)} %pad_maximum_fusion.2), channel_id=1, source_target_pairs={{0,32},{16,48},{32,64},{48,80},{64,96},{80,112},{96,0},{112,16},{1... | collective-permute-start | bytes 98312 | tf_op jit(solution)/shard_map/ppermute | solution.py:87
  26.3 14.6 %collective-permute-start.2 = (f32[2,256,16]{1,2,0:T(8,128)S(1)}, f32[2,256,16]{1,2,0:T(8,128)S(1)}, u32[]{:S(2)}, u32[]{:S(2)}) collective-permute-start(f32[2,256,16]{1,2,0:T(8,128)S(1)} %pad_maximum_fusion.2), channel_id=1, source_target_pairs={{0,96},{16,112},{32,0},{48,16},{64,32},{80,48},{96,64},{112,80},{1... | collective-permute-start | bytes 98312 | tf_op jit(solution)/shard_map/ppermute | solution.py:88
  39.0 9.0 %collective-permute-start.3 = (f32[2,256,16]{1,2,0:T(8,128)S(1)}, f32[2,256,16]{1,2,0:T(8,128)S(1)}, u32[]{:S(2)}, u32[]{:S(2)}) collective-permute-start(f32[2,256,16]{1,2,0:T(8,128)S(1)} %collective-permute-done.1), channel_id=1, source_target_pairs={{0,32},{16,48},{32,64},{48,80},{64,96},{80,112},{96,0},{112,16},{1... | collective-permute-start | bytes 98312 | tf_op jit(solution)/shard_map/ppermute | solution.py:89
  48.0 7.0 %collective-permute-start.4 = (f32[8,256,16]{1,2,0:T(8,128)S(1)}, f32[8,256,16]{1,2,0:T(8,128)S(1)}, u32[]{:S(2)}, u32[]{:S(2)}) collective-permute-start(f32[8,256,16]{1,2,0:T(8,128)S(1)} %get-tuple-element.10), channel_id=1, source_target_pairs={{0,128},{16,144},{32,160},{48,176},{64,192},{80,208},{96,224},{112... | collective-permute-start | bytes 393224 | tf_op jit(solution)/shard_map/ppermute | solution.py:87
  51.2 6.0 %collective-permute-start.5 = (f32[8,256,16]{1,2,0:T(8,128)S(1)}, f32[8,256,16]{1,2,0:T(8,128)S(1)}, u32[]{:S(2)}, u32[]{:S(2)}) collective-permute-start(f32[8,256,16]{1,2,0:T(8,128)S(1)} %get-tuple-element.10), channel_id=1, source_target_pairs={{0,384},{16,400},{32,416},{48,432},{64,448},{80,464},{96,480},{112... | collective-permute-start | bytes 393224 | tf_op jit(solution)/shard_map/ppermute | solution.py:88
  55.0 6.9 %collective-permute-start.6 = (f32[8,256,16]{1,2,0:T(8,128)S(1)}, f32[8,256,16]{1,2,0:T(8,128)S(1)}, u32[]{:S(2)}, u32[]{:S(2)}) collective-permute-start(f32[8,256,16]{1,2,0:T(8,128)S(1)} %collective-permute-done.4), channel_id=1, source_target_pairs={{0,128},{16,144},{32,160},{48,176},{64,192},{80,208},{96,224},{112... | collective-permute-start | bytes 393224 | tf_op jit(solution)/shard_map/ppermute | solution.py:89
  66.0 14.6 %copy-start.19 = (s32[4]{0:T(128)S(1)}, s32[4]{0:T(128)}, u32[]{:S(2)}) copy-start(s32[4]{0:T(128)} %constant.257.clone) | copy-start | bytes 52
  66.0 15.4 %copy-start.6 = (bf16[128,4096]{1,0:T(8,128)(2,1)S(1)}, bf16[128,4096]{1,0:T(8,128)(2,1)}, u32[]{:S(2)}) copy-start(bf16[128,4096]{1,0:T(8,128)(2,1)} %param.13) | copy-start | bytes 3145732
  66.0 64.4 %all-to-all-start.1 = ((bf16[16,128,512]{1,2,0:T(8,128)(2,1)}), bf16[16,128,512]{1,2,0:T(8,128)(2,1)}, u32[]{:S(2)}, u32[]{:S(2)}) async-start(bf16[16,128,512]{1,2,0:T(8,128)(2,1)} %bitcast.157), calls=%async_computation.1 | async-start | bytes 4194304 | tf_op jit(solution)/shard_map/all_to_all | solution.py:145
  80.6 1.1 copy-start.16
  80.6 1.1 copy-start.18
  134.1 3.0 copy-start
  139.1 1.2 copy-start.7
  140.3 10.2 %copy-start.20 = (s32[16,1]{0,1:T(1,128)S(1)}, s32[16,1]{0,1:T(1,128)}, u32[]{:S(2)}) copy-start(s32[16,1]{0,1:T(1,128)} %add.435) | copy-start | bytes 196
  140.3 10.8 %copy-start.3 = (f32[32,256,16]{1,2,0:T(8,128)S(1)}, f32[32,256,16]{1,2,0:T(8,128)}, u32[]{:S(2)}) copy-start(f32[32,256,16]{1,2,0:T(8,128)} %get-tuple-element.9) | copy-start | bytes 1572868
  140.8 7.7 %collective-permute-start.7 = (bf16[128,512]{0,1:T(8,128)(2,1)S(1)}, bf16[128,512]{0,1:T(8,128)(2,1)S(1)}, u32[]{:S(2)}, u32[]{:S(2)}) collective-permute-start(bf16[128,512]{0,1:T(8,128)(2,1)S(1)} %bitcast.174), channel_id=1, source_target_pairs={{0,1},{1,2},{2,3},{3,0},{4,5},{5,6},{6,7},{7,4},{8,9},{9,10},{10,1... | collective-permute-start | bytes 393224 | tf_op jit(solution)/shard_map/ppermute | solution.py:54
  143.4 9.5 %collective-permute-start.8 = (bf16[128,512]{0,1:T(8,128)(2,1)S(1)}, bf16[128,512]{0,1:T(8,128)(2,1)S(1)}, u32[]{:S(2)}, u32[]{:S(2)}) collective-permute-start(bf16[128,512]{0,1:T(8,128)(2,1)S(1)} %bitcast.175), channel_id=1, source_target_pairs={{0,3},{1,0},{2,1},{3,2},{4,7},{5,4},{6,5},{7,6},{8,11},{9,8},{10,9... | collective-permute-start | bytes 393224 | tf_op jit(solution)/shard_map/ppermute | solution.py:55
  148.5 7.6 %collective-permute-start.9 = (bf16[128,512]{0,1:T(8,128)(2,1)S(1)}, bf16[128,512]{0,1:T(8,128)(2,1)}, u32[]{:S(2)}, u32[]{:S(2)}) collective-permute-start(bf16[128,512]{0,1:T(8,128)(2,1)S(1)} %collective-permute-done.7), channel_id=1, source_target_pairs={{0,1},{1,2},{2,3},{3,0},{4,5},{5,6},{6,7},{7,4},{8,9},{9,10},{10,1... | collective-permute-start | bytes 393224 | tf_op jit(solution)/shard_map/ppermute | solution.py:56
  157.1 12.5 %collective-permute-start.10 = (bf16[512,512]{0,1:T(8,128)(2,1)S(1)}, bf16[512,512]{0,1:T(8,128)(2,1)S(1)}, u32[]{:S(2)}, u32[]{:S(2)}) collective-permute-start(bf16[512,512]{0,1:T(8,128)(2,1)S(1)} %pad_maximum_fusion), channel_id=1, source_target_pairs={{0,4},{1,5},{2,6},{3,7},{4,8},{5,9},{6,10},{7,11},{8,12},{9,13},{1... | collective-permute-start | bytes 1572872 | tf_op jit(solution)/shard_map/ppermute | solution.py:54
  160.2 21.0 %copy-start.4 = (bf16[2048,256]{1,0:T(8,128)(2,1)}, bf16[2048,256]{1,0:T(8,128)(2,1)S(1)}, u32[]{:S(2)}) copy-start(bf16[2048,256]{1,0:T(8,128)(2,1)S(1)} %bitcast_select_fusion.2) | copy-start | bytes 3145732
  160.2 12.4 %collective-permute-start.11 = (bf16[512,512]{0,1:T(8,128)(2,1)S(1)}, bf16[512,512]{0,1:T(8,128)(2,1)S(1)}, u32[]{:S(2)}, u32[]{:S(2)}) collective-permute-start(bf16[512,512]{0,1:T(8,128)(2,1)S(1)} %pad_maximum_fusion), channel_id=1, source_target_pairs={{0,12},{1,13},{2,14},{3,15},{4,0},{5,1},{6,2},{7,3},{8,4},{9,5},{1... | collective-permute-start | bytes 1572872 | tf_op jit(solution)/shard_map/ppermute | solution.py:55
  169.6 11.6 %collective-permute-start.12 = (bf16[512,512]{0,1:T(8,128)(2,1)S(1)}, bf16[512,512]{0,1:T(8,128)(2,1)S(1)}, u32[]{:S(2)}, u32[]{:S(2)}) collective-permute-start(bf16[512,512]{0,1:T(8,128)(2,1)S(1)} %collective-permute-done.10), channel_id=1, source_target_pairs={{0,4},{1,5},{2,6},{3,7},{4,8},{5,9},{6,10},{7,11},{8,12},{9,13},{1... | collective-permute-start | bytes 1572872 | tf_op jit(solution)/shard_map/ppermute | solution.py:56
  181.2 1.6 copy-start.1
  181.2 1.6 copy-start.9
  181.2 1.6 copy-start.11
  182.0 0.8 copy-start.13
  246.2 1.2 copy-start.8
  247.9 7.7 %collective-permute-start.13 = (bf16[128,512]{0,1:T(8,128)(2,1)S(1)}, bf16[128,512]{0,1:T(8,128)(2,1)S(1)}, u32[]{:S(2)}, u32[]{:S(2)}) collective-permute-start(bf16[128,512]{0,1:T(8,128)(2,1)S(1)} %bitcast.178), channel_id=1, source_target_pairs={{0,1},{1,2},{2,3},{3,0},{4,5},{5,6},{6,7},{7,4},{8,9},{9,10},{10,1... | collective-permute-start | bytes 393224 | tf_op jit(solution)/shard_map/ppermute | solution.py:54
  249.8 7.7 %collective-permute-start.14 = (bf16[128,512]{0,1:T(8,128)(2,1)S(1)}, bf16[128,512]{0,1:T(8,128)(2,1)S(1)}, u32[]{:S(2)}, u32[]{:S(2)}) collective-permute-start(bf16[128,512]{0,1:T(8,128)(2,1)S(1)} %bitcast.179), channel_id=1, source_target_pairs={{0,3},{1,0},{2,1},{3,2},{4,7},{5,4},{6,5},{7,6},{8,11},{9,8},{10,9... | collective-permute-start | bytes 393224 | tf_op jit(solution)/shard_map/ppermute | solution.py:55
  255.6 7.5 %collective-permute-start.15 = (bf16[128,512]{0,1:T(8,128)(2,1)S(1)}, bf16[128,512]{0,1:T(8,128)(2,1)S(1)}, u32[]{:S(2)}, u32[]{:S(2)}) collective-permute-start(bf16[128,512]{0,1:T(8,128)(2,1)S(1)} %collective-permute-done.13), channel_id=1, source_target_pairs={{0,1},{1,2},{2,3},{3,0},{4,5},{5,6},{6,7},{7,4},{8,9},{9,10},{10,1... | collective-permute-start | bytes 393224 | tf_op jit(solution)/shard_map/ppermute | solution.py:56
  263.2 11.5 %collective-permute-start.16 = (bf16[512,512]{0,1:T(8,128)(2,1)S(1)}, bf16[512,512]{0,1:T(8,128)(2,1)S(1)}, u32[]{:S(2)}, u32[]{:S(2)}) collective-permute-start(bf16[512,512]{0,1:T(8,128)(2,1)S(1)} %pad_maximum_fusion.1), channel_id=1, source_target_pairs={{0,4},{1,5},{2,6},{3,7},{4,8},{5,9},{6,10},{7,11},{8,12},{9,13},{1... | collective-permute-start | bytes 1572872 | tf_op jit(solution)/shard_map/ppermute | solution.py:54
  265.9 20.0 %copy-start.2 = (f32[256,512]{1,0:T(8,128)S(1)}, f32[256,512]{1,0:T(8,128)}, u32[]{:S(2)}) copy-start(f32[256,512]{1,0:T(8,128)} %copy.69) | copy-start | bytes 1572868
  265.9 20.0 %copy-start.5 = (bf16[2048,256]{1,0:T(8,128)(2,1)S(1)}, bf16[2048,256]{1,0:T(8,128)(2,1)}, u32[]{:S(2)}) copy-start(bf16[2048,256]{1,0:T(8,128)(2,1)} %copy-done.4) | copy-start | bytes 3145732
  265.9 20.0 %copy-start.10 = (f32[1,256,512]{2,1,0:T(8,128)S(1)}, f32[1,256,512]{2,1,0:T(8,128)}, u32[]{:S(2)}) copy-start(f32[1,256,512]{2,1,0:T(8,128)} %param.17) | copy-start | bytes 1572868
  265.9 20.0 %copy-start.12 = (f32[1,256,512]{2,1,0:T(8,128)S(1)}, f32[1,256,512]{2,1,0:T(8,128)}, u32[]{:S(2)}) copy-start(f32[1,256,512]{2,1,0:T(8,128)} %param.18) | copy-start | bytes 1572868
  265.9 20.0 %copy-start.14 = (f32[256,512]{1,0:T(8,128)S(1)}, f32[256,512]{1,0:T(8,128)}, u32[]{:S(2)}) copy-start(f32[256,512]{1,0:T(8,128)} %copy-done.13) | copy-start | bytes 1572868
  265.9 10.9 %collective-permute-start.17 = (bf16[512,512]{0,1:T(8,128)(2,1)S(1)}, bf16[512,512]{0,1:T(8,128)(2,1)S(1)}, u32[]{:S(2)}, u32[]{:S(2)}) collective-permute-start(bf16[512,512]{0,1:T(8,128)(2,1)S(1)} %pad_maximum_fusion.1), channel_id=1, source_target_pairs={{0,12},{1,13},{2,14},{3,15},{4,0},{5,1},{6,2},{7,3},{8,4},{9,5},{1... | collective-permute-start | bytes 1572872 | tf_op jit(solution)/shard_map/ppermute | solution.py:55
  274.7 11.1 %collective-permute-start.18 = (bf16[512,512]{0,1:T(8,128)(2,1)S(1)}, bf16[512,512]{0,1:T(8,128)(2,1)S(1)}, u32[]{:S(2)}, u32[]{:S(2)}) collective-permute-start(bf16[512,512]{0,1:T(8,128)(2,1)S(1)} %collective-permute-done.16), channel_id=1, source_target_pairs={{0,4},{1,5},{2,6},{3,7},{4,8},{5,9},{6,10},{7,11},{8,12},{9,13},{1... | collective-permute-start | bytes 1572872 | tf_op jit(solution)/shard_map/ppermute | solution.py:56
  287.5 39.6 %copy-start.17 = (f32[256,16]{0,1:T(8,128)S(1)}, f32[256,16]{0,1:T(8,128)}, u32[]{:S(2)}) copy-start(f32[256,16]{0,1:T(8,128)} %param.20) | copy-start | bytes 49156

commit v8 on v7

--- a/solution.py
+++ b/solution.py
@@ -138,6 +138,7 @@
     ring_rows = jnp.take(
         feature_rows.reshape(members, rows, block), order, axis=0
     ).reshape(group_rows, block)
+    feature_rows, attention = lax.optimization_barrier((feature_rows, attention))
     for inner_step in range(2):
         partial = jnp.dot(
             feature_rows, master.astype(jnp.bfloat16), preferred_element_type=jnp.float32

time: 329 us -> 326 us (level)
    all_to_all x1, waiting for transfers between devices: 42.8 us -> 47.8 us  [on_device(): lax.all_to_all(partial.reshape(members, rows, width), 'fsdp', split_axis=...]
    ppermute x2, waiting for transfers between devices: 10.2 us -> 6.4 us  [island_gather(): moved[-1] = lax.ppermute(moved[0], 'island', shift(axis, 1))]
    unnamed x64 -> x58, local copies, waits for them, and re-layouts: 6.62 us -> 7.34 us
  transfers between devices with their start and end apart: 21 -> 21, of which waited for: 13 -> 12; matrix products, arithmetic and copies ran while one was open for 5% -> 4% of each run, Pallas kernels for 0% -> 0%
where the time goes in v8:
time: 326 us; the launch traced here: 325 us
  waiting for transfers between devices  101 us (31%)
  blocking collectives  93.1 us (29%)
  starting transfers between devices  84.4 us (26%)
  local copies, waits for them, and re-layouts  19.4 us (6%)
  matrix products  12 us (4%)
  other arithmetic  11.9 us (4%)
    all_to_all x1, blocking collectives, on_device(): lax.all_to_all(partial.reshape(members, rows, width), 'fsdp', split_axis=...  56.4 us
    all_to_all x1, waiting for transfers between devices, on_device(): lax.all_to_all(partial.reshape(members, rows, width), 'fsdp', split_axis=...  47.8 us
    all_to_all x1, blocking collectives, on_device(): lax.all_to_all(sent.reshape(block + 2, groups, cols), 'island', split_axi...  36.7 us
    ppermute x4, waiting for transfers between devices, along(): far = lax.ppermute(up, 'fsdp', _shift(cols, rows, dx, dz))  26.3 us
    ppermute x4, starting transfers between devices, along(): down = lax.ppermute(part, 'fsdp', _shift(cols, rows, -dx, -dz))  19.7 us
    all_to_all x1, starting transfers between devices, on_device(): lax.all_to_all(partial.reshape(members, rows, width), 'fsdp', split_axis=...  15.3 us
    ppermute x2, waiting for transfers between devices, island_gather(): moved[-2] = lax.ppermute(moved[-1], 'island', shift(axis, 1))  11.5 us
    ppermute x2, starting transfers between devices, island_gather(): moved[-1] = lax.ppermute(moved[0], 'island', shift(axis, 1))  11.5 us
  transfers between devices with their start and end apart: 21, of which 12 were waited for; matrix products, arithmetic and copies ran while one was open for 4% of the time, Pallas kernels for 0%

profile of v8, /device:TPU:1, one launch (start us, length us, event | category | flops | bytes accessed | tf_op | source)
XLA Modules:
  0.0 324.6 jit_solution(15674418067396945167)
XLA Ops:
  0.6 1.6 copy.55
  2.3 1.3 copy.56
  3.6 9.1 %all-to-all-start = ((bf16[128,16,256]{2,0,1:T(8,128)(2,1)}), bf16[128,16,256]{2,0,1:T(8,128)(2,1)S(1)}, u32[]{:S(2)}, u32[]{:S(2)}) async-start(bf16[128,16,256]{2,0,1:T(8,128)(2,1)} %copy.56), calls=%async_computation | async-start | bytes 2097152 | tf_op jit(solution)/shard_map/all_to_all | solution.py:130
  12.8 3.4 %collective-permute-start = (f32[1,256,16]{1,2,0:T(8,128)S(1)}, f32[1,256,16]{1,2,0:T(8,128)S(1)}, u32[]{:S(2)}, u32[]{:S(2)}) collective-permute-start(f32[1,256,16]{1,2,0:T(8,128)S(1)} %bitcast.170), channel_id=1, source_target_pairs={{0,16},{16,0},{32,48},{48,32},{64,80},{80,64},{96,112},{112,96},{1... | collective-permute-start | bytes 49160 | tf_op jit(solution)/shard_map/ppermute | solution.py:92
  16.4 1.2 copy.83
  17.8 1.6 sort.17
  19.5 2.3 divide_convert_fusion
  21.8 8.3 %collective-permute-start.1 = (f32[2,256,16]{1,2,0:T(8,128)S(1)}, f32[2,256,16]{1,2,0:T(8,128)S(1)}, u32[]{:S(2)}, u32[]{:S(2)}) collective-permute-start(f32[2,256,16]{1,2,0:T(8,128)S(1)} %pad_maximum_fusion.2), channel_id=1, source_target_pairs={{0,32},{16,48},{32,64},{48,80},{64,96},{80,112},{96,0},{112,16},{1... | collective-permute-start | bytes 98312 | tf_op jit(solution)/shard_map/ppermute | solution.py:87
  30.1 2.9 collective-permute-start.2
  33.0 6.0 %collective-permute-done.1 = f32[2,256,16]{1,2,0:T(8,128)S(1)} collective-permute-done((f32[2,256,16]{1,2,0:T(8,128)S(1)}, f32[2,256,16]{1,2,0:T(8,128)S(1)}, u32[]{:S(2)}, u32[]{:S(2)}) %collective-permute-start.1) | collective-permute-done | bytes 32800 | tf_op jit(solution)/shard_map/ppermute | solution.py:87
  39.0 1.9 collective-permute-start.3
  40.9 6.6 %collective-permute-done.3 = f32[2,256,16]{1,2,0:T(8,128)S(1)} collective-permute-done((f32[2,256,16]{1,2,0:T(8,128)S(1)}, f32[2,256,16]{1,2,0:T(8,128)S(1)}, u32[]{:S(2)}, u32[]{:S(2)}) %collective-permute-start.3) | collective-permute-done | bytes 32800 | tf_op jit(solution)/shard_map/ppermute | solution.py:89
  47.5 3.2 collective-permute-start.4
  50.8 3.4 %collective-permute-start.5 = (f32[8,256,16]{1,2,0:T(8,128)S(1)}, f32[8,256,16]{1,2,0:T(8,128)S(1)}, u32[]{:S(2)}, u32[]{:S(2)}) collective-permute-start(f32[8,256,16]{1,2,0:T(8,128)S(1)} %get-tuple-element.12), channel_id=1, source_target_pairs={{0,384},{16,400},{32,416},{48,432},{64,448},{80,464},{96,480},{112... | collective-permute-start | bytes 393224 | tf_op jit(solution)/shard_map/ppermute | solution.py:88
  54.5 1.9 collective-permute-start.6
  56.5 4.9 %collective-permute-done.6 = f32[8,256,16]{1,2,0:T(8,128)S(1)} collective-permute-done((f32[8,256,16]{1,2,0:T(8,128)S(1)}, f32[8,256,16]{1,2,0:T(8,128)S(1)}, u32[]{:S(2)}, u32[]{:S(2)}) %collective-permute-start.6) | collective-permute-done | bytes 131104 | tf_op jit(solution)/shard_map/ppermute | solution.py:89
  61.4 0.6 gather_fusion
  62.2 2.0 convolution_convert_fusion.1
  64.2 15.3 %all-to-all-start.1 = ((bf16[16,128,512]{2,1,0:T(8,128)(2,1)}), bf16[16,128,512]{2,1,0:T(8,128)(2,1)}, u32[]{:S(2)}, u32[]{:S(2)}) async-start(bf16[16,128,512]{2,1,0:T(8,128)(2,1)} %bitcast.149), calls=%async_computation.1 | async-start | bytes 4194304 | tf_op jit(solution)/shard_map/all_to_all | solution.py:146
  79.8 1.7 copy.62
  81.5 47.8 %all-to-all-done.1 = bf16[16,128,512]{2,1,0:T(8,128)(2,1)} async-done(((bf16[16,128,512]{2,1,0:T(8,128)(2,1)}), bf16[16,128,512]{2,1,0:T(8,128)(2,1)}, u32[]{:S(2)}, u32[]{:S(2)}) %all-to-all-start.1) | async-done | bytes 2097184 | tf_op jit(solution)/shard_map/all_to_all | solution.py:146
  129.4 1.9 convert_reduce_fusion.1
  131.4 1.8 fusion.66
  133.2 2.9 copy.61
  136.1 2.2 fusion.12
  138.6 1.0 copy-done.5
  139.5 0.5 fusion.9
  140.0 1.9 collective-permute-start.7
  141.9 0.7 broadcast_bitcast_fusion
  142.6 5.1 %collective-permute-start.8 = (bf16[128,512]{0,1:T(8,128)(2,1)S(1)}, bf16[128,512]{0,1:T(8,128)(2,1)S(1)}, u32[]{:S(2)}, u32[]{:S(2)}) collective-permute-start(bf16[128,512]{0,1:T(8,128)(2,1)S(1)} %bitcast.163), channel_id=1, source_target_pairs={{0,3},{1,0},{2,1},{3,2},{4,7},{5,4},{6,5},{7,6},{8,11},{9,8},{10,9... | collective-permute-start | bytes 393224 | tf_op jit(solution)/shard_map/ppermute | solution.py:55
  147.8 1.9 collective-permute-start.9
  149.7 0.6 pad_clamp_fusion
  150.3 1.0 copy.69
  151.3 0.7 gather_fusion.1
  152.0 3.3 %collective-permute-done.9 = bf16[128,512]{0,1:T(8,128)(2,1)} collective-permute-done((bf16[128,512]{0,1:T(8,128)(2,1)S(1)}, bf16[128,512]{0,1:T(8,128)(2,1)}, u32[]{:S(2)}, u32[]{:S(2)}) %collective-permute-start.9) | collective-permute-done | bytes 131104 | tf_op jit(solution)/shard_map/ppermute | solution.py:56
  155.4 1.0 pad_maximum_fusion
  156.3 1.9 collective-permute-start.10
  158.3 1.1 bitcast_select_fusion.2
  159.4 4.6 %collective-permute-start.11 = (bf16[512,512]{0,1:T(8,128)(2,1)S(1)}, bf16[512,512]{0,1:T(8,128)(2,1)S(1)}, u32[]{:S(2)}, u32[]{:S(2)}) collective-permute-start(bf16[512,512]{0,1:T(8,128)(2,1)S(1)} %pad_maximum_fusion), channel_id=1, source_target_pairs={{0,12},{1,13},{2,14},{3,15},{4,0},{5,1},{6,2},{7,3},{8,4},{9,5},{1... | collective-permute-start | bytes 1572872 | tf_op jit(solution)/shard_map/ppermute | solution.py:55
  164.0 4.8 %collective-permute-done.10 = bf16[512,512]{0,1:T(8,128)(2,1)S(1)} collective-permute-done((bf16[512,512]{0,1:T(8,128)(2,1)S(1)}, bf16[512,512]{0,1:T(8,128)(2,1)S(1)}, u32[]{:S(2)}, u32[]{:S(2)}) %collective-permute-start.10) | collective-permute-done | bytes 524320 | tf_op jit(solution)/shard_map/ppermute | solution.py:54
  168.8 1.9 collective-permute-start.12
  170.8 0.9 constant_dynamic-update-slice_fusion.16
  171.9 8.5 %collective-permute-done.12 = bf16[512,512]{0,1:T(8,128)(2,1)S(1)} collective-permute-done((bf16[512,512]{0,1:T(8,128)(2,1)S(1)}, bf16[512,512]{0,1:T(8,128)(2,1)S(1)}, u32[]{:S(2)}, u32[]{:S(2)}) %collective-permute-start.12) | collective-permute-done | bytes 524320 | tf_op jit(solution)/shard_map/ppermute | solution.py:56
  180.5 0.8 fusion.67
  181.8 1.0 convolution_convert_fusion
  182.9 56.4 %all_to_all.38 = bf16[16,128,512]{2,1,0:T(8,128)(2,1)S(1)} all-to-all(bf16[16,128,512]{2,1,0:T(8,128)(2,1)S(1)} %bitcast.148), channel_id=1, replica_groups=mesh['island'=32,'fsdp'=16] {'fsdp'}, dimensions={0} | all-to-all | bytes 4194304 | tf_op jit(solution)/shard_map/all_to_all | solution.py:146
  239.7 1.8 fusion.68
  241.5 1.9 copy.67
  243.4 1.5 fusion.11
  245.2 1.0 copy-done.6
  246.2 0.5 fusion.10
  246.7 1.9 collective-permute-start.13
  248.6 5.2 %collective-permute-start.14 = (bf16[128,512]{0,1:T(8,128)(2,1)S(1)}, bf16[128,512]{0,1:T(8,128)(2,1)S(1)}, u32[]{:S(2)}, u32[]{:S(2)}) collective-permute-start(bf16[128,512]{0,1:T(8,128)(2,1)S(1)} %bitcast.167), channel_id=1, source_target_pairs={{0,3},{1,0},{2,1},{3,2},{4,7},{5,4},{6,5},{7,6},{8,11},{9,8},{10,9... | collective-permute-start | bytes 393224 | tf_op jit(solution)/shard_map/ppermute | solution.py:55
  253.8 0.6 collective-permute-done.13
  254.4 1.9 collective-permute-start.15
  256.3 5.6 %collective-permute-done.15 = bf16[128,512]{0,1:T(8,128)(2,1)S(1)} collective-permute-done((bf16[128,512]{0,1:T(8,128)(2,1)S(1)}, bf16[128,512]{0,1:T(8,128)(2,1)S(1)}, u32[]{:S(2)}, u32[]{:S(2)}) %collective-permute-start.15) | collective-permute-done | bytes 131104 | tf_op jit(solution)/shard_map/ppermute | solution.py:56
  262.0 1.9 collective-permute-start.16
  264.7 4.8 %collective-permute-start.17 = (bf16[512,512]{0,1:T(8,128)(2,1)S(1)}, bf16[512,512]{0,1:T(8,128)(2,1)S(1)}, u32[]{:S(2)}, u32[]{:S(2)}) collective-permute-start(bf16[512,512]{0,1:T(8,128)(2,1)S(1)} %pad_maximum_fusion.1), channel_id=1, source_target_pairs={{0,12},{1,13},{2,14},{3,15},{4,0},{5,1},{6,2},{7,3},{8,4},{9,5},{1... | collective-permute-start | bytes 1572872 | tf_op jit(solution)/shard_map/ppermute | solution.py:55
  269.6 3.9 %collective-permute-done.16 = bf16[512,512]{0,1:T(8,128)(2,1)S(1)} collective-permute-done((bf16[512,512]{0,1:T(8,128)(2,1)S(1)}, bf16[512,512]{0,1:T(8,128)(2,1)S(1)}, u32[]{:S(2)}, u32[]{:S(2)}) %collective-permute-start.16) | collective-permute-done | bytes 524320 | tf_op jit(solution)/shard_map/ppermute | solution.py:54
  273.5 1.9 collective-permute-start.18
  275.7 8.9 %collective-permute-done.18 = bf16[512,512]{0,1:T(8,128)(2,1)S(1)} collective-permute-done((bf16[512,512]{0,1:T(8,128)(2,1)S(1)}, bf16[512,512]{0,1:T(8,128)(2,1)S(1)}, u32[]{:S(2)}, u32[]{:S(2)}) %collective-permute-start.18) | collective-permute-done | bytes 524320 | tf_op jit(solution)/shard_map/ppermute | solution.py:56
  284.7 1.4 fusion.28
  286.5 36.7 %all_to_all.39 = bf16[258,32,16]{0,2,1:T(8,128)(2,1)S(1)} all-to-all(bf16[258,32,16]{0,2,1:T(8,128)(2,1)S(1)} %bitcast.155), channel_id=1, replica_groups=mesh['island'=32,'fsdp'=16] {'island'}, dimensions={1} | all-to-all | bytes 528384 | tf_op jit(solution)/shard_map/all_to_all | solution.py:189
  323.9 0.7 multiply_subtract_fusion.1
  (96 shorter events, 4.6 us)
Async XLA Ops:
  2.3 10.5 %copy-start.13 = (f32[256,16]{0,1:T(8,128)S(1)}, f32[256,16]{0,1:T(8,128)}, u32[]{:S(2)}) copy-start(f32[256,16]{0,1:T(8,128)} %param.19) | copy-start | bytes 49156
  2.3 14.1 %copy-start.4 = (bf16[128,4096]{1,0:T(8,128)(2,1)S(1)}, bf16[128,4096]{1,0:T(8,128)(2,1)}, u32[]{:S(2)}) copy-start(bf16[128,4096]{1,0:T(8,128)(2,1)} %param.13) | copy-start | bytes 3145732
  3.6 14.0 %copy-start.14 = (bf16[128,512]{1,0:T(8,128)(2,1)S(1)}, bf16[128,512]{1,0:T(8,128)(2,1)}, u32[]{:S(2)}) copy-start(bf16[128,512]{1,0:T(8,128)(2,1)} %param.14) | copy-start | bytes 393220
  3.6 15.8 %copy-start.16 = (s32[1,128]{1,0:T(1,128)S(1)}, s32[1,128]{1,0:T(1,128)}, u32[]{:S(2)}) copy-start(s32[1,128]{1,0:T(1,128)} %param.16) | copy-start | bytes 1540
  3.6 58.6 %all-to-all-start = ((bf16[128,16,256]{2,0,1:T(8,128)(2,1)}), bf16[128,16,256]{2,0,1:T(8,128)(2,1)S(1)}, u32[]{:S(2)}, u32[]{:S(2)}) async-start(bf16[128,16,256]{2,0,1:T(8,128)(2,1)} %copy.56), calls=%async_computation | async-start | bytes 2097152 | tf_op jit(solution)/shard_map/all_to_all | solution.py:130
  12.8 9.0 %collective-permute-start = (f32[1,256,16]{1,2,0:T(8,128)S(1)}, f32[1,256,16]{1,2,0:T(8,128)S(1)}, u32[]{:S(2)}, u32[]{:S(2)}) collective-permute-start(f32[1,256,16]{1,2,0:T(8,128)S(1)} %bitcast.170), channel_id=1, source_target_pairs={{0,16},{16,0},{32,48},{48,32},{64,80},{80,64},{96,112},{112,96},{1... | collective-permute-start | bytes 49160 | tf_op jit(solution)/shard_map/ppermute | solution.py:92
  21.8 17.2 %collective-permute-start.1 = (f32[2,256,16]{1,2,0:T(8,128)S(1)}, f32[2,256,16]{1,2,0:T(8,128)S(1)}, u32[]{:S(2)}, u32[]{:S(2)}) collective-permute-start(f32[2,256,16]{1,2,0:T(8,128)S(1)} %pad_maximum_fusion.2), channel_id=1, source_target_pairs={{0,32},{16,48},{32,64},{48,80},{64,96},{80,112},{96,0},{112,16},{1... | collective-permute-start | bytes 98312 | tf_op jit(solution)/shard_map/ppermute | solution.py:87
  30.1 10.8 %collective-permute-start.2 = (f32[2,256,16]{1,2,0:T(8,128)S(1)}, f32[2,256,16]{1,2,0:T(8,128)S(1)}, u32[]{:S(2)}, u32[]{:S(2)}) collective-permute-start(f32[2,256,16]{1,2,0:T(8,128)S(1)} %pad_maximum_fusion.2), channel_id=1, source_target_pairs={{0,96},{16,112},{32,0},{48,16},{64,32},{80,48},{96,64},{112,80},{1... | collective-permute-start | bytes 98312 | tf_op jit(solution)/shard_map/ppermute | solution.py:88
  39.0 8.6 %collective-permute-start.3 = (f32[2,256,16]{1,2,0:T(8,128)S(1)}, f32[2,256,16]{1,2,0:T(8,128)S(1)}, u32[]{:S(2)}, u32[]{:S(2)}) collective-permute-start(f32[2,256,16]{1,2,0:T(8,128)S(1)} %collective-permute-done.1), channel_id=1, source_target_pairs={{0,32},{16,48},{32,64},{48,80},{64,96},{80,112},{96,0},{112,16},{1... | collective-permute-start | bytes 98312 | tf_op jit(solution)/shard_map/ppermute | solution.py:89
  47.5 7.0 %collective-permute-start.4 = (f32[8,256,16]{1,2,0:T(8,128)S(1)}, f32[8,256,16]{1,2,0:T(8,128)S(1)}, u32[]{:S(2)}, u32[]{:S(2)}) collective-permute-start(f32[8,256,16]{1,2,0:T(8,128)S(1)} %get-tuple-element.12), channel_id=1, source_target_pairs={{0,128},{16,144},{32,160},{48,176},{64,192},{80,208},{96,224},{112... | collective-permute-start | bytes 393224 | tf_op jit(solution)/shard_map/ppermute | solution.py:87
  50.8 5.7 %collective-permute-start.5 = (f32[8,256,16]{1,2,0:T(8,128)S(1)}, f32[8,256,16]{1,2,0:T(8,128)S(1)}, u32[]{:S(2)}, u32[]{:S(2)}) collective-permute-start(f32[8,256,16]{1,2,0:T(8,128)S(1)} %get-tuple-element.12), channel_id=1, source_target_pairs={{0,384},{16,400},{32,416},{48,432},{64,448},{80,464},{96,480},{112... | collective-permute-start | bytes 393224 | tf_op jit(solution)/shard_map/ppermute | solution.py:88
  54.5 6.9 %collective-permute-start.6 = (f32[8,256,16]{1,2,0:T(8,128)S(1)}, f32[8,256,16]{1,2,0:T(8,128)S(1)}, u32[]{:S(2)}, u32[]{:S(2)}) collective-permute-start(f32[8,256,16]{1,2,0:T(8,128)S(1)} %collective-permute-done.4), channel_id=1, source_target_pairs={{0,128},{16,144},{32,160},{48,176},{64,192},{80,208},{96,224},{112... | collective-permute-start | bytes 393224 | tf_op jit(solution)/shard_map/ppermute | solution.py:89
  64.2 15.4 %copy-start.17 = (s32[4]{0:T(128)S(1)}, s32[4]{0:T(128)}, u32[]{:S(2)}) copy-start(s32[4]{0:T(128)} %constant.257.clone) | copy-start | bytes 52
  64.2 65.2 %all-to-all-start.1 = ((bf16[16,128,512]{2,1,0:T(8,128)(2,1)}), bf16[16,128,512]{2,1,0:T(8,128)(2,1)}, u32[]{:S(2)}, u32[]{:S(2)}) async-start(bf16[16,128,512]{2,1,0:T(8,128)(2,1)} %bitcast.149), calls=%async_computation.1 | async-start | bytes 4194304 | tf_op jit(solution)/shard_map/all_to_all | solution.py:146
  138.3 1.2 copy-start.5
  140.0 7.7 %collective-permute-start.7 = (bf16[128,512]{0,1:T(8,128)(2,1)S(1)}, bf16[128,512]{0,1:T(8,128)(2,1)S(1)}, u32[]{:S(2)}, u32[]{:S(2)}) collective-permute-start(bf16[128,512]{0,1:T(8,128)(2,1)S(1)} %bitcast.162), channel_id=1, source_target_pairs={{0,1},{1,2},{2,3},{3,0},{4,5},{5,6},{6,7},{7,4},{8,9},{9,10},{10,1... | collective-permute-start | bytes 393224 | tf_op jit(solution)/shard_map/ppermute | solution.py:54
  142.6 9.4 %collective-permute-start.8 = (bf16[128,512]{0,1:T(8,128)(2,1)S(1)}, bf16[128,512]{0,1:T(8,128)(2,1)S(1)}, u32[]{:S(2)}, u32[]{:S(2)}) collective-permute-start(bf16[128,512]{0,1:T(8,128)(2,1)S(1)} %bitcast.163), channel_id=1, source_target_pairs={{0,3},{1,0},{2,1},{3,2},{4,7},{5,4},{6,5},{7,6},{8,11},{9,8},{10,9... | collective-permute-start | bytes 393224 | tf_op jit(solution)/shard_map/ppermute | solution.py:55
  147.8 7.6 %collective-permute-start.9 = (bf16[128,512]{0,1:T(8,128)(2,1)S(1)}, bf16[128,512]{0,1:T(8,128)(2,1)}, u32[]{:S(2)}, u32[]{:S(2)}) collective-permute-start(bf16[128,512]{0,1:T(8,128)(2,1)S(1)} %collective-permute-done.7), channel_id=1, source_target_pairs={{0,1},{1,2},{2,3},{3,0},{4,5},{5,6},{6,7},{7,4},{8,9},{9,10},{10,1... | collective-permute-start | bytes 393224 | tf_op jit(solution)/shard_map/ppermute | solution.py:56
  156.3 12.5 %collective-permute-start.10 = (bf16[512,512]{0,1:T(8,128)(2,1)S(1)}, bf16[512,512]{0,1:T(8,128)(2,1)S(1)}, u32[]{:S(2)}, u32[]{:S(2)}) collective-permute-start(bf16[512,512]{0,1:T(8,128)(2,1)S(1)} %pad_maximum_fusion), channel_id=1, source_target_pairs={{0,4},{1,5},{2,6},{3,7},{4,8},{5,9},{6,10},{7,11},{8,12},{9,13},{1... | collective-permute-start | bytes 1572872 | tf_op jit(solution)/shard_map/ppermute | solution.py:54
  159.4 21.0 %copy-start.2 = (bf16[2048,256]{1,0:T(8,128)(2,1)}, bf16[2048,256]{1,0:T(8,128)(2,1)S(1)}, u32[]{:S(2)}) copy-start(bf16[2048,256]{1,0:T(8,128)(2,1)S(1)} %bitcast_select_fusion.2) | copy-start | bytes 3145732
  159.4 12.4 %collective-permute-start.11 = (bf16[512,512]{0,1:T(8,128)(2,1)S(1)}, bf16[512,512]{0,1:T(8,128)(2,1)S(1)}, u32[]{:S(2)}, u32[]{:S(2)}) collective-permute-start(bf16[512,512]{0,1:T(8,128)(2,1)S(1)} %pad_maximum_fusion), channel_id=1, source_target_pairs={{0,12},{1,13},{2,14},{3,15},{4,0},{5,1},{6,2},{7,3},{8,4},{9,5},{1... | collective-permute-start | bytes 1572872 | tf_op jit(solution)/shard_map/ppermute | solution.py:55
  168.8 11.6 %collective-permute-start.12 = (bf16[512,512]{0,1:T(8,128)(2,1)S(1)}, bf16[512,512]{0,1:T(8,128)(2,1)S(1)}, u32[]{:S(2)}, u32[]{:S(2)}) collective-permute-start(bf16[512,512]{0,1:T(8,128)(2,1)S(1)} %collective-permute-done.10), channel_id=1, source_target_pairs={{0,4},{1,5},{2,6},{3,7},{4,8},{5,9},{6,10},{7,11},{8,12},{9,13},{1... | collective-permute-start | bytes 1572872 | tf_op jit(solution)/shard_map/ppermute | solution.py:56
  180.5 1.0 copy-start
  180.5 1.2 copy-start.7
  180.5 1.3 copy-start.9
  181.8 1.1 copy-start.11
  245.0 1.2 copy-start.6
  246.7 7.7 %collective-permute-start.13 = (bf16[128,512]{0,1:T(8,128)(2,1)S(1)}, bf16[128,512]{0,1:T(8,128)(2,1)S(1)}, u32[]{:S(2)}, u32[]{:S(2)}) collective-permute-start(bf16[128,512]{0,1:T(8,128)(2,1)S(1)} %bitcast.166), channel_id=1, source_target_pairs={{0,1},{1,2},{2,3},{3,0},{4,5},{5,6},{6,7},{7,4},{8,9},{9,10},{10,1... | collective-permute-start | bytes 393224 | tf_op jit(solution)/shard_map/ppermute | solution.py:54
  248.6 7.7 %collective-permute-start.14 = (bf16[128,512]{0,1:T(8,128)(2,1)S(1)}, bf16[128,512]{0,1:T(8,128)(2,1)S(1)}, u32[]{:S(2)}, u32[]{:S(2)}) collective-permute-start(bf16[128,512]{0,1:T(8,128)(2,1)S(1)} %bitcast.167), channel_id=1, source_target_pairs={{0,3},{1,0},{2,1},{3,2},{4,7},{5,4},{6,5},{7,6},{8,11},{9,8},{10,9... | collective-permute-start | bytes 393224 | tf_op jit(solution)/shard_map/ppermute | solution.py:55
  254.4 7.5 %collective-permute-start.15 = (bf16[128,512]{0,1:T(8,128)(2,1)S(1)}, bf16[128,512]{0,1:T(8,128)(2,1)S(1)}, u32[]{:S(2)}, u32[]{:S(2)}) collective-permute-start(bf16[128,512]{0,1:T(8,128)(2,1)S(1)} %collective-permute-done.13), channel_id=1, source_target_pairs={{0,1},{1,2},{2,3},{3,0},{4,5},{5,6},{6,7},{7,4},{8,9},{9,10},{10,1... | collective-permute-start | bytes 393224 | tf_op jit(solution)/shard_map/ppermute | solution.py:56
  262.0 11.5 %collective-permute-start.16 = (bf16[512,512]{0,1:T(8,128)(2,1)S(1)}, bf16[512,512]{0,1:T(8,128)(2,1)S(1)}, u32[]{:S(2)}, u32[]{:S(2)}) collective-permute-start(bf16[512,512]{0,1:T(8,128)(2,1)S(1)} %pad_maximum_fusion.1), channel_id=1, source_target_pairs={{0,4},{1,5},{2,6},{3,7},{4,8},{5,9},{6,10},{7,11},{8,12},{9,13},{1... | collective-permute-start | bytes 1572872 | tf_op jit(solution)/shard_map/ppermute | solution.py:54
  264.6 20.0 %copy-start.1 = (f32[256,512]{1,0:T(8,128)S(1)}, f32[256,512]{1,0:T(8,128)}, u32[]{:S(2)}) copy-start(f32[256,512]{1,0:T(8,128)} %copy.69) | copy-start | bytes 1572868
  264.6 20.0 %copy-start.3 = (bf16[2048,256]{1,0:T(8,128)(2,1)S(1)}, bf16[2048,256]{1,0:T(8,128)(2,1)}, u32[]{:S(2)}) copy-start(bf16[2048,256]{1,0:T(8,128)(2,1)} %copy-done.2) | copy-start | bytes 3145732
  264.6 20.0 %copy-start.8 = (f32[1,256,512]{2,1,0:T(8,128)S(1)}, f32[1,256,512]{2,1,0:T(8,128)}, u32[]{:S(2)}) copy-start(f32[1,256,512]{2,1,0:T(8,128)} %param.17) | copy-start | bytes 1572868
  264.7 20.0 %copy-start.10 = (f32[1,256,512]{2,1,0:T(8,128)S(1)}, f32[1,256,512]{2,1,0:T(8,128)}, u32[]{:S(2)}) copy-start(f32[1,256,512]{2,1,0:T(8,128)} %param.18) | copy-start | bytes 1572868
  264.7 20.0 %copy-start.12 = (f32[256,512]{1,0:T(8,128)S(1)}, f32[256,512]{1,0:T(8,128)}, u32[]{:S(2)}) copy-start(f32[256,512]{1,0:T(8,128)} %copy-done.11) | copy-start | bytes 1572868
  264.7 10.9 %collective-permute-start.17 = (bf16[512,512]{0,1:T(8,128)(2,1)S(1)}, bf16[512,512]{0,1:T(8,128)(2,1)S(1)}, u32[]{:S(2)}, u32[]{:S(2)}) collective-permute-start(bf16[512,512]{0,1:T(8,128)(2,1)S(1)} %pad_maximum_fusion.1), channel_id=1, source_target_pairs={{0,12},{1,13},{2,14},{3,15},{4,0},{5,1},{6,2},{7,3},{8,4},{9,5},{1... | collective-permute-start | bytes 1572872 | tf_op jit(solution)/shard_map/ppermute | solution.py:55
  273.5 11.1 %collective-permute-start.18 = (bf16[512,512]{0,1:T(8,128)(2,1)S(1)}, bf16[512,512]{0,1:T(8,128)(2,1)S(1)}, u32[]{:S(2)}, u32[]{:S(2)}) collective-permute-start(bf16[512,512]{0,1:T(8,128)(2,1)S(1)} %collective-permute-done.16), channel_id=1, source_target_pairs={{0,4},{1,5},{2,6},{3,7},{4,8},{5,9},{6,10},{7,11},{8,12},{9,13},{1... | collective-permute-start | bytes 1572872 | tf_op jit(solution)/shard_map/ppermute | solution.py:56
  286.2 37.7 %copy-start.15 = (f32[256,16]{0,1:T(8,128)S(1)}, f32[256,16]{0,1:T(8,128)}, u32[]{:S(2)}) copy-start(f32[256,16]{0,1:T(8,128)} %param.20) | copy-start | bytes 49156

commit v9 on v8

--- a/solution.py
+++ b/solution.py
@@ -86,7 +86,7 @@
         if size == 4:
             moved[-1] = lax.ppermute(moved[0], "island", shift(axis, 1))
             moved[1] = lax.ppermute(moved[0], "island", shift(axis, -1))
-            moved[-2] = lax.ppermute(moved[-1], "island", shift(axis, 1))
+            moved[-2] = lax.ppermute(moved[0], "island", shift(axis, 2))
         else:
             for k in range(1, size):
                 moved[-k] = lax.ppermute(moved[-k + 1], "island", shift(axis, 1))

time: 326 us -> 325 us (level)
  waiting for transfers between devices: 101 us -> 90.4 us
  blocking collectives: 93.1 us -> 100 us
  starting transfers between devices: 84.4 us -> 87.7 us
    ppermute x2, starting transfers between devices: 3.82 us -> 13.8 us  [island_gather(): moved[-2] = lax.ppermute(moved[0], 'island', shift(axis, 2))]
    all_to_all x1, blocking collectives: 36.7 us -> 44.2 us  [on_device(): lax.all_to_all(sent.reshape(block + 2, groups, cols), 'island', split_axi...]
    all_to_all x1, starting transfers between devices: 15.3 us -> 8.61 us  [on_device(): lax.all_to_all(partial.reshape(members, rows, width), 'fsdp', split_axis=...]
    ppermute x2, waiting for transfers between devices: 6.4 us -> 0.01 us  [island_gather(): moved[-1] = lax.ppermute(moved[0], 'island', shift(axis, 1))]
    ppermute x2, waiting for transfers between devices: 11.5 us -> 6.83 us  [island_gather(): moved[-2] = lax.ppermute(moved[0], 'island', shift(axis, 2))]
  transfers between devices with their start and end apart: 21 -> 21, of which waited for: 12 -> 10; matrix products, arithmetic and copies ran while one was open for 4% -> 4% of each run, Pallas kernels for 0% -> 0%
where the time goes in v9:
time: 325 us; the launch traced here: 324 us
  blocking collectives  100 us (31%)
  waiting for transfers between devices  90.4 us (28%)
  starting transfers between devices  87.7 us (27%)
  local copies, waits for them, and re-layouts  19.4 us (6%)
  matrix products  12 us (4%)
  other arithmetic  11.9 us (4%)
    all_to_all x1, blocking collectives, on_device(): lax.all_to_all(partial.reshape(members, rows, width), 'fsdp', split_axis=...  55.8 us
    all_to_all x1, waiting for transfers between devices, on_device(): lax.all_to_all(partial.reshape(members, rows, width), 'fsdp', split_axis=...  47.9 us
    all_to_all x1, blocking collectives, on_device(): lax.all_to_all(sent.reshape(block + 2, groups, cols), 'island', split_axi...  44.2 us
    ppermute x4, waiting for transfers between devices, along(): far = lax.ppermute(up, 'fsdp', _shift(cols, rows, dx, dz))  26.3 us
    ppermute x4, starting transfers between devices, along(): down = lax.ppermute(part, 'fsdp', _shift(cols, rows, -dx, -dz))  19.7 us
    ppermute x2, starting transfers between devices, island_gather(): moved[-2] = lax.ppermute(moved[0], 'island', shift(axis, 2))  13.8 us
    ppermute x2, starting transfers between devices, island_gather(): moved[-1] = lax.ppermute(moved[0], 'island', shift(axis, 1))  11.5 us
    ppermute x4, waiting for transfers between devices, along(): up = lax.ppermute(part, 'fsdp', _shift(cols, rows, dx, dz))  9.29 us
  transfers between devices with their start and end apart: 21, of which 10 were waited for; matrix products, arithmetic and copies ran while one was open for 4% of the time, Pallas kernels for 0%

profile of v9, /device:TPU:1, one launch (start us, length us, event | category | flops | bytes accessed | tf_op | source)
XLA Modules:
  0.0 323.7 jit_solution(5745459792675840717)
XLA Ops:
  0.6 1.6 copy.55
  2.3 1.3 copy.56
  3.6 9.1 %all-to-all-start = ((bf16[128,16,256]{2,0,1:T(8,128)(2,1)}), bf16[128,16,256]{2,0,1:T(8,128)(2,1)S(1)}, u32[]{:S(2)}, u32[]{:S(2)}) async-start(bf16[128,16,256]{2,0,1:T(8,128)(2,1)} %copy.56), calls=%async_computation | async-start | bytes 2097152 | tf_op jit(solution)/shard_map/all_to_all | solution.py:130
  12.8 3.4 %collective-permute-start = (f32[1,256,16]{1,2,0:T(8,128)S(1)}, f32[1,256,16]{1,2,0:T(8,128)S(1)}, u32[]{:S(2)}, u32[]{:S(2)}) collective-permute-start(f32[1,256,16]{1,2,0:T(8,128)S(1)} %bitcast.170), channel_id=1, source_target_pairs={{0,16},{16,0},{32,48},{48,32},{64,80},{80,64},{96,112},{112,96},{1... | collective-permute-start | bytes 49160 | tf_op jit(solution)/shard_map/ppermute | solution.py:92
  16.4 1.2 copy.83
  17.8 1.6 sort.17
  19.5 2.3 divide_convert_fusion
  21.8 8.3 %collective-permute-start.1 = (f32[2,256,16]{1,2,0:T(8,128)S(1)}, f32[2,256,16]{1,2,0:T(8,128)S(1)}, u32[]{:S(2)}, u32[]{:S(2)}) collective-permute-start(f32[2,256,16]{1,2,0:T(8,128)S(1)} %pad_maximum_fusion.2), channel_id=1, source_target_pairs={{0,32},{16,48},{32,64},{48,80},{64,96},{80,112},{96,0},{112,16},{1... | collective-permute-start | bytes 98312 | tf_op jit(solution)/shard_map/ppermute | solution.py:87
  30.1 2.9 collective-permute-start.2
  32.9 10.3 %collective-permute-start.3 = (f32[2,256,16]{1,2,0:T(8,128)S(1)}, f32[2,256,16]{1,2,0:T(8,128)S(1)}, u32[]{:S(2)}, u32[]{:S(2)}) collective-permute-start(f32[2,256,16]{1,2,0:T(8,128)S(1)} %pad_maximum_fusion.2), channel_id=1, source_target_pairs={{0,64},{16,80},{32,96},{48,112},{64,0},{80,16},{96,32},{112,48},{1... | collective-permute-start | bytes 98312 | tf_op jit(solution)/shard_map/ppermute | solution.py:89
  43.3 3.2 collective-permute-done.3
  46.5 3.2 collective-permute-start.4
  49.7 3.4 %collective-permute-start.5 = (f32[8,256,16]{1,2,0:T(8,128)S(1)}, f32[8,256,16]{1,2,0:T(8,128)S(1)}, u32[]{:S(2)}, u32[]{:S(2)}) collective-permute-start(f32[8,256,16]{1,2,0:T(8,128)S(1)} %get-tuple-element.12), channel_id=1, source_target_pairs={{0,384},{16,400},{32,416},{48,432},{64,448},{80,464},{96,480},{112... | collective-permute-start | bytes 393224 | tf_op jit(solution)/shard_map/ppermute | solution.py:88
  53.1 3.5 %collective-permute-start.6 = (f32[8,256,16]{1,2,0:T(8,128)S(1)}, f32[8,256,16]{1,2,0:T(8,128)S(1)}, u32[]{:S(2)}, u32[]{:S(2)}) collective-permute-start(f32[8,256,16]{1,2,0:T(8,128)S(1)} %get-tuple-element.12), channel_id=1, source_target_pairs={{0,256},{16,272},{32,288},{48,304},{64,320},{80,336},{96,352},{112... | collective-permute-start | bytes 393224 | tf_op jit(solution)/shard_map/ppermute | solution.py:89
  56.7 3.6 %collective-permute-done.6 = f32[8,256,16]{1,2,0:T(8,128)S(1)} collective-permute-done((f32[8,256,16]{1,2,0:T(8,128)S(1)}, f32[8,256,16]{1,2,0:T(8,128)S(1)}, u32[]{:S(2)}, u32[]{:S(2)}) %collective-permute-start.6) | collective-permute-done | bytes 131104 | tf_op jit(solution)/shard_map/ppermute | solution.py:89
  60.3 0.6 gather_fusion
  61.1 2.0 convolution_convert_fusion.1
  63.1 8.6 %all-to-all-start.1 = ((bf16[16,128,512]{2,1,0:T(8,128)(2,1)}), bf16[16,128,512]{2,1,0:T(8,128)(2,1)}, u32[]{:S(2)}, u32[]{:S(2)}) async-start(bf16[16,128,512]{2,1,0:T(8,128)(2,1)} %bitcast.149), calls=%async_computation.1 | async-start | bytes 4194304 | tf_op jit(solution)/shard_map/all_to_all | solution.py:146
  72.0 1.7 copy.62
  73.7 47.9 %all-to-all-done.1 = bf16[16,128,512]{2,1,0:T(8,128)(2,1)} async-done(((bf16[16,128,512]{2,1,0:T(8,128)(2,1)}), bf16[16,128,512]{2,1,0:T(8,128)(2,1)}, u32[]{:S(2)}, u32[]{:S(2)}) %all-to-all-start.1) | async-done | bytes 2097184 | tf_op jit(solution)/shard_map/all_to_all | solution.py:146
  121.6 1.9 convert_reduce_fusion.1
  123.7 1.8 fusion.66
  125.4 2.9 copy.61
  128.3 2.2 fusion.12
  130.8 1.0 copy-done.5
  131.7 0.5 fusion.9
  132.2 1.9 collective-permute-start.7
  134.1 0.7 broadcast_bitcast_fusion
  134.8 5.1 %collective-permute-start.8 = (bf16[128,512]{0,1:T(8,128)(2,1)S(1)}, bf16[128,512]{0,1:T(8,128)(2,1)S(1)}, u32[]{:S(2)}, u32[]{:S(2)}) collective-permute-start(bf16[128,512]{0,1:T(8,128)(2,1)S(1)} %bitcast.163), channel_id=1, source_target_pairs={{0,3},{1,0},{2,1},{3,2},{4,7},{5,4},{6,5},{7,6},{8,11},{9,8},{10,9... | collective-permute-start | bytes 393224 | tf_op jit(solution)/shard_map/ppermute | solution.py:55
  140.0 1.9 collective-permute-start.9
  141.9 0.6 pad_clamp_fusion
  142.5 1.0 copy.69
  143.5 0.7 gather_fusion.1
  144.2 3.3 %collective-permute-done.9 = bf16[128,512]{0,1:T(8,128)(2,1)} collective-permute-done((bf16[128,512]{0,1:T(8,128)(2,1)S(1)}, bf16[128,512]{0,1:T(8,128)(2,1)}, u32[]{:S(2)}, u32[]{:S(2)}) %collective-permute-start.9) | collective-permute-done | bytes 131104 | tf_op jit(solution)/shard_map/ppermute | solution.py:56
  147.6 1.0 pad_maximum_fusion
  148.5 1.9 collective-permute-start.10
  150.5 1.1 bitcast_select_fusion.2
  151.6 4.6 %collective-permute-start.11 = (bf16[512,512]{0,1:T(8,128)(2,1)S(1)}, bf16[512,512]{0,1:T(8,128)(2,1)S(1)}, u32[]{:S(2)}, u32[]{:S(2)}) collective-permute-start(bf16[512,512]{0,1:T(8,128)(2,1)S(1)} %pad_maximum_fusion), channel_id=1, source_target_pairs={{0,12},{1,13},{2,14},{3,15},{4,0},{5,1},{6,2},{7,3},{8,4},{9,5},{1... | collective-permute-start | bytes 1572872 | tf_op jit(solution)/shard_map/ppermute | solution.py:55
  156.2 4.8 %collective-permute-done.10 = bf16[512,512]{0,1:T(8,128)(2,1)S(1)} collective-permute-done((bf16[512,512]{0,1:T(8,128)(2,1)S(1)}, bf16[512,512]{0,1:T(8,128)(2,1)S(1)}, u32[]{:S(2)}, u32[]{:S(2)}) %collective-permute-start.10) | collective-permute-done | bytes 524320 | tf_op jit(solution)/shard_map/ppermute | solution.py:54
  161.0 1.9 collective-permute-start.12
  163.0 0.9 constant_dynamic-update-slice_fusion.16
  164.1 8.5 %collective-permute-done.12 = bf16[512,512]{0,1:T(8,128)(2,1)S(1)} collective-permute-done((bf16[512,512]{0,1:T(8,128)(2,1)S(1)}, bf16[512,512]{0,1:T(8,128)(2,1)S(1)}, u32[]{:S(2)}, u32[]{:S(2)}) %collective-permute-start.12) | collective-permute-done | bytes 524320 | tf_op jit(solution)/shard_map/ppermute | solution.py:56
  172.7 0.8 fusion.67
  174.1 1.0 convolution_convert_fusion
  175.1 55.8 %all_to_all.38 = bf16[16,128,512]{2,1,0:T(8,128)(2,1)S(1)} all-to-all(bf16[16,128,512]{2,1,0:T(8,128)(2,1)S(1)} %bitcast.148), channel_id=1, replica_groups=mesh['island'=32,'fsdp'=16] {'fsdp'}, dimensions={0} | all-to-all | bytes 4194304 | tf_op jit(solution)/shard_map/all_to_all | solution.py:146
  230.9 0.3 convert_reduce_fusion
  231.4 1.8 fusion.68
  233.1 1.9 copy.67
  235.0 1.5 fusion.11
  236.9 1.0 copy-done.6
  237.8 0.5 fusion.10
  238.3 1.9 collective-permute-start.13
  240.2 5.2 %collective-permute-start.14 = (bf16[128,512]{0,1:T(8,128)(2,1)S(1)}, bf16[128,512]{0,1:T(8,128)(2,1)S(1)}, u32[]{:S(2)}, u32[]{:S(2)}) collective-permute-start(bf16[128,512]{0,1:T(8,128)(2,1)S(1)} %bitcast.167), channel_id=1, source_target_pairs={{0,3},{1,0},{2,1},{3,2},{4,7},{5,4},{6,5},{7,6},{8,11},{9,8},{10,9... | collective-permute-start | bytes 393224 | tf_op jit(solution)/shard_map/ppermute | solution.py:55
  245.4 0.6 collective-permute-done.13
  246.0 1.9 collective-permute-start.15
  247.9 5.6 %collective-permute-done.15 = bf16[128,512]{0,1:T(8,128)(2,1)S(1)} collective-permute-done((bf16[128,512]{0,1:T(8,128)(2,1)S(1)}, bf16[128,512]{0,1:T(8,128)(2,1)S(1)}, u32[]{:S(2)}, u32[]{:S(2)}) %collective-permute-start.15) | collective-permute-done | bytes 131104 | tf_op jit(solution)/shard_map/ppermute | solution.py:56
  253.6 1.9 collective-permute-start.16
  256.3 4.8 %collective-permute-start.17 = (bf16[512,512]{0,1:T(8,128)(2,1)S(1)}, bf16[512,512]{0,1:T(8,128)(2,1)S(1)}, u32[]{:S(2)}, u32[]{:S(2)}) collective-permute-start(bf16[512,512]{0,1:T(8,128)(2,1)S(1)} %pad_maximum_fusion.1), channel_id=1, source_target_pairs={{0,12},{1,13},{2,14},{3,15},{4,0},{5,1},{6,2},{7,3},{8,4},{9,5},{1... | collective-permute-start | bytes 1572872 | tf_op jit(solution)/shard_map/ppermute | solution.py:55
  261.2 3.9 %collective-permute-done.16 = bf16[512,512]{0,1:T(8,128)(2,1)S(1)} collective-permute-done((bf16[512,512]{0,1:T(8,128)(2,1)S(1)}, bf16[512,512]{0,1:T(8,128)(2,1)S(1)}, u32[]{:S(2)}, u32[]{:S(2)}) %collective-permute-start.16) | collective-permute-done | bytes 524320 | tf_op jit(solution)/shard_map/ppermute | solution.py:54
  265.1 1.9 collective-permute-start.18
  267.3 8.9 %collective-permute-done.18 = bf16[512,512]{0,1:T(8,128)(2,1)S(1)} collective-permute-done((bf16[512,512]{0,1:T(8,128)(2,1)S(1)}, bf16[512,512]{0,1:T(8,128)(2,1)S(1)}, u32[]{:S(2)}, u32[]{:S(2)}) %collective-permute-start.18) | collective-permute-done | bytes 524320 | tf_op jit(solution)/shard_map/ppermute | solution.py:56
  276.3 1.4 fusion.28
  278.1 44.2 %all_to_all.39 = bf16[258,32,16]{0,2,1:T(8,128)(2,1)S(1)} all-to-all(bf16[258,32,16]{0,2,1:T(8,128)(2,1)S(1)} %bitcast.155), channel_id=1, replica_groups=mesh['island'=32,'fsdp'=16] {'island'}, dimensions={1} | all-to-all | bytes 528384 | tf_op jit(solution)/shard_map/all_to_all | solution.py:189
  323.0 0.7 multiply_subtract_fusion.1
  (96 shorter events, 3.9 us)
Async XLA Ops:
  2.3 10.5 %copy-start.13 = (f32[256,16]{0,1:T(8,128)S(1)}, f32[256,16]{0,1:T(8,128)}, u32[]{:S(2)}) copy-start(f32[256,16]{0,1:T(8,128)} %param.19) | copy-start | bytes 49156
  2.3 14.1 %copy-start.4 = (bf16[128,4096]{1,0:T(8,128)(2,1)S(1)}, bf16[128,4096]{1,0:T(8,128)(2,1)}, u32[]{:S(2)}) copy-start(bf16[128,4096]{1,0:T(8,128)(2,1)} %param.13) | copy-start | bytes 3145732
  3.6 14.0 %copy-start.14 = (bf16[128,512]{1,0:T(8,128)(2,1)S(1)}, bf16[128,512]{1,0:T(8,128)(2,1)}, u32[]{:S(2)}) copy-start(bf16[128,512]{1,0:T(8,128)(2,1)} %param.14) | copy-start | bytes 393220
  3.6 15.8 %copy-start.16 = (s32[1,128]{1,0:T(1,128)S(1)}, s32[1,128]{1,0:T(1,128)}, u32[]{:S(2)}) copy-start(s32[1,128]{1,0:T(1,128)} %param.16) | copy-start | bytes 1540
  3.6 57.4 %all-to-all-start = ((bf16[128,16,256]{2,0,1:T(8,128)(2,1)}), bf16[128,16,256]{2,0,1:T(8,128)(2,1)S(1)}, u32[]{:S(2)}, u32[]{:S(2)}) async-start(bf16[128,16,256]{2,0,1:T(8,128)(2,1)} %copy.56), calls=%async_computation | async-start | bytes 2097152 | tf_op jit(solution)/shard_map/all_to_all | solution.py:130
  12.8 9.0 %collective-permute-start = (f32[1,256,16]{1,2,0:T(8,128)S(1)}, f32[1,256,16]{1,2,0:T(8,128)S(1)}, u32[]{:S(2)}, u32[]{:S(2)}) collective-permute-start(f32[1,256,16]{1,2,0:T(8,128)S(1)} %bitcast.170), channel_id=1, source_target_pairs={{0,16},{16,0},{32,48},{48,32},{64,80},{80,64},{96,112},{112,96},{1... | collective-permute-start | bytes 49160 | tf_op jit(solution)/shard_map/ppermute | solution.py:92
  21.8 21.4 %collective-permute-start.1 = (f32[2,256,16]{1,2,0:T(8,128)S(1)}, f32[2,256,16]{1,2,0:T(8,128)S(1)}, u32[]{:S(2)}, u32[]{:S(2)}) collective-permute-start(f32[2,256,16]{1,2,0:T(8,128)S(1)} %pad_maximum_fusion.2), channel_id=1, source_target_pairs={{0,32},{16,48},{32,64},{48,80},{64,96},{80,112},{96,0},{112,16},{1... | collective-permute-start | bytes 98312 | tf_op jit(solution)/shard_map/ppermute | solution.py:87
  30.1 13.2 %collective-permute-start.2 = (f32[2,256,16]{1,2,0:T(8,128)S(1)}, f32[2,256,16]{1,2,0:T(8,128)S(1)}, u32[]{:S(2)}, u32[]{:S(2)}) collective-permute-start(f32[2,256,16]{1,2,0:T(8,128)S(1)} %pad_maximum_fusion.2), channel_id=1, source_target_pairs={{0,96},{16,112},{32,0},{48,16},{64,32},{80,48},{96,64},{112,80},{1... | collective-permute-start | bytes 98312 | tf_op jit(solution)/shard_map/ppermute | solution.py:88
  32.9 13.6 %collective-permute-start.3 = (f32[2,256,16]{1,2,0:T(8,128)S(1)}, f32[2,256,16]{1,2,0:T(8,128)S(1)}, u32[]{:S(2)}, u32[]{:S(2)}) collective-permute-start(f32[2,256,16]{1,2,0:T(8,128)S(1)} %pad_maximum_fusion.2), channel_id=1, source_target_pairs={{0,64},{16,80},{32,96},{48,112},{64,0},{80,16},{96,32},{112,48},{1... | collective-permute-start | bytes 98312 | tf_op jit(solution)/shard_map/ppermute | solution.py:89
  46.5 10.1 %collective-permute-start.4 = (f32[8,256,16]{1,2,0:T(8,128)S(1)}, f32[8,256,16]{1,2,0:T(8,128)S(1)}, u32[]{:S(2)}, u32[]{:S(2)}) collective-permute-start(f32[8,256,16]{1,2,0:T(8,128)S(1)} %get-tuple-element.12), channel_id=1, source_target_pairs={{0,128},{16,144},{32,160},{48,176},{64,192},{80,208},{96,224},{112... | collective-permute-start | bytes 393224 | tf_op jit(solution)/shard_map/ppermute | solution.py:87
  49.7 7.0 %collective-permute-start.5 = (f32[8,256,16]{1,2,0:T(8,128)S(1)}, f32[8,256,16]{1,2,0:T(8,128)S(1)}, u32[]{:S(2)}, u32[]{:S(2)}) collective-permute-start(f32[8,256,16]{1,2,0:T(8,128)S(1)} %get-tuple-element.12), channel_id=1, source_target_pairs={{0,384},{16,400},{32,416},{48,432},{64,448},{80,464},{96,480},{112... | collective-permute-start | bytes 393224 | tf_op jit(solution)/shard_map/ppermute | solution.py:88
  53.1 7.2 %collective-permute-start.6 = (f32[8,256,16]{1,2,0:T(8,128)S(1)}, f32[8,256,16]{1,2,0:T(8,128)S(1)}, u32[]{:S(2)}, u32[]{:S(2)}) collective-permute-start(f32[8,256,16]{1,2,0:T(8,128)S(1)} %get-tuple-element.12), channel_id=1, source_target_pairs={{0,256},{16,272},{32,288},{48,304},{64,320},{80,336},{96,352},{112... | collective-permute-start | bytes 393224 | tf_op jit(solution)/shard_map/ppermute | solution.py:89
  63.1 8.6 %copy-start.17 = (s32[4]{0:T(128)S(1)}, s32[4]{0:T(128)}, u32[]{:S(2)}) copy-start(s32[4]{0:T(128)} %constant.257.clone) | copy-start | bytes 52
  63.1 58.5 %all-to-all-start.1 = ((bf16[16,128,512]{2,1,0:T(8,128)(2,1)}), bf16[16,128,512]{2,1,0:T(8,128)(2,1)}, u32[]{:S(2)}, u32[]{:S(2)}) async-start(bf16[16,128,512]{2,1,0:T(8,128)(2,1)} %bitcast.149), calls=%async_computation.1 | async-start | bytes 4194304 | tf_op jit(solution)/shard_map/all_to_all | solution.py:146
  130.5 1.2 copy-start.5
  132.2 7.7 %collective-permute-start.7 = (bf16[128,512]{0,1:T(8,128)(2,1)S(1)}, bf16[128,512]{0,1:T(8,128)(2,1)S(1)}, u32[]{:S(2)}, u32[]{:S(2)}) collective-permute-start(bf16[128,512]{0,1:T(8,128)(2,1)S(1)} %bitcast.162), channel_id=1, source_target_pairs={{0,1},{1,2},{2,3},{3,0},{4,5},{5,6},{6,7},{7,4},{8,9},{9,10},{10,1... | collective-permute-start | bytes 393224 | tf_op jit(solution)/shard_map/ppermute | solution.py:54
  134.8 9.4 %collective-permute-start.8 = (bf16[128,512]{0,1:T(8,128)(2,1)S(1)}, bf16[128,512]{0,1:T(8,128)(2,1)S(1)}, u32[]{:S(2)}, u32[]{:S(2)}) collective-permute-start(bf16[128,512]{0,1:T(8,128)(2,1)S(1)} %bitcast.163), channel_id=1, source_target_pairs={{0,3},{1,0},{2,1},{3,2},{4,7},{5,4},{6,5},{7,6},{8,11},{9,8},{10,9... | collective-permute-start | bytes 393224 | tf_op jit(solution)/shard_map/ppermute | solution.py:55
  140.0 7.6 %collective-permute-start.9 = (bf16[128,512]{0,1:T(8,128)(2,1)S(1)}, bf16[128,512]{0,1:T(8,128)(2,1)}, u32[]{:S(2)}, u32[]{:S(2)}) collective-permute-start(bf16[128,512]{0,1:T(8,128)(2,1)S(1)} %collective-permute-done.7), channel_id=1, source_target_pairs={{0,1},{1,2},{2,3},{3,0},{4,5},{5,6},{6,7},{7,4},{8,9},{9,10},{10,1... | collective-permute-start | bytes 393224 | tf_op jit(solution)/shard_map/ppermute | solution.py:56
  148.5 12.5 %collective-permute-start.10 = (bf16[512,512]{0,1:T(8,128)(2,1)S(1)}, bf16[512,512]{0,1:T(8,128)(2,1)S(1)}, u32[]{:S(2)}, u32[]{:S(2)}) collective-permute-start(bf16[512,512]{0,1:T(8,128)(2,1)S(1)} %pad_maximum_fusion), channel_id=1, source_target_pairs={{0,4},{1,5},{2,6},{3,7},{4,8},{5,9},{6,10},{7,11},{8,12},{9,13},{1... | collective-permute-start | bytes 1572872 | tf_op jit(solution)/shard_map/ppermute | solution.py:54
  151.6 21.1 %copy-start.2 = (bf16[2048,256]{1,0:T(8,128)(2,1)}, bf16[2048,256]{1,0:T(8,128)(2,1)S(1)}, u32[]{:S(2)}) copy-start(bf16[2048,256]{1,0:T(8,128)(2,1)S(1)} %bitcast_select_fusion.2) | copy-start | bytes 3145732
  151.6 12.4 %collective-permute-start.11 = (bf16[512,512]{0,1:T(8,128)(2,1)S(1)}, bf16[512,512]{0,1:T(8,128)(2,1)S(1)}, u32[]{:S(2)}, u32[]{:S(2)}) collective-permute-start(bf16[512,512]{0,1:T(8,128)(2,1)S(1)} %pad_maximum_fusion), channel_id=1, source_target_pairs={{0,12},{1,13},{2,14},{3,15},{4,0},{5,1},{6,2},{7,3},{8,4},{9,5},{1... | collective-permute-start | bytes 1572872 | tf_op jit(solution)/shard_map/ppermute | solution.py:55
  161.0 11.6 %collective-permute-start.12 = (bf16[512,512]{0,1:T(8,128)(2,1)S(1)}, bf16[512,512]{0,1:T(8,128)(2,1)S(1)}, u32[]{:S(2)}, u32[]{:S(2)}) collective-permute-start(bf16[512,512]{0,1:T(8,128)(2,1)S(1)} %collective-permute-done.10), channel_id=1, source_target_pairs={{0,4},{1,5},{2,6},{3,7},{4,8},{5,9},{6,10},{7,11},{8,12},{9,13},{1... | collective-permute-start | bytes 1572872 | tf_op jit(solution)/shard_map/ppermute | solution.py:56
  172.7 1.0 copy-start
  172.7 1.2 copy-start.7
  172.7 1.3 copy-start.9
  174.0 1.1 copy-start.11
  236.6 1.2 copy-start.6
  238.3 7.7 %collective-permute-start.13 = (bf16[128,512]{0,1:T(8,128)(2,1)S(1)}, bf16[128,512]{0,1:T(8,128)(2,1)S(1)}, u32[]{:S(2)}, u32[]{:S(2)}) collective-permute-start(bf16[128,512]{0,1:T(8,128)(2,1)S(1)} %bitcast.166), channel_id=1, source_target_pairs={{0,1},{1,2},{2,3},{3,0},{4,5},{5,6},{6,7},{7,4},{8,9},{9,10},{10,1... | collective-permute-start | bytes 393224 | tf_op jit(solution)/shard_map/ppermute | solution.py:54
  240.2 7.7 %collective-permute-start.14 = (bf16[128,512]{0,1:T(8,128)(2,1)S(1)}, bf16[128,512]{0,1:T(8,128)(2,1)S(1)}, u32[]{:S(2)}, u32[]{:S(2)}) collective-permute-start(bf16[128,512]{0,1:T(8,128)(2,1)S(1)} %bitcast.167), channel_id=1, source_target_pairs={{0,3},{1,0},{2,1},{3,2},{4,7},{5,4},{6,5},{7,6},{8,11},{9,8},{10,9... | collective-permute-start | bytes 393224 | tf_op jit(solution)/shard_map/ppermute | solution.py:55
  246.0 7.5 %collective-permute-start.15 = (bf16[128,512]{0,1:T(8,128)(2,1)S(1)}, bf16[128,512]{0,1:T(8,128)(2,1)S(1)}, u32[]{:S(2)}, u32[]{:S(2)}) collective-permute-start(bf16[128,512]{0,1:T(8,128)(2,1)S(1)} %collective-permute-done.13), channel_id=1, source_target_pairs={{0,1},{1,2},{2,3},{3,0},{4,5},{5,6},{6,7},{7,4},{8,9},{9,10},{10,1... | collective-permute-start | bytes 393224 | tf_op jit(solution)/shard_map/ppermute | solution.py:56
  253.6 11.5 %collective-permute-start.16 = (bf16[512,512]{0,1:T(8,128)(2,1)S(1)}, bf16[512,512]{0,1:T(8,128)(2,1)S(1)}, u32[]{:S(2)}, u32[]{:S(2)}) collective-permute-start(bf16[512,512]{0,1:T(8,128)(2,1)S(1)} %pad_maximum_fusion.1), channel_id=1, source_target_pairs={{0,4},{1,5},{2,6},{3,7},{4,8},{5,9},{6,10},{7,11},{8,12},{9,13},{1... | collective-permute-start | bytes 1572872 | tf_op jit(solution)/shard_map/ppermute | solution.py:54
  256.3 20.0 %copy-start.1 = (f32[256,512]{1,0:T(8,128)S(1)}, f32[256,512]{1,0:T(8,128)}, u32[]{:S(2)}) copy-start(f32[256,512]{1,0:T(8,128)} %copy.69) | copy-start | bytes 1572868
  256.3 20.0 %copy-start.3 = (bf16[2048,256]{1,0:T(8,128)(2,1)S(1)}, bf16[2048,256]{1,0:T(8,128)(2,1)}, u32[]{:S(2)}) copy-start(bf16[2048,256]{1,0:T(8,128)(2,1)} %copy-done.2) | copy-start | bytes 3145732
  256.3 20.0 %copy-start.8 = (f32[1,256,512]{2,1,0:T(8,128)S(1)}, f32[1,256,512]{2,1,0:T(8,128)}, u32[]{:S(2)}) copy-start(f32[1,256,512]{2,1,0:T(8,128)} %param.17) | copy-start | bytes 1572868
  256.3 20.0 %copy-start.10 = (f32[1,256,512]{2,1,0:T(8,128)S(1)}, f32[1,256,512]{2,1,0:T(8,128)}, u32[]{:S(2)}) copy-start(f32[1,256,512]{2,1,0:T(8,128)} %param.18) | copy-start | bytes 1572868
  256.3 20.0 %copy-start.12 = (f32[256,512]{1,0:T(8,128)S(1)}, f32[256,512]{1,0:T(8,128)}, u32[]{:S(2)}) copy-start(f32[256,512]{1,0:T(8,128)} %copy-done.11) | copy-start | bytes 1572868
  256.3 10.9 %collective-permute-start.17 = (bf16[512,512]{0,1:T(8,128)(2,1)S(1)}, bf16[512,512]{0,1:T(8,128)(2,1)S(1)}, u32[]{:S(2)}, u32[]{:S(2)}) collective-permute-start(bf16[512,512]{0,1:T(8,128)(2,1)S(1)} %pad_maximum_fusion.1), channel_id=1, source_target_pairs={{0,12},{1,13},{2,14},{3,15},{4,0},{5,1},{6,2},{7,3},{8,4},{9,5},{1... | collective-permute-start | bytes 1572872 | tf_op jit(solution)/shard_map/ppermute | solution.py:55
  265.1 11.1 %collective-permute-start.18 = (bf16[512,512]{0,1:T(8,128)(2,1)S(1)}, bf16[512,512]{0,1:T(8,128)(2,1)S(1)}, u32[]{:S(2)}, u32[]{:S(2)}) collective-permute-start(bf16[512,512]{0,1:T(8,128)(2,1)S(1)} %collective-permute-done.16), channel_id=1, source_target_pairs={{0,4},{1,5},{2,6},{3,7},{4,8},{5,9},{6,10},{7,11},{8,12},{9,13},{1... | collective-permute-start | bytes 1572872 | tf_op jit(solution)/shard_map/ppermute | solution.py:56
  277.9 45.1 %copy-start.15 = (f32[256,16]{0,1:T(8,128)S(1)}, f32[256,16]{0,1:T(8,128)}, u32[]{:S(2)}) copy-start(f32[256,16]{0,1:T(8,128)} %param.20) | copy-start | bytes 49156

commit v10 on v9

--- a/solution.py
+++ b/solution.py
@@ -53,7 +53,7 @@
         if size == 4:
             up = lax.ppermute(part, "fsdp", _shift(cols, rows, dx, dz))
             down = lax.ppermute(part, "fsdp", _shift(cols, rows, -dx, -dz))
-            far = lax.ppermute(up, "fsdp", _shift(cols, rows, dx, dz))
+            far = lax.ppermute(part, "fsdp", _shift(cols, rows, 2 * dx, 2 * dz))
             return [part, up, down, far]
         got = [part]
         for _ in range(size - 1):

time: 325 us -> 333 us (1.025)
  waiting for transfers between devices: 90.4 us -> 99.2 us
    ppermute x4, waiting for transfers between devices: 0.03 us -> 4.31 us  [along(): down = lax.ppermute(part, 'fsdp', _shift(cols, rows, -dx, -dz))]
  transfers between devices with their start and end apart: 21 -> 21, of which waited for: 10 -> 12; matrix products, arithmetic and copies ran while one was open for 4% -> 4% of each run, Pallas kernels for 0% -> 0%
where the time goes in v10:
time: 333 us; the launch traced here: 332 us
  waiting for transfers between devices  99.2 us (30%)
  blocking collectives  99.1 us (30%)
  starting transfers between devices  87.7 us (26%)
  local copies, waits for them, and re-layouts  19.4 us (6%)
  matrix products  12 us (4%)
  other arithmetic  11.9 us (4%)
    all_to_all x1, blocking collectives, on_device(): lax.all_to_all(partial.reshape(members, rows, width), 'fsdp', split_axis=...  56.6 us
    all_to_all x1, waiting for transfers between devices, on_device(): lax.all_to_all(partial.reshape(members, rows, width), 'fsdp', split_axis=...  47.2 us
    all_to_all x1, blocking collectives, on_device(): lax.all_to_all(sent.reshape(block + 2, groups, cols), 'island', split_axi...  42.6 us
    ppermute x4, waiting for transfers between devices, along(): far = lax.ppermute(part, 'fsdp', _shift(cols, rows, 2 * dx, 2 * dz))  29 us
    ppermute x4, starting transfers between devices, along(): down = lax.ppermute(part, 'fsdp', _shift(cols, rows, -dx, -dz))  19.7 us
    ppermute x2, starting transfers between devices, island_gather(): moved[-2] = lax.ppermute(moved[0], 'island', shift(axis, 2))  13.8 us
    ppermute x4, waiting for transfers between devices, along(): up = lax.ppermute(part, 'fsdp', _shift(cols, rows, dx, dz))  11.8 us
    ppermute x2, starting transfers between devices, island_gather(): moved[-1] = lax.ppermute(moved[0], 'island', shift(axis, 1))  11.5 us
  transfers between devices with their start and end apart: 21, of which 12 were waited for; matrix products, arithmetic and copies ran while one was open for 4% of the time, Pallas kernels for 0%

profile of v10, /device:TPU:1, one launch (start us, length us, event | category | flops | bytes accessed | tf_op | source)
XLA Modules:
  0.0 331.7 jit_solution(3343313406179287350)
XLA Ops:
  0.6 1.6 copy.55
  2.3 1.3 copy.56
  3.6 9.1 %all-to-all-start = ((bf16[128,16,256]{2,0,1:T(8,128)(2,1)}), bf16[128,16,256]{2,0,1:T(8,128)(2,1)S(1)}, u32[]{:S(2)}, u32[]{:S(2)}) async-start(bf16[128,16,256]{2,0,1:T(8,128)(2,1)} %copy.56), calls=%async_computation | async-start | bytes 2097152 | tf_op jit(solution)/shard_map/all_to_all | solution.py:130
  12.8 3.4 %collective-permute-start = (f32[1,256,16]{1,2,0:T(8,128)S(1)}, f32[1,256,16]{1,2,0:T(8,128)S(1)}, u32[]{:S(2)}, u32[]{:S(2)}) collective-permute-start(f32[1,256,16]{1,2,0:T(8,128)S(1)} %bitcast.172), channel_id=1, source_target_pairs={{0,16},{16,0},{32,48},{48,32},{64,80},{80,64},{96,112},{112,96},{1... | collective-permute-start | bytes 49160 | tf_op jit(solution)/shard_map/ppermute | solution.py:92
  16.4 1.2 copy.83
  17.8 1.6 sort.17
  19.5 2.3 divide_convert_fusion
  21.8 8.3 %collective-permute-start.1 = (f32[2,256,16]{1,2,0:T(8,128)S(1)}, f32[2,256,16]{1,2,0:T(8,128)S(1)}, u32[]{:S(2)}, u32[]{:S(2)}) collective-permute-start(f32[2,256,16]{1,2,0:T(8,128)S(1)} %pad_maximum_fusion.2), channel_id=1, source_target_pairs={{0,32},{16,48},{32,64},{48,80},{64,96},{80,112},{96,0},{112,16},{1... | collective-permute-start | bytes 98312 | tf_op jit(solution)/shard_map/ppermute | solution.py:87
  30.1 2.9 collective-permute-start.2
  32.9 10.3 %collective-permute-start.3 = (f32[2,256,16]{1,2,0:T(8,128)S(1)}, f32[2,256,16]{1,2,0:T(8,128)S(1)}, u32[]{:S(2)}, u32[]{:S(2)}) collective-permute-start(f32[2,256,16]{1,2,0:T(8,128)S(1)} %pad_maximum_fusion.2), channel_id=1, source_target_pairs={{0,64},{16,80},{32,96},{48,112},{64,0},{80,16},{96,32},{112,48},{1... | collective-permute-start | bytes 98312 | tf_op jit(solution)/shard_map/ppermute | solution.py:89
  43.3 3.2 collective-permute-done.3
  46.5 3.2 collective-permute-start.4
  49.7 3.4 %collective-permute-start.5 = (f32[8,256,16]{1,2,0:T(8,128)S(1)}, f32[8,256,16]{1,2,0:T(8,128)S(1)}, u32[]{:S(2)}, u32[]{:S(2)}) collective-permute-start(f32[8,256,16]{1,2,0:T(8,128)S(1)} %get-tuple-element.12), channel_id=1, source_target_pairs={{0,384},{16,400},{32,416},{48,432},{64,448},{80,464},{96,480},{112... | collective-permute-start | bytes 393224 | tf_op jit(solution)/shard_map/ppermute | solution.py:88
  53.1 3.5 %collective-permute-start.6 = (f32[8,256,16]{1,2,0:T(8,128)S(1)}, f32[8,256,16]{1,2,0:T(8,128)S(1)}, u32[]{:S(2)}, u32[]{:S(2)}) collective-permute-start(f32[8,256,16]{1,2,0:T(8,128)S(1)} %get-tuple-element.12), channel_id=1, source_target_pairs={{0,256},{16,272},{32,288},{48,304},{64,320},{80,336},{96,352},{112... | collective-permute-start | bytes 393224 | tf_op jit(solution)/shard_map/ppermute | solution.py:89
  56.7 3.6 %collective-permute-done.6 = f32[8,256,16]{1,2,0:T(8,128)S(1)} collective-permute-done((f32[8,256,16]{1,2,0:T(8,128)S(1)}, f32[8,256,16]{1,2,0:T(8,128)S(1)}, u32[]{:S(2)}, u32[]{:S(2)}) %collective-permute-start.6) | collective-permute-done | bytes 131104 | tf_op jit(solution)/shard_map/ppermute | solution.py:89
  60.3 0.6 gather_fusion
  61.1 2.0 convolution_convert_fusion.1
  63.1 8.6 %all-to-all-start.1 = ((bf16[16,128,512]{2,1,0:T(8,128)(2,1)}), bf16[16,128,512]{2,1,0:T(8,128)(2,1)}, u32[]{:S(2)}, u32[]{:S(2)}) async-start(bf16[16,128,512]{2,1,0:T(8,128)(2,1)} %bitcast.149), calls=%async_computation.1 | async-start | bytes 4194304 | tf_op jit(solution)/shard_map/all_to_all | solution.py:146
  72.0 0.7 broadcast_bitcast_fusion
  72.7 1.7 copy.62
  74.4 47.2 %all-to-all-done.1 = bf16[16,128,512]{2,1,0:T(8,128)(2,1)} async-done(((bf16[16,128,512]{2,1,0:T(8,128)(2,1)}), bf16[16,128,512]{2,1,0:T(8,128)(2,1)}, u32[]{:S(2)}, u32[]{:S(2)}) %all-to-all-start.1) | async-done | bytes 2097184 | tf_op jit(solution)/shard_map/all_to_all | solution.py:146
  121.6 1.9 convert_reduce_fusion.1
  123.7 1.8 fusion.66
  125.4 2.9 copy.61
  128.3 2.2 fusion.12
  130.8 1.0 copy-done.5
  131.7 0.5 fusion.9
  132.2 1.9 collective-permute-start.7
  134.1 5.2 %collective-permute-start.8 = (bf16[128,512]{0,1:T(8,128)(2,1)S(1)}, bf16[128,512]{0,1:T(8,128)(2,1)S(1)}, u32[]{:S(2)}, u32[]{:S(2)}) collective-permute-start(bf16[128,512]{0,1:T(8,128)(2,1)S(1)} %bitcast.168), channel_id=1, source_target_pairs={{0,3},{1,0},{2,1},{3,2},{4,7},{5,4},{6,5},{7,6},{8,11},{9,8},{10,9... | collective-permute-start | bytes 393224 | tf_op jit(solution)/shard_map/ppermute | solution.py:55
  139.3 1.9 collective-permute-start.9
  141.2 0.6 pad_clamp_fusion
  141.8 1.0 copy.69
  142.8 0.7 gather_fusion.1
  144.0 5.3 %collective-permute-done.9 = bf16[128,512]{0,1:T(8,128)(2,1)} collective-permute-done((bf16[128,512]{0,1:T(8,128)(2,1)S(1)}, bf16[128,512]{0,1:T(8,128)(2,1)}, u32[]{:S(2)}, u32[]{:S(2)}) %collective-permute-start.9) | collective-permute-done | bytes 131104 | tf_op jit(solution)/shard_map/ppermute | solution.py:56
  149.2 1.0 pad_maximum_fusion
  150.2 1.9 collective-permute-start.10
  152.1 1.1 bitcast_select_fusion.2
  153.3 4.6 %collective-permute-start.11 = (bf16[512,512]{0,1:T(8,128)(2,1)S(1)}, bf16[512,512]{0,1:T(8,128)(2,1)S(1)}, u32[]{:S(2)}, u32[]{:S(2)}) collective-permute-start(bf16[512,512]{0,1:T(8,128)(2,1)S(1)} %pad_maximum_fusion), channel_id=1, source_target_pairs={{0,12},{1,13},{2,14},{3,15},{4,0},{5,1},{6,2},{7,3},{8,4},{9,5},{1... | collective-permute-start | bytes 1572872 | tf_op jit(solution)/shard_map/ppermute | solution.py:55
  157.9 1.9 collective-permute-start.12
  159.9 0.9 constant_dynamic-update-slice_fusion.16
  160.8 5.4 %collective-permute-done.10 = bf16[512,512]{0,1:T(8,128)(2,1)S(1)} collective-permute-done((bf16[512,512]{0,1:T(8,128)(2,1)S(1)}, bf16[512,512]{0,1:T(8,128)(2,1)S(1)}, u32[]{:S(2)}, u32[]{:S(2)}) %collective-permute-start.10) | collective-permute-done | bytes 524320 | tf_op jit(solution)/shard_map/ppermute | solution.py:54
  166.3 2.2 collective-permute-done.11
  168.6 8.0 %collective-permute-done.12 = bf16[512,512]{0,1:T(8,128)(2,1)S(1)} collective-permute-done((bf16[512,512]{0,1:T(8,128)(2,1)S(1)}, bf16[512,512]{0,1:T(8,128)(2,1)S(1)}, u32[]{:S(2)}, u32[]{:S(2)}) %collective-permute-start.12) | collective-permute-done | bytes 524320 | tf_op jit(solution)/shard_map/ppermute | solution.py:56
  176.7 0.8 fusion.67
  178.0 1.0 convolution_convert_fusion
  179.1 56.6 %all_to_all.38 = bf16[16,128,512]{2,1,0:T(8,128)(2,1)S(1)} all-to-all(bf16[16,128,512]{2,1,0:T(8,128)(2,1)S(1)} %bitcast.148), channel_id=1, replica_groups=mesh['island'=32,'fsdp'=16] {'fsdp'}, dimensions={0} | all-to-all | bytes 4194304 | tf_op jit(solution)/shard_map/all_to_all | solution.py:146
  236.1 1.8 fusion.68
  237.9 1.9 copy.67
  239.8 1.5 fusion.11
  241.6 1.0 copy-done.6
  242.6 0.5 fusion.10
  243.0 1.9 collective-permute-start.13
  245.0 5.2 %collective-permute-start.14 = (bf16[128,512]{0,1:T(8,128)(2,1)S(1)}, bf16[128,512]{0,1:T(8,128)(2,1)S(1)}, u32[]{:S(2)}, u32[]{:S(2)}) collective-permute-start(bf16[128,512]{0,1:T(8,128)(2,1)S(1)} %bitcast.163), channel_id=1, source_target_pairs={{0,3},{1,0},{2,1},{3,2},{4,7},{5,4},{6,5},{7,6},{8,11},{9,8},{10,9... | collective-permute-start | bytes 393224 | tf_op jit(solution)/shard_map/ppermute | solution.py:55
  250.1 1.9 collective-permute-start.15
  252.1 8.1 %collective-permute-done.15 = bf16[128,512]{0,1:T(8,128)(2,1)S(1)} collective-permute-done((bf16[128,512]{0,1:T(8,128)(2,1)S(1)}, bf16[128,512]{0,1:T(8,128)(2,1)S(1)}, u32[]{:S(2)}, u32[]{:S(2)}) %collective-permute-start.15) | collective-permute-done | bytes 131104 | tf_op jit(solution)/shard_map/ppermute | solution.py:56
  260.3 1.9 collective-permute-start.16
  263.0 4.8 %collective-permute-start.17 = (bf16[512,512]{0,1:T(8,128)(2,1)S(1)}, bf16[512,512]{0,1:T(8,128)(2,1)S(1)}, u32[]{:S(2)}, u32[]{:S(2)}) collective-permute-start(bf16[512,512]{0,1:T(8,128)(2,1)S(1)} %pad_maximum_fusion.1), channel_id=1, source_target_pairs={{0,12},{1,13},{2,14},{3,15},{4,0},{5,1},{6,2},{7,3},{8,4},{9,5},{1... | collective-permute-start | bytes 1572872 | tf_op jit(solution)/shard_map/ppermute | solution.py:55
  267.9 1.9 collective-permute-start.18
  269.9 6.4 %collective-permute-done.16 = bf16[512,512]{0,1:T(8,128)(2,1)S(1)} collective-permute-done((bf16[512,512]{0,1:T(8,128)(2,1)S(1)}, bf16[512,512]{0,1:T(8,128)(2,1)S(1)}, u32[]{:S(2)}, u32[]{:S(2)}) %collective-permute-start.16) | collective-permute-done | bytes 524320 | tf_op jit(solution)/shard_map/ppermute | solution.py:54
  276.4 1.7 collective-permute-done.17
  278.2 7.7 %collective-permute-done.18 = bf16[512,512]{0,1:T(8,128)(2,1)S(1)} collective-permute-done((bf16[512,512]{0,1:T(8,128)(2,1)S(1)}, bf16[512,512]{0,1:T(8,128)(2,1)S(1)}, u32[]{:S(2)}, u32[]{:S(2)}) %collective-permute-start.18) | collective-permute-done | bytes 524320 | tf_op jit(solution)/shard_map/ppermute | solution.py:56
  286.0 1.4 fusion.28
  287.7 42.6 %all_to_all.39 = bf16[258,32,16]{0,2,1:T(8,128)(2,1)S(1)} all-to-all(bf16[258,32,16]{0,2,1:T(8,128)(2,1)S(1)} %bitcast.155), channel_id=1, replica_groups=mesh['island'=32,'fsdp'=16] {'island'}, dimensions={1} | all-to-all | bytes 528384 | tf_op jit(solution)/shard_map/all_to_all | solution.py:189
  331.0 0.7 multiply_subtract_fusion.1
  (96 shorter events, 4.6 us)
Async XLA Ops:
  2.3 10.5 %copy-start.13 = (f32[256,16]{0,1:T(8,128)S(1)}, f32[256,16]{0,1:T(8,128)}, u32[]{:S(2)}) copy-start(f32[256,16]{0,1:T(8,128)} %param.19) | copy-start | bytes 49156
  2.3 14.1 %copy-start.4 = (bf16[128,4096]{1,0:T(8,128)(2,1)S(1)}, bf16[128,4096]{1,0:T(8,128)(2,1)}, u32[]{:S(2)}) copy-start(bf16[128,4096]{1,0:T(8,128)(2,1)} %param.13) | copy-start | bytes 3145732
  3.6 14.0 %copy-start.14 = (bf16[128,512]{1,0:T(8,128)(2,1)S(1)}, bf16[128,512]{1,0:T(8,128)(2,1)}, u32[]{:S(2)}) copy-start(bf16[128,512]{1,0:T(8,128)(2,1)} %param.14) | copy-start | bytes 393220
  3.6 15.8 %copy-start.16 = (s32[1,128]{1,0:T(1,128)S(1)}, s32[1,128]{1,0:T(1,128)}, u32[]{:S(2)}) copy-start(s32[1,128]{1,0:T(1,128)} %param.16) | copy-start | bytes 1540
  3.6 57.4 %all-to-all-start = ((bf16[128,16,256]{2,0,1:T(8,128)(2,1)}), bf16[128,16,256]{2,0,1:T(8,128)(2,1)S(1)}, u32[]{:S(2)}, u32[]{:S(2)}) async-start(bf16[128,16,256]{2,0,1:T(8,128)(2,1)} %copy.56), calls=%async_computation | async-start | bytes 2097152 | tf_op jit(solution)/shard_map/all_to_all | solution.py:130
  12.8 9.0 %collective-permute-start = (f32[1,256,16]{1,2,0:T(8,128)S(1)}, f32[1,256,16]{1,2,0:T(8,128)S(1)}, u32[]{:S(2)}, u32[]{:S(2)}) collective-permute-start(f32[1,256,16]{1,2,0:T(8,128)S(1)} %bitcast.172), channel_id=1, source_target_pairs={{0,16},{16,0},{32,48},{48,32},{64,80},{80,64},{96,112},{112,96},{1... | collective-permute-start | bytes 49160 | tf_op jit(solution)/shard_map/ppermute | solution.py:92
  21.8 21.4 %collective-permute-start.1 = (f32[2,256,16]{1,2,0:T(8,128)S(1)}, f32[2,256,16]{1,2,0:T(8,128)S(1)}, u32[]{:S(2)}, u32[]{:S(2)}) collective-permute-start(f32[2,256,16]{1,2,0:T(8,128)S(1)} %pad_maximum_fusion.2), channel_id=1, source_target_pairs={{0,32},{16,48},{32,64},{48,80},{64,96},{80,112},{96,0},{112,16},{1... | collective-permute-start | bytes 98312 | tf_op jit(solution)/shard_map/ppermute | solution.py:87
  30.1 13.2 %collective-permute-start.2 = (f32[2,256,16]{1,2,0:T(8,128)S(1)}, f32[2,256,16]{1,2,0:T(8,128)S(1)}, u32[]{:S(2)}, u32[]{:S(2)}) collective-permute-start(f32[2,256,16]{1,2,0:T(8,128)S(1)} %pad_maximum_fusion.2), channel_id=1, source_target_pairs={{0,96},{16,112},{32,0},{48,16},{64,32},{80,48},{96,64},{112,80},{1... | collective-permute-start | bytes 98312 | tf_op jit(solution)/shard_map/ppermute | solution.py:88
  32.9 13.6 %collective-permute-start.3 = (f32[2,256,16]{1,2,0:T(8,128)S(1)}, f32[2,256,16]{1,2,0:T(8,128)S(1)}, u32[]{:S(2)}, u32[]{:S(2)}) collective-permute-start(f32[2,256,16]{1,2,0:T(8,128)S(1)} %pad_maximum_fusion.2), channel_id=1, source_target_pairs={{0,64},{16,80},{32,96},{48,112},{64,0},{80,16},{96,32},{112,48},{1... | collective-permute-start | bytes 98312 | tf_op jit(solution)/shard_map/ppermute | solution.py:89
  46.5 10.1 %collective-permute-start.4 = (f32[8,256,16]{1,2,0:T(8,128)S(1)}, f32[8,256,16]{1,2,0:T(8,128)S(1)}, u32[]{:S(2)}, u32[]{:S(2)}) collective-permute-start(f32[8,256,16]{1,2,0:T(8,128)S(1)} %get-tuple-element.12), channel_id=1, source_target_pairs={{0,128},{16,144},{32,160},{48,176},{64,192},{80,208},{96,224},{112... | collective-permute-start | bytes 393224 | tf_op jit(solution)/shard_map/ppermute | solution.py:87
  49.7 7.0 %collective-permute-start.5 = (f32[8,256,16]{1,2,0:T(8,128)S(1)}, f32[8,256,16]{1,2,0:T(8,128)S(1)}, u32[]{:S(2)}, u32[]{:S(2)}) collective-permute-start(f32[8,256,16]{1,2,0:T(8,128)S(1)} %get-tuple-element.12), channel_id=1, source_target_pairs={{0,384},{16,400},{32,416},{48,432},{64,448},{80,464},{96,480},{112... | collective-permute-start | bytes 393224 | tf_op jit(solution)/shard_map/ppermute | solution.py:88
  53.1 7.2 %collective-permute-start.6 = (f32[8,256,16]{1,2,0:T(8,128)S(1)}, f32[8,256,16]{1,2,0:T(8,128)S(1)}, u32[]{:S(2)}, u32[]{:S(2)}) collective-permute-start(f32[8,256,16]{1,2,0:T(8,128)S(1)} %get-tuple-element.12), channel_id=1, source_target_pairs={{0,256},{16,272},{32,288},{48,304},{64,320},{80,336},{96,352},{112... | collective-permute-start | bytes 393224 | tf_op jit(solution)/shard_map/ppermute | solution.py:89
  63.1 8.6 %copy-start.17 = (s32[4]{0:T(128)S(1)}, s32[4]{0:T(128)}, u32[]{:S(2)}) copy-start(s32[4]{0:T(128)} %constant.257.clone) | copy-start | bytes 52
  63.1 58.5 %all-to-all-start.1 = ((bf16[16,128,512]{2,1,0:T(8,128)(2,1)}), bf16[16,128,512]{2,1,0:T(8,128)(2,1)}, u32[]{:S(2)}, u32[]{:S(2)}) async-start(bf16[16,128,512]{2,1,0:T(8,128)(2,1)} %bitcast.149), calls=%async_computation.1 | async-start | bytes 4194304 | tf_op jit(solution)/shard_map/all_to_all | solution.py:146
  130.5 1.2 copy-start.5
  132.2 11.4 %collective-permute-start.7 = (bf16[128,512]{0,1:T(8,128)(2,1)S(1)}, bf16[128,512]{0,1:T(8,128)(2,1)S(1)}, u32[]{:S(2)}, u32[]{:S(2)}) collective-permute-start(bf16[128,512]{0,1:T(8,128)(2,1)S(1)} %bitcast.167), channel_id=1, source_target_pairs={{0,1},{1,2},{2,3},{3,0},{4,5},{5,6},{6,7},{7,4},{8,9},{9,10},{10,1... | collective-permute-start | bytes 393224 | tf_op jit(solution)/shard_map/ppermute | solution.py:54
  134.1 9.8 %collective-permute-start.8 = (bf16[128,512]{0,1:T(8,128)(2,1)S(1)}, bf16[128,512]{0,1:T(8,128)(2,1)S(1)}, u32[]{:S(2)}, u32[]{:S(2)}) collective-permute-start(bf16[128,512]{0,1:T(8,128)(2,1)S(1)} %bitcast.168), channel_id=1, source_target_pairs={{0,3},{1,0},{2,1},{3,2},{4,7},{5,4},{6,5},{7,6},{8,11},{9,8},{10,9... | collective-permute-start | bytes 393224 | tf_op jit(solution)/shard_map/ppermute | solution.py:55
  139.3 9.9 %collective-permute-start.9 = (bf16[128,512]{0,1:T(8,128)(2,1)S(1)}, bf16[128,512]{0,1:T(8,128)(2,1)}, u32[]{:S(2)}, u32[]{:S(2)}) collective-permute-start(bf16[128,512]{0,1:T(8,128)(2,1)S(1)} %bitcast.169), channel_id=1, source_target_pairs={{0,2},{1,3},{2,0},{3,1},{4,6},{5,7},{6,4},{7,5},{8,10},{9,11},{10,... | collective-permute-start | bytes 393224 | tf_op jit(solution)/shard_map/ppermute | solution.py:56
  150.2 16.1 %collective-permute-start.10 = (bf16[512,512]{0,1:T(8,128)(2,1)S(1)}, bf16[512,512]{0,1:T(8,128)(2,1)S(1)}, u32[]{:S(2)}, u32[]{:S(2)}) collective-permute-start(bf16[512,512]{0,1:T(8,128)(2,1)S(1)} %pad_maximum_fusion), channel_id=1, source_target_pairs={{0,4},{1,5},{2,6},{3,7},{4,8},{5,9},{6,10},{7,11},{8,12},{9,13},{1... | collective-permute-start | bytes 1572872 | tf_op jit(solution)/shard_map/ppermute | solution.py:54
  153.2 23.4 %copy-start.2 = (bf16[2048,256]{1,0:T(8,128)(2,1)}, bf16[2048,256]{1,0:T(8,128)(2,1)S(1)}, u32[]{:S(2)}) copy-start(bf16[2048,256]{1,0:T(8,128)(2,1)S(1)} %bitcast_select_fusion.2) | copy-start | bytes 3145732
  153.3 15.3 %collective-permute-start.11 = (bf16[512,512]{0,1:T(8,128)(2,1)S(1)}, bf16[512,512]{0,1:T(8,128)(2,1)S(1)}, u32[]{:S(2)}, u32[]{:S(2)}) collective-permute-start(bf16[512,512]{0,1:T(8,128)(2,1)S(1)} %pad_maximum_fusion), channel_id=1, source_target_pairs={{0,12},{1,13},{2,14},{3,15},{4,0},{5,1},{6,2},{7,3},{8,4},{9,5},{1... | collective-permute-start | bytes 1572872 | tf_op jit(solution)/shard_map/ppermute | solution.py:55
  157.9 18.7 %collective-permute-start.12 = (bf16[512,512]{0,1:T(8,128)(2,1)S(1)}, bf16[512,512]{0,1:T(8,128)(2,1)S(1)}, u32[]{:S(2)}, u32[]{:S(2)}) collective-permute-start(bf16[512,512]{0,1:T(8,128)(2,1)S(1)} %pad_maximum_fusion), channel_id=1, source_target_pairs={{0,8},{1,9},{2,10},{3,11},{4,12},{5,13},{6,14},{7,15},{8,0},{9,1},... | collective-permute-start | bytes 1572872 | tf_op jit(solution)/shard_map/ppermute | solution.py:56
  176.7 1.0 copy-start
  176.7 1.2 copy-start.7
  176.7 1.3 copy-start.9
  178.0 1.1 copy-start.11
  241.3 1.2 copy-start.6
  243.0 9.0 %collective-permute-start.13 = (bf16[128,512]{0,1:T(8,128)(2,1)S(1)}, bf16[128,512]{0,1:T(8,128)(2,1)S(1)}, u32[]{:S(2)}, u32[]{:S(2)}) collective-permute-start(bf16[128,512]{0,1:T(8,128)(2,1)S(1)} %bitcast.162), channel_id=1, source_target_pairs={{0,1},{1,2},{2,3},{3,0},{4,5},{5,6},{6,7},{7,4},{8,9},{9,10},{10,1... | collective-permute-start | bytes 393224 | tf_op jit(solution)/shard_map/ppermute | solution.py:54
  245.0 7.1 %collective-permute-start.14 = (bf16[128,512]{0,1:T(8,128)(2,1)S(1)}, bf16[128,512]{0,1:T(8,128)(2,1)S(1)}, u32[]{:S(2)}, u32[]{:S(2)}) collective-permute-start(bf16[128,512]{0,1:T(8,128)(2,1)S(1)} %bitcast.163), channel_id=1, source_target_pairs={{0,3},{1,0},{2,1},{3,2},{4,7},{5,4},{6,5},{7,6},{8,11},{9,8},{10,9... | collective-permute-start | bytes 393224 | tf_op jit(solution)/shard_map/ppermute | solution.py:55
  250.1 10.1 %collective-permute-start.15 = (bf16[128,512]{0,1:T(8,128)(2,1)S(1)}, bf16[128,512]{0,1:T(8,128)(2,1)S(1)}, u32[]{:S(2)}, u32[]{:S(2)}) collective-permute-start(bf16[128,512]{0,1:T(8,128)(2,1)S(1)} %bitcast.164), channel_id=1, source_target_pairs={{0,2},{1,3},{2,0},{3,1},{4,6},{5,7},{6,4},{7,5},{8,10},{9,11},{10,... | collective-permute-start | bytes 393224 | tf_op jit(solution)/shard_map/ppermute | solution.py:56
  260.3 16.1 %collective-permute-start.16 = (bf16[512,512]{0,1:T(8,128)(2,1)S(1)}, bf16[512,512]{0,1:T(8,128)(2,1)S(1)}, u32[]{:S(2)}, u32[]{:S(2)}) collective-permute-start(bf16[512,512]{0,1:T(8,128)(2,1)S(1)} %pad_maximum_fusion.1), channel_id=1, source_target_pairs={{0,4},{1,5},{2,6},{3,7},{4,8},{5,9},{6,10},{7,11},{8,12},{9,13},{1... | collective-permute-start | bytes 1572872 | tf_op jit(solution)/shard_map/ppermute | solution.py:54
  262.9 23.0 %copy-start.1 = (f32[256,512]{1,0:T(8,128)S(1)}, f32[256,512]{1,0:T(8,128)}, u32[]{:S(2)}) copy-start(f32[256,512]{1,0:T(8,128)} %copy.69) | copy-start | bytes 1572868
  262.9 23.0 %copy-start.3 = (bf16[2048,256]{1,0:T(8,128)(2,1)S(1)}, bf16[2048,256]{1,0:T(8,128)(2,1)}, u32[]{:S(2)}) copy-start(bf16[2048,256]{1,0:T(8,128)(2,1)} %copy-done.2) | copy-start | bytes 3145732
  262.9 23.0 %copy-start.8 = (f32[1,256,512]{2,1,0:T(8,128)S(1)}, f32[1,256,512]{2,1,0:T(8,128)}, u32[]{:S(2)}) copy-start(f32[1,256,512]{2,1,0:T(8,128)} %param.17) | copy-start | bytes 1572868
  263.0 23.0 %copy-start.10 = (f32[1,256,512]{2,1,0:T(8,128)S(1)}, f32[1,256,512]{2,1,0:T(8,128)}, u32[]{:S(2)}) copy-start(f32[1,256,512]{2,1,0:T(8,128)} %param.18) | copy-start | bytes 1572868
  263.0 23.0 %copy-start.12 = (f32[256,512]{1,0:T(8,128)S(1)}, f32[256,512]{1,0:T(8,128)}, u32[]{:S(2)}) copy-start(f32[256,512]{1,0:T(8,128)} %copy-done.11) | copy-start | bytes 1572868
  263.0 15.1 %collective-permute-start.17 = (bf16[512,512]{0,1:T(8,128)(2,1)S(1)}, bf16[512,512]{0,1:T(8,128)(2,1)S(1)}, u32[]{:S(2)}, u32[]{:S(2)}) collective-permute-start(bf16[512,512]{0,1:T(8,128)(2,1)S(1)} %pad_maximum_fusion.1), channel_id=1, source_target_pairs={{0,12},{1,13},{2,14},{3,15},{4,0},{5,1},{6,2},{7,3},{8,4},{9,5},{1... | collective-permute-start | bytes 1572872 | tf_op jit(solution)/shard_map/ppermute | solution.py:55
  267.9 18.0 %collective-permute-start.18 = (bf16[512,512]{0,1:T(8,128)(2,1)S(1)}, bf16[512,512]{0,1:T(8,128)(2,1)S(1)}, u32[]{:S(2)}, u32[]{:S(2)}) collective-permute-start(bf16[512,512]{0,1:T(8,128)(2,1)S(1)} %pad_maximum_fusion.1), channel_id=1, source_target_pairs={{0,8},{1,9},{2,10},{3,11},{4,12},{5,13},{6,14},{7,15},{8,0},{9,1},... | collective-permute-start | bytes 1572872 | tf_op jit(solution)/shard_map/ppermute | solution.py:56
  287.5 43.5 %copy-start.15 = (f32[256,16]{0,1:T(8,128)S(1)}, f32[256,16]{0,1:T(8,128)}, u32[]{:S(2)}) copy-start(f32[256,16]{0,1:T(8,128)} %param.20) | copy-start | bytes 49156

commit v11 on v9

--- a/solution.py
+++ b/solution.py
@@ -119,10 +119,16 @@
     scale_in = 1.0 / math.sqrt(hidden.shape[1])
     attention = attention_weights(query_rows, key_rows, segment_ids[0])
     groups = lax.axis_size("island")
+    own_count = token_counts[0].astype(jnp.float32)
+    counted = jnp.concatenate(
+        [anchor, jnp.full((1, anchor.shape[1]), own_count, jnp.float32)], axis=0
+    )
     if groups == 32:
-        master = island_gather(anchor, (4, 4, 2))
+        gathered = island_gather(counted, (4, 4, 2))
     else:
-        master = lax.all_gather(anchor, "island", axis=1, tiled=True)
+        gathered = lax.all_gather(counted, "island", axis=1, tiled=True)
+    master = gathered[: anchor.shape[0]]
+    counts = gathered[anchor.shape[0]].reshape(groups, anchor.shape[1])
     start_point = master
     block = master.shape[0]
     first = first_moment[0]
@@ -175,23 +181,15 @@
         master = master - inner_rate * (first / (jnp.sqrt(second) + epsilon) + decay * master)
     delta = start_point - master
     cols = anchor.shape[1]
-    own_count = token_counts[0].astype(jnp.float32)
-    count_high = own_count.astype(jnp.bfloat16)
-    count_low = (own_count - count_high.astype(jnp.float32)).astype(jnp.bfloat16)
-    sent = jnp.concatenate(
-        [
-            delta.astype(jnp.bfloat16),
-            jnp.full((1, delta.shape[1]), count_high, jnp.bfloat16),
-            jnp.full((1, delta.shape[1]), count_low, jnp.bfloat16),
-        ],
-        axis=0,
-    )
     received = lax.all_to_all(
-        sent.reshape(block + 2, groups, cols), "island", split_axis=1, concat_axis=0, tiled=True
-    ).reshape(groups, block + 2, cols).astype(jnp.float32)
-    counts = received[:, block] + received[:, block + 1]
+        delta.astype(jnp.bfloat16).reshape(block, groups, cols),
+        "island",
+        split_axis=1,
+        concat_axis=0,
+        tiled=True,
+    ).reshape(groups, block, cols).astype(jnp.float32)
     total = jnp.sum(counts, axis=0)
-    average = jnp.sum(counts[:, None, :] * received[:, :block], axis=0) / total
+    average = jnp.sum(counts[:, None, :] * received, axis=0) / total
     new_momentum = outer_beta * outer_momentum + average
     new_anchor = anchor - outer_rate * (average + outer_beta * new_momentum)
     return (new_anchor, new_momentum)

time: 325 us -> 323 us (level)
  blocking collectives: 100 us -> 56 us
  waiting for transfers between devices: 90.4 us -> 111 us
  starting transfers between devices: 87.7 us -> 108 us
    all_to_all x1 -> x0, blocking collectives: 44.2 us -> none  [on_device(): lax.all_to_all(sent.reshape(block + 2, groups, cols), 'island', split_axi...]
    all_to_all x0 -> x1, waiting for transfers between devices: none -> 18.8 us  [on_device(): lax.all_to_all(delta.astype(jnp.bfloat16).reshape(block, groups, cols), '...]
    all_to_all x0 -> x1, starting transfers between devices: none -> 16.8 us  [on_device(): lax.all_to_all(delta.astype(jnp.bfloat16).reshape(block, groups, cols), '...]
    all_to_all x1, starting transfers between devices: 8.61 us -> 12.2 us  [on_device(): lax.all_to_all(partial.reshape(members, rows, width), 'fsdp', split_axis=...]
    unnamed x58 -> x62, local copies, waits for them, and re-layouts: 7.34 us -> 7.3 us
  transfers between devices with their start and end apart: 21 -> 22, of which waited for: 10 -> 11; matrix products, arithmetic and copies ran while one was open for 4% -> 4% of each run, Pallas kernels for 0% -> 0%
where the time goes in v11:
time: 323 us; the launch traced here: 322 us
  waiting for transfers between devices  111 us (34%)
  starting transfers between devices  108 us (33%)
  blocking collectives  56 us (17%)
  local copies, waits for them, and re-layouts  20 us (6%)
  other arithmetic  12.6 us (4%)
  matrix products  11.8 us (4%)
    all_to_all x1, blocking collectives, on_device(): lax.all_to_all(partial.reshape(members, rows, width), 'fsdp', split_axis=...  56 us
    all_to_all x1, waiting for transfers between devices, on_device(): lax.all_to_all(partial.reshape(members, rows, width), 'fsdp', split_axis=...  47.9 us
    ppermute x4, waiting for transfers between devices, along(): far = lax.ppermute(up, 'fsdp', _shift(cols, rows, dx, dz))  26.3 us
    ppermute x4, starting transfers between devices, along(): down = lax.ppermute(part, 'fsdp', _shift(cols, rows, -dx, -dz))  19.5 us
    all_to_all x1, waiting for transfers between devices, on_device(): lax.all_to_all(delta.astype(jnp.bfloat16).reshape(block, groups, cols), '...  18.8 us
    all_to_all x1, starting transfers between devices, on_device(): lax.all_to_all(delta.astype(jnp.bfloat16).reshape(block, groups, cols), '...  16.8 us
    ppermute x2, starting transfers between devices, island_gather(): moved[-2] = lax.ppermute(moved[0], 'island', shift(axis, 2))  13.8 us
    all_to_all x1, starting transfers between devices, on_device(): lax.all_to_all(partial.reshape(members, rows, width), 'fsdp', split_axis=...  12.2 us
  transfers between devices with their start and end apart: 22, of which 11 were waited for; matrix products, arithmetic and copies ran while one was open for 4% of the time, Pallas kernels for 0%

profile of v11, /device:TPU:1, one launch (start us, length us, event | category | flops | bytes accessed | tf_op | source)
XLA Modules:
  0.0 321.7 jit_solution(1664907192748584887)
XLA Ops:
  0.6 1.6 copy.59
  2.3 1.3 copy.60
  3.6 9.1 %all-to-all-start = ((bf16[128,16,256]{2,0,1:T(8,128)(2,1)}), bf16[128,16,256]{2,0,1:T(8,128)(2,1)S(1)}, u32[]{:S(2)}, u32[]{:S(2)}) async-start(bf16[128,16,256]{2,0,1:T(8,128)(2,1)} %copy.60), calls=%async_computation | async-start | bytes 2097152 | tf_op jit(solution)/shard_map/all_to_all | solution.py:136
  13.4 3.4 %collective-permute-start = (f32[1,257,16]{1,2,0:T(8,128)S(1)}, f32[1,257,16]{1,2,0:T(8,128)S(1)}, u32[]{:S(2)}, u32[]{:S(2)}) collective-permute-start(f32[1,257,16]{1,2,0:T(8,128)S(1)} %pad_bitcast_fusion), channel_id=1, source_target_pairs={{0,16},{16,0},{32,48},{48,32},{64,80},{80,64},{96,112},{112,96},{1... | collective-permute-start | bytes 49352 | tf_op jit(solution)/shard_map/ppermute | solution.py:92
  17.5 1.6 sort.17
  19.2 2.1 divide_convert_fusion
  21.3 8.3 %collective-permute-start.1 = (f32[2,257,16]{1,2,0:T(8,128)S(1)}, f32[2,257,16]{1,2,0:T(8,128)S(1)}, u32[]{:S(2)}, u32[]{:S(2)}) collective-permute-start(f32[2,257,16]{1,2,0:T(8,128)S(1)} %pad_maximum_fusion.2), channel_id=1, source_target_pairs={{0,32},{16,48},{32,64},{48,80},{64,96},{80,112},{96,0},{112,16},{1... | collective-permute-start | bytes 98696 | tf_op jit(solution)/shard_map/ppermute | solution.py:87
  29.6 2.9 collective-permute-start.2
  32.4 10.3 %collective-permute-start.3 = (f32[2,257,16]{1,2,0:T(8,128)S(1)}, f32[2,257,16]{1,2,0:T(8,128)S(1)}, u32[]{:S(2)}, u32[]{:S(2)}) collective-permute-start(f32[2,257,16]{1,2,0:T(8,128)S(1)} %pad_maximum_fusion.2), channel_id=1, source_target_pairs={{0,64},{16,80},{32,96},{48,112},{64,0},{80,16},{96,32},{112,48},{1... | collective-permute-start | bytes 98696 | tf_op jit(solution)/shard_map/ppermute | solution.py:89
  42.8 3.4 %collective-permute-done.3 = f32[2,257,16]{1,2,0:T(8,128)S(1)} collective-permute-done((f32[2,257,16]{1,2,0:T(8,128)S(1)}, f32[2,257,16]{1,2,0:T(8,128)S(1)}, u32[]{:S(2)}, u32[]{:S(2)}) %collective-permute-start.3) | collective-permute-done | bytes 32928 | tf_op jit(solution)/shard_map/ppermute | solution.py:89
  46.2 3.2 collective-permute-start.4
  49.4 3.3 %collective-permute-start.5 = (f32[8,257,16]{1,2,0:T(8,128)S(1)}, f32[8,257,16]{1,2,0:T(8,128)S(1)}, u32[]{:S(2)}, u32[]{:S(2)}) collective-permute-start(f32[8,257,16]{1,2,0:T(8,128)S(1)} %get-tuple-element.12), channel_id=1, source_target_pairs={{0,384},{16,400},{32,416},{48,432},{64,448},{80,464},{96,480},{112... | collective-permute-start | bytes 394760 | tf_op jit(solution)/shard_map/ppermute | solution.py:88
  52.7 3.5 %collective-permute-start.6 = (f32[8,257,16]{1,2,0:T(8,128)S(1)}, f32[8,257,16]{1,2,0:T(8,128)S(1)}, u32[]{:S(2)}, u32[]{:S(2)}) collective-permute-start(f32[8,257,16]{1,2,0:T(8,128)S(1)} %get-tuple-element.12), channel_id=1, source_target_pairs={{0,256},{16,272},{32,288},{48,304},{64,320},{80,336},{96,352},{112... | collective-permute-start | bytes 394760 | tf_op jit(solution)/shard_map/ppermute | solution.py:89
  56.4 4.3 %collective-permute-done.6 = f32[8,257,16]{1,2,0:T(8,128)S(1)} collective-permute-done((f32[8,257,16]{1,2,0:T(8,128)S(1)}, f32[8,257,16]{1,2,0:T(8,128)S(1)}, u32[]{:S(2)}, u32[]{:S(2)}) %collective-permute-start.6) | collective-permute-done | bytes 131616 | tf_op jit(solution)/shard_map/ppermute | solution.py:89
  60.7 0.6 gather_fusion
  61.4 0.9 copy-done.1
  62.4 2.0 convolution_convert_fusion.1
  64.4 12.2 %all-to-all-start.1 = ((bf16[16,128,512]{2,1,0:T(8,128)(2,1)}), bf16[16,128,512]{2,1,0:T(8,128)(2,1)}, u32[]{:S(2)}, u32[]{:S(2)}) async-start(bf16[16,128,512]{2,1,0:T(8,128)(2,1)} %bitcast.152), calls=%async_computation.1 | async-start | bytes 4194304 | tf_op jit(solution)/shard_map/all_to_all | solution.py:152
  76.9 1.7 copy.66
  78.6 47.9 %all-to-all-done.1 = bf16[16,128,512]{2,1,0:T(8,128)(2,1)} async-done(((bf16[16,128,512]{2,1,0:T(8,128)(2,1)}), bf16[16,128,512]{2,1,0:T(8,128)(2,1)}, u32[]{:S(2)}, u32[]{:S(2)}) %all-to-all-start.1) | async-done | bytes 2097184 | tf_op jit(solution)/shard_map/all_to_all | solution.py:152
  126.5 1.9 convert_reduce_fusion.1
  128.5 1.8 fusion.65
  130.3 2.9 copy.65
  133.2 2.2 fusion.12
  135.6 1.0 copy-done.7
  137.1 1.9 collective-permute-start.7
  139.0 0.7 broadcast_bitcast_fusion
  139.7 5.1 %collective-permute-start.8 = (bf16[128,512]{0,1:T(8,128)(2,1)S(1)}, bf16[128,512]{0,1:T(8,128)(2,1)S(1)}, u32[]{:S(2)}, u32[]{:S(2)}) collective-permute-start(bf16[128,512]{0,1:T(8,128)(2,1)S(1)} %bitcast.165), channel_id=1, source_target_pairs={{0,3},{1,0},{2,1},{3,2},{4,7},{5,4},{6,5},{7,6},{8,11},{9,8},{10,9... | collective-permute-start | bytes 393224 | tf_op jit(solution)/shard_map/ppermute | solution.py:55
  144.8 1.9 collective-permute-start.9
  146.8 0.6 pad_clamp_fusion
  147.4 1.0 copy.73
  148.4 0.7 gather_fusion.1
  149.1 3.3 %collective-permute-done.9 = bf16[128,512]{0,1:T(8,128)(2,1)} collective-permute-done((bf16[128,512]{0,1:T(8,128)(2,1)S(1)}, bf16[128,512]{0,1:T(8,128)(2,1)}, u32[]{:S(2)}, u32[]{:S(2)}) %collective-permute-start.9) | collective-permute-done | bytes 131104 | tf_op jit(solution)/shard_map/ppermute | solution.py:56
  152.4 1.0 pad_maximum_fusion
  153.4 1.9 collective-permute-start.10
  155.3 1.1 bitcast_select_fusion.2
  156.5 4.6 %collective-permute-start.11 = (bf16[512,512]{0,1:T(8,128)(2,1)S(1)}, bf16[512,512]{0,1:T(8,128)(2,1)S(1)}, u32[]{:S(2)}, u32[]{:S(2)}) collective-permute-start(bf16[512,512]{0,1:T(8,128)(2,1)S(1)} %pad_maximum_fusion), channel_id=1, source_target_pairs={{0,12},{1,13},{2,14},{3,15},{4,0},{5,1},{6,2},{7,3},{8,4},{9,5},{1... | collective-permute-start | bytes 1572872 | tf_op jit(solution)/shard_map/ppermute | solution.py:55
  161.1 4.7 %collective-permute-done.10 = bf16[512,512]{0,1:T(8,128)(2,1)S(1)} collective-permute-done((bf16[512,512]{0,1:T(8,128)(2,1)S(1)}, bf16[512,512]{0,1:T(8,128)(2,1)S(1)}, u32[]{:S(2)}, u32[]{:S(2)}) %collective-permute-start.10) | collective-permute-done | bytes 524320 | tf_op jit(solution)/shard_map/ppermute | solution.py:54
  165.8 1.9 collective-permute-start.12
  167.9 0.9 constant_dynamic-update-slice_fusion.16
  168.9 8.5 %collective-permute-done.12 = bf16[512,512]{0,1:T(8,128)(2,1)S(1)} collective-permute-done((bf16[512,512]{0,1:T(8,128)(2,1)S(1)}, bf16[512,512]{0,1:T(8,128)(2,1)S(1)}, u32[]{:S(2)}, u32[]{:S(2)}) %collective-permute-start.12) | collective-permute-done | bytes 524320 | tf_op jit(solution)/shard_map/ppermute | solution.py:56
  177.5 0.8 fusion.66
  178.9 1.0 convolution_convert_fusion
  179.9 56.0 %all_to_all.38 = bf16[16,128,512]{2,1,0:T(8,128)(2,1)S(1)} all-to-all(bf16[16,128,512]{2,1,0:T(8,128)(2,1)S(1)} %bitcast.151), channel_id=1, replica_groups=mesh['island'=32,'fsdp'=16] {'fsdp'}, dimensions={0} | all-to-all | bytes 4194304 | tf_op jit(solution)/shard_map/all_to_all | solution.py:152
  236.4 1.8 fusion.67
  238.2 1.9 copy.71
  240.1 1.5 fusion.11
  241.9 1.0 copy-done.8
  243.3 1.9 collective-permute-start.13
  245.3 5.2 %collective-permute-start.14 = (bf16[128,512]{0,1:T(8,128)(2,1)S(1)}, bf16[128,512]{0,1:T(8,128)(2,1)S(1)}, u32[]{:S(2)}, u32[]{:S(2)}) collective-permute-start(bf16[128,512]{0,1:T(8,128)(2,1)S(1)} %bitcast.169), channel_id=1, source_target_pairs={{0,3},{1,0},{2,1},{3,2},{4,7},{5,4},{6,5},{7,6},{8,11},{9,8},{10,9... | collective-permute-start | bytes 393224 | tf_op jit(solution)/shard_map/ppermute | solution.py:55
  250.4 0.6 collective-permute-done.13
  251.0 1.9 collective-permute-start.15
  253.0 5.6 %collective-permute-done.15 = bf16[128,512]{0,1:T(8,128)(2,1)S(1)} collective-permute-done((bf16[128,512]{0,1:T(8,128)(2,1)S(1)}, bf16[128,512]{0,1:T(8,128)(2,1)S(1)}, u32[]{:S(2)}, u32[]{:S(2)}) %collective-permute-start.15) | collective-permute-done | bytes 131104 | tf_op jit(solution)/shard_map/ppermute | solution.py:56
  258.7 2.2 collective-permute-start.16
  260.9 4.6 %collective-permute-start.17 = (bf16[512,512]{0,1:T(8,128)(2,1)S(1)}, bf16[512,512]{0,1:T(8,128)(2,1)S(1)}, u32[]{:S(2)}, u32[]{:S(2)}) collective-permute-start(bf16[512,512]{0,1:T(8,128)(2,1)S(1)} %pad_maximum_fusion.1), channel_id=1, source_target_pairs={{0,12},{1,13},{2,14},{3,15},{4,0},{5,1},{6,2},{7,3},{8,4},{9,5},{1... | collective-permute-start | bytes 1572872 | tf_op jit(solution)/shard_map/ppermute | solution.py:55
  265.5 5.0 %collective-permute-done.16 = bf16[512,512]{0,1:T(8,128)(2,1)S(1)} collective-permute-done((bf16[512,512]{0,1:T(8,128)(2,1)S(1)}, bf16[512,512]{0,1:T(8,128)(2,1)S(1)}, u32[]{:S(2)}, u32[]{:S(2)}) %collective-permute-start.16) | collective-permute-done | bytes 524320 | tf_op jit(solution)/shard_map/ppermute | solution.py:54
  270.4 1.9 collective-permute-start.18
  272.6 8.9 %collective-permute-done.18 = bf16[512,512]{0,1:T(8,128)(2,1)S(1)} collective-permute-done((bf16[512,512]{0,1:T(8,128)(2,1)S(1)}, bf16[512,512]{0,1:T(8,128)(2,1)S(1)}, u32[]{:S(2)}, u32[]{:S(2)}) %collective-permute-start.18) | collective-permute-done | bytes 524320 | tf_op jit(solution)/shard_map/ppermute | solution.py:56
  281.7 1.4 fusion.28
  283.1 0.8 copy.74
  283.9 16.8 %all-to-all-start.3 = ((bf16[256,32,16]{0,2,1:T(8,128)(2,1)}), bf16[256,32,16]{0,2,1:T(8,128)(2,1)S(1)}, u32[]{:S(2)}, u32[]{:S(2)}) async-start(bf16[256,32,16]{0,2,1:T(8,128)(2,1)} %bitcast.69), calls=%async_computation.3 | async-start | bytes 524288 | tf_op jit(solution)/shard_map/all_to_all | solution.py:184
  300.7 1.1 slice_reduce_fusion
  302.0 18.8 %all-to-all-done.3 = bf16[256,32,16]{0,2,1:T(8,128)(2,1)S(1)} async-done(((bf16[256,32,16]{0,2,1:T(8,128)(2,1)}), bf16[256,32,16]{0,2,1:T(8,128)(2,1)S(1)}, u32[]{:S(2)}, u32[]{:S(2)}) %all-to-all-start.3) | async-done | bytes 262176 | tf_op jit(solution)/shard_map/all_to_all | solution.py:184
  321.0 0.7 multiply_subtract_fusion.1
  (99 shorter events, 4.8 us)
Async XLA Ops:
  2.3 11.1 %copy-start.15 = (f32[256,16]{0,1:T(8,128)S(1)}, f32[256,16]{0,1:T(8,128)}, u32[]{:S(2)}) copy-start(f32[256,16]{0,1:T(8,128)} %param.19) | copy-start | bytes 49156
  2.3 14.8 %copy-start.6 = (bf16[128,4096]{1,0:T(8,128)(2,1)S(1)}, bf16[128,4096]{1,0:T(8,128)(2,1)}, u32[]{:S(2)}) copy-start(bf16[128,4096]{1,0:T(8,128)(2,1)} %param.13) | copy-start | bytes 3145732
  3.6 13.7 %copy-start.16 = (bf16[128,512]{1,0:T(8,128)(2,1)S(1)}, bf16[128,512]{1,0:T(8,128)(2,1)}, u32[]{:S(2)}) copy-start(bf16[128,512]{1,0:T(8,128)(2,1)} %param.14) | copy-start | bytes 393220
  3.6 15.5 %copy-start.18 = (s32[1,128]{1,0:T(1,128)S(1)}, s32[1,128]{1,0:T(1,128)}, u32[]{:S(2)}) copy-start(s32[1,128]{1,0:T(1,128)} %param.16) | copy-start | bytes 1540
  3.6 58.8 %all-to-all-start = ((bf16[128,16,256]{2,0,1:T(8,128)(2,1)}), bf16[128,16,256]{2,0,1:T(8,128)(2,1)S(1)}, u32[]{:S(2)}, u32[]{:S(2)}) async-start(bf16[128,16,256]{2,0,1:T(8,128)(2,1)} %copy.60), calls=%async_computation | async-start | bytes 2097152 | tf_op jit(solution)/shard_map/all_to_all | solution.py:136
  13.4 7.9 %collective-permute-start = (f32[1,257,16]{1,2,0:T(8,128)S(1)}, f32[1,257,16]{1,2,0:T(8,128)S(1)}, u32[]{:S(2)}, u32[]{:S(2)}) collective-permute-start(f32[1,257,16]{1,2,0:T(8,128)S(1)} %pad_bitcast_fusion), channel_id=1, source_target_pairs={{0,16},{16,0},{32,48},{48,32},{64,80},{80,64},{96,112},{112,96},{1... | collective-permute-start | bytes 49352 | tf_op jit(solution)/shard_map/ppermute | solution.py:92
  21.3 21.4 %collective-permute-start.1 = (f32[2,257,16]{1,2,0:T(8,128)S(1)}, f32[2,257,16]{1,2,0:T(8,128)S(1)}, u32[]{:S(2)}, u32[]{:S(2)}) collective-permute-start(f32[2,257,16]{1,2,0:T(8,128)S(1)} %pad_maximum_fusion.2), channel_id=1, source_target_pairs={{0,32},{16,48},{32,64},{48,80},{64,96},{80,112},{96,0},{112,16},{1... | collective-permute-start | bytes 98696 | tf_op jit(solution)/shard_map/ppermute | solution.py:87
  29.6 13.2 %collective-permute-start.2 = (f32[2,257,16]{1,2,0:T(8,128)S(1)}, f32[2,257,16]{1,2,0:T(8,128)S(1)}, u32[]{:S(2)}, u32[]{:S(2)}) collective-permute-start(f32[2,257,16]{1,2,0:T(8,128)S(1)} %pad_maximum_fusion.2), channel_id=1, source_target_pairs={{0,96},{16,112},{32,0},{48,16},{64,32},{80,48},{96,64},{112,80},{1... | collective-permute-start | bytes 98696 | tf_op jit(solution)/shard_map/ppermute | solution.py:88
  32.4 13.7 %collective-permute-start.3 = (f32[2,257,16]{1,2,0:T(8,128)S(1)}, f32[2,257,16]{1,2,0:T(8,128)S(1)}, u32[]{:S(2)}, u32[]{:S(2)}) collective-permute-start(f32[2,257,16]{1,2,0:T(8,128)S(1)} %pad_maximum_fusion.2), channel_id=1, source_target_pairs={{0,64},{16,80},{32,96},{48,112},{64,0},{80,16},{96,32},{112,48},{1... | collective-permute-start | bytes 98696 | tf_op jit(solution)/shard_map/ppermute | solution.py:89
  46.2 10.1 %collective-permute-start.4 = (f32[8,257,16]{1,2,0:T(8,128)S(1)}, f32[8,257,16]{1,2,0:T(8,128)S(1)}, u32[]{:S(2)}, u32[]{:S(2)}) collective-permute-start(f32[8,257,16]{1,2,0:T(8,128)S(1)} %get-tuple-element.12), channel_id=1, source_target_pairs={{0,128},{16,144},{32,160},{48,176},{64,192},{80,208},{96,224},{112... | collective-permute-start | bytes 394760 | tf_op jit(solution)/shard_map/ppermute | solution.py:87
  49.4 7.0 %collective-permute-start.5 = (f32[8,257,16]{1,2,0:T(8,128)S(1)}, f32[8,257,16]{1,2,0:T(8,128)S(1)}, u32[]{:S(2)}, u32[]{:S(2)}) collective-permute-start(f32[8,257,16]{1,2,0:T(8,128)S(1)} %get-tuple-element.12), channel_id=1, source_target_pairs={{0,384},{16,400},{32,416},{48,432},{64,448},{80,464},{96,480},{112... | collective-permute-start | bytes 394760 | tf_op jit(solution)/shard_map/ppermute | solution.py:88
  52.7 7.9 %collective-permute-start.6 = (f32[8,257,16]{1,2,0:T(8,128)S(1)}, f32[8,257,16]{1,2,0:T(8,128)S(1)}, u32[]{:S(2)}, u32[]{:S(2)}) collective-permute-start(f32[8,257,16]{1,2,0:T(8,128)S(1)} %get-tuple-element.12), channel_id=1, source_target_pairs={{0,256},{16,272},{32,288},{48,304},{64,320},{80,336},{96,352},{112... | collective-permute-start | bytes 394760 | tf_op jit(solution)/shard_map/ppermute | solution.py:89
  61.4 0.9 copy-start.1
  64.4 12.2 %copy-start.19 = (s32[4]{0:T(128)S(1)}, s32[4]{0:T(128)}, u32[]{:S(2)}) copy-start(s32[4]{0:T(128)} %constant.257.clone) | copy-start | bytes 52
  64.4 12.5 %copy-start = (bf16[4,8,128,128]{2,3,1,0:T(8,128)(2,1)S(1)}, bf16[4,8,128,128]{2,3,1,0:T(8,128)(2,1)}, u32[]{:S(2)}) copy-start(bf16[4,8,128,128]{2,3,1,0:T(8,128)(2,1)} %divide_convert_fusion) | copy-start | bytes 3145732
  64.4 62.0 %all-to-all-start.1 = ((bf16[16,128,512]{2,1,0:T(8,128)(2,1)}), bf16[16,128,512]{2,1,0:T(8,128)(2,1)}, u32[]{:S(2)}, u32[]{:S(2)}) async-start(bf16[16,128,512]{2,1,0:T(8,128)(2,1)} %bitcast.152), calls=%async_computation.1 | async-start | bytes 4194304 | tf_op jit(solution)/shard_map/all_to_all | solution.py:152
  135.4 1.2 copy-start.7
  137.1 7.7 %collective-permute-start.7 = (bf16[128,512]{0,1:T(8,128)(2,1)S(1)}, bf16[128,512]{0,1:T(8,128)(2,1)S(1)}, u32[]{:S(2)}, u32[]{:S(2)}) collective-permute-start(bf16[128,512]{0,1:T(8,128)(2,1)S(1)} %bitcast.164), channel_id=1, source_target_pairs={{0,1},{1,2},{2,3},{3,0},{4,5},{5,6},{6,7},{7,4},{8,9},{9,10},{10,1... | collective-permute-start | bytes 393224 | tf_op jit(solution)/shard_map/ppermute | solution.py:54
  139.7 9.5 %collective-permute-start.8 = (bf16[128,512]{0,1:T(8,128)(2,1)S(1)}, bf16[128,512]{0,1:T(8,128)(2,1)S(1)}, u32[]{:S(2)}, u32[]{:S(2)}) collective-permute-start(bf16[128,512]{0,1:T(8,128)(2,1)S(1)} %bitcast.165), channel_id=1, source_target_pairs={{0,3},{1,0},{2,1},{3,2},{4,7},{5,4},{6,5},{7,6},{8,11},{9,8},{10,9... | collective-permute-start | bytes 393224 | tf_op jit(solution)/shard_map/ppermute | solution.py:55
  144.8 7.6 %collective-permute-start.9 = (bf16[128,512]{0,1:T(8,128)(2,1)S(1)}, bf16[128,512]{0,1:T(8,128)(2,1)}, u32[]{:S(2)}, u32[]{:S(2)}) collective-permute-start(bf16[128,512]{0,1:T(8,128)(2,1)S(1)} %collective-permute-done.7), channel_id=1, source_target_pairs={{0,1},{1,2},{2,3},{3,0},{4,5},{5,6},{6,7},{7,4},{8,9},{9,10},{10,1... | collective-permute-start | bytes 393224 | tf_op jit(solution)/shard_map/ppermute | solution.py:56
  153.4 12.4 %collective-permute-start.10 = (bf16[512,512]{0,1:T(8,128)(2,1)S(1)}, bf16[512,512]{0,1:T(8,128)(2,1)S(1)}, u32[]{:S(2)}, u32[]{:S(2)}) collective-permute-start(bf16[512,512]{0,1:T(8,128)(2,1)S(1)} %pad_maximum_fusion), channel_id=1, source_target_pairs={{0,4},{1,5},{2,6},{3,7},{4,8},{5,9},{6,10},{7,11},{8,12},{9,13},{1... | collective-permute-start | bytes 1572872 | tf_op jit(solution)/shard_map/ppermute | solution.py:54
  156.5 21.0 %copy-start.4 = (bf16[2048,256]{1,0:T(8,128)(2,1)}, bf16[2048,256]{1,0:T(8,128)(2,1)S(1)}, u32[]{:S(2)}) copy-start(bf16[2048,256]{1,0:T(8,128)(2,1)S(1)} %bitcast_select_fusion.2) | copy-start | bytes 3145732
  156.5 12.4 %collective-permute-start.11 = (bf16[512,512]{0,1:T(8,128)(2,1)S(1)}, bf16[512,512]{0,1:T(8,128)(2,1)S(1)}, u32[]{:S(2)}, u32[]{:S(2)}) collective-permute-start(bf16[512,512]{0,1:T(8,128)(2,1)S(1)} %pad_maximum_fusion), channel_id=1, source_target_pairs={{0,12},{1,13},{2,14},{3,15},{4,0},{5,1},{6,2},{7,3},{8,4},{9,5},{1... | collective-permute-start | bytes 1572872 | tf_op jit(solution)/shard_map/ppermute | solution.py:55
  165.8 11.6 %collective-permute-start.12 = (bf16[512,512]{0,1:T(8,128)(2,1)S(1)}, bf16[512,512]{0,1:T(8,128)(2,1)S(1)}, u32[]{:S(2)}, u32[]{:S(2)}) collective-permute-start(bf16[512,512]{0,1:T(8,128)(2,1)S(1)} %collective-permute-done.10), channel_id=1, source_target_pairs={{0,4},{1,5},{2,6},{3,7},{4,8},{5,9},{6,10},{7,11},{8,12},{9,13},{1... | collective-permute-start | bytes 1572872 | tf_op jit(solution)/shard_map/ppermute | solution.py:56
  177.5 1.0 copy-start.2
  177.5 1.2 copy-start.9
  177.5 1.3 copy-start.11
  178.9 1.1 copy-start.13
  241.6 1.2 copy-start.8
  243.3 7.7 %collective-permute-start.13 = (bf16[128,512]{0,1:T(8,128)(2,1)S(1)}, bf16[128,512]{0,1:T(8,128)(2,1)S(1)}, u32[]{:S(2)}, u32[]{:S(2)}) collective-permute-start(bf16[128,512]{0,1:T(8,128)(2,1)S(1)} %bitcast.168), channel_id=1, source_target_pairs={{0,1},{1,2},{2,3},{3,0},{4,5},{5,6},{6,7},{7,4},{8,9},{9,10},{10,1... | collective-permute-start | bytes 393224 | tf_op jit(solution)/shard_map/ppermute | solution.py:54
  245.3 7.7 %collective-permute-start.14 = (bf16[128,512]{0,1:T(8,128)(2,1)S(1)}, bf16[128,512]{0,1:T(8,128)(2,1)S(1)}, u32[]{:S(2)}, u32[]{:S(2)}) collective-permute-start(bf16[128,512]{0,1:T(8,128)(2,1)S(1)} %bitcast.169), channel_id=1, source_target_pairs={{0,3},{1,0},{2,1},{3,2},{4,7},{5,4},{6,5},{7,6},{8,11},{9,8},{10,9... | collective-permute-start | bytes 393224 | tf_op jit(solution)/shard_map/ppermute | solution.py:55
  251.0 7.5 %collective-permute-start.15 = (bf16[128,512]{0,1:T(8,128)(2,1)S(1)}, bf16[128,512]{0,1:T(8,128)(2,1)S(1)}, u32[]{:S(2)}, u32[]{:S(2)}) collective-permute-start(bf16[128,512]{0,1:T(8,128)(2,1)S(1)} %collective-permute-done.13), channel_id=1, source_target_pairs={{0,1},{1,2},{2,3},{3,0},{4,5},{5,6},{6,7},{7,4},{8,9},{9,10},{10,1... | collective-permute-start | bytes 393224 | tf_op jit(solution)/shard_map/ppermute | solution.py:56
  258.6 23.0 %copy-start.3 = (f32[256,512]{1,0:T(8,128)S(1)}, f32[256,512]{1,0:T(8,128)}, u32[]{:S(2)}) copy-start(f32[256,512]{1,0:T(8,128)} %copy.73) | copy-start | bytes 1572868
  258.6 23.0 %copy-start.5 = (bf16[2048,256]{1,0:T(8,128)(2,1)S(1)}, bf16[2048,256]{1,0:T(8,128)(2,1)}, u32[]{:S(2)}) copy-start(bf16[2048,256]{1,0:T(8,128)(2,1)} %copy-done.4) | copy-start | bytes 3145732
  258.6 23.0 %copy-start.10 = (f32[1,256,512]{2,1,0:T(8,128)S(1)}, f32[1,256,512]{2,1,0:T(8,128)}, u32[]{:S(2)}) copy-start(f32[1,256,512]{2,1,0:T(8,128)} %param.17) | copy-start | bytes 1572868
  258.6 23.0 %copy-start.12 = (f32[1,256,512]{2,1,0:T(8,128)S(1)}, f32[1,256,512]{2,1,0:T(8,128)}, u32[]{:S(2)}) copy-start(f32[1,256,512]{2,1,0:T(8,128)} %param.18) | copy-start | bytes 1572868
  258.6 23.0 %copy-start.14 = (f32[256,512]{1,0:T(8,128)S(1)}, f32[256,512]{1,0:T(8,128)}, u32[]{:S(2)}) copy-start(f32[256,512]{1,0:T(8,128)} %copy-done.13) | copy-start | bytes 1572868
  258.7 11.8 %collective-permute-start.16 = (bf16[512,512]{0,1:T(8,128)(2,1)S(1)}, bf16[512,512]{0,1:T(8,128)(2,1)S(1)}, u32[]{:S(2)}, u32[]{:S(2)}) collective-permute-start(bf16[512,512]{0,1:T(8,128)(2,1)S(1)} %pad_maximum_fusion.1), channel_id=1, source_target_pairs={{0,4},{1,5},{2,6},{3,7},{4,8},{5,9},{6,10},{7,11},{8,12},{9,13},{1... | collective-permute-start | bytes 1572872 | tf_op jit(solution)/shard_map/ppermute | solution.py:54
  260.9 11.7 %collective-permute-start.17 = (bf16[512,512]{0,1:T(8,128)(2,1)S(1)}, bf16[512,512]{0,1:T(8,128)(2,1)S(1)}, u32[]{:S(2)}, u32[]{:S(2)}) collective-permute-start(bf16[512,512]{0,1:T(8,128)(2,1)S(1)} %pad_maximum_fusion.1), channel_id=1, source_target_pairs={{0,12},{1,13},{2,14},{3,15},{4,0},{5,1},{6,2},{7,3},{8,4},{9,5},{1... | collective-permute-start | bytes 1572872 | tf_op jit(solution)/shard_map/ppermute | solution.py:55
  270.4 11.1 %collective-permute-start.18 = (bf16[512,512]{0,1:T(8,128)(2,1)S(1)}, bf16[512,512]{0,1:T(8,128)(2,1)S(1)}, u32[]{:S(2)}, u32[]{:S(2)}) collective-permute-start(bf16[512,512]{0,1:T(8,128)(2,1)S(1)} %collective-permute-done.16), channel_id=1, source_target_pairs={{0,4},{1,5},{2,6},{3,7},{4,8},{5,9},{6,10},{7,11},{8,12},{9,13},{1... | collective-permute-start | bytes 1572872 | tf_op jit(solution)/shard_map/ppermute | solution.py:56
  283.1 37.9 %copy-start.17 = (f32[256,16]{0,1:T(8,128)S(1)}, f32[256,16]{0,1:T(8,128)}, u32[]{:S(2)}) copy-start(f32[256,16]{0,1:T(8,128)} %param.20) | copy-start | bytes 49156
  283.9 36.9 %all-to-all-start.3 = ((bf16[256,32,16]{0,2,1:T(8,128)(2,1)}), bf16[256,32,16]{0,2,1:T(8,128)(2,1)S(1)}, u32[]{:S(2)}, u32[]{:S(2)}) async-start(bf16[256,32,16]{0,2,1:T(8,128)(2,1)} %bitcast.69), calls=%async_computation.3 | async-start | bytes 524288 | tf_op jit(solution)/shard_map/all_to_all | solution.py:184
